TPU v7x, 32 devices: a whole 2x2x4 slice. The times are simulated.
32 devices in a mesh: tm: 16 (over z, y, x), space: 2 (over core).
Axes of the slice: x: 2, y: 2, z: 4, core: 2. Of those that a mesh axis runs over, the one named last changes fastest.
Arguments:
- adjoint: float32 [16, 16, 64, 128], P('tm', 'space'), may hold values from -6 to 6
- base_flow: float32 [3, 16, 16, 64, 128], P(None, 'tm', 'space'), may hold values from -5 to 5
- source: float32 [16, 16, 64, 128], P('tm', 'space'), may hold values from -6 to 6
- pulse: float32 [16], P('tm'), may hold values from 0.3 to 3
- actuator: int32 [16, 128], P('space'), may hold values from 0 to 127
Outputs:
- updated: float32 [16, 16, 64, 128], P('tm', 'space')
- gradient: float32 [128], P('tm')
Inputs may be any that keep to these rules, and one draw needn't show every extreme that they name: Each lower-wall cell names the actuator that drives it.
All inputs are finite; a program needn't handle non-finite values.
Results may differ from a plain program's by a relative error of at most 0.00019.
Values sent between devices are 32-bit elements; how exact they have to be, the bound alone decides.
No kernel may reach another device: no remote copies, remote signals or barrier semaphores. Data moves between devices by JAX's collectives and lax.ppermute only.
A program may use at most 64 MiB of HBM per device.

v0:
```python
import math

import jax
import jax.numpy as jnp
from jax import lax
from jax.sharding import PartitionSpec as P

NACT = 128


omega_rate = 0.25
pseudo_step = 0.2
viscosity = 0.2
reaction = 0.5


def swapped(x, axis, bit):
    return lax.ppermute(x, axis, [(i, i ^ 1 << bit) for i in range(lax.axis_size(axis))])


def padded(x, sides, width):
    for axis, dim in sides:
        count, length = (lax.axis_size(axis), x.shape[dim])
        up = [(i, (i + 1) % count) for i in range(count)]
        down = [(j, i) for i, j in up]
        last = lax.slice_in_dim(x, length - width, length, axis=dim)
        initial = lax.slice_in_dim(x, 0, width, axis=dim)
        before = lax.ppermute(last, axis, up)
        after = lax.ppermute(initial, axis, down)
        x = jnp.concatenate([before, x, after], axis=dim)
    return x


def wall_plus(field):
    zeros = jnp.zeros_like(field[:, :1])
    return jnp.concatenate([field[:, 1:], zeros], axis=1)


def wall_minus(field):
    zeros = jnp.zeros_like(field[:, :1])
    return jnp.concatenate([zeros, field[:, :-1]], axis=1)


def twiddle(position, span, count, sense):
    expo = position % span * (count // (2 * span))
    angle = sense * 2.0 * math.pi * expo.astype(jnp.float32) / count
    return (jnp.cos(angle), jnp.sin(angle))


def butterfly_term(field, position, count):
    sections = count.bit_length() - 1
    real_part = field
    imag_part = jnp.zeros_like(field)
    for bit_num in range(sections - 1, -1, -1):
        span = 1 << bit_num
        other = swapped(jnp.stack([real_part, imag_part]), "tm", bit_num)
        upper = position // span % 2 == 1
        w_real, w_imag = twiddle(position, span, count, -1.0)
        own_re = jnp.where(upper, -w_real, 1.0)
        own_im = jnp.where(upper, -w_imag, 0.0)
        oth_re = jnp.where(upper, w_real, 1.0)
        oth_im = jnp.where(upper, w_imag, 0.0)
        new_real = own_re * real_part - own_im * imag_part + oth_re * other[0] - oth_im * other[1]
        new_imag = own_re * imag_part + own_im * real_part + oth_re * other[1] + oth_im * other[0]
        real_part, imag_part = (new_real, new_imag)
    mode = jnp.int32(0)
    for bit_num in range(sections):
        mode = mode + position // (1 << bit_num) % 2 * (1 << sections - 1 - bit_num)
    signed = jnp.where(mode < count // 2, mode, mode - count)
    signed = jnp.where(mode == count // 2, 0, signed).astype(jnp.float32)
    real_part, imag_part = (omega_rate * signed * imag_part, -omega_rate * signed * real_part)
    for bit_num in range(sections):
        span = 1 << bit_num
        other = swapped(jnp.stack([real_part, imag_part]), "tm", bit_num)
        upper = position // span % 2 == 1
        w_real, w_imag = twiddle(position, span, count, 1.0)
        own_re = jnp.where(upper, -w_real, 1.0)
        own_im = jnp.where(upper, -w_imag, 0.0)
        oth_re = jnp.where(upper, 1.0, w_real)
        oth_im = jnp.where(upper, 0.0, w_imag)
        new_real = own_re * real_part - own_im * imag_part + oth_re * other[0] - oth_im * other[1]
        new_imag = own_re * imag_part + own_im * real_part + oth_re * other[1] + oth_im * other[0]
        real_part, imag_part = (new_real, new_imag)
    return real_part / count


def on_device(adjoint, base_flow, source, pulse, actuator):
    count = lax.axis_size("tm")
    position = lax.axis_index("tm")
    field = adjoint[0]
    flux_x = base_flow[0, 0] * field
    flux_y = base_flow[1, 0] * field
    flux_z = base_flow[2, 0] * field
    extended = padded(jnp.stack([field, flux_x]), (("space", 1),), 1)
    time_term = butterfly_term(field, position, count)
    advect = 0.5 * (extended[1, 2:] - extended[1, :-2])
    advect = advect + 0.5 * (wall_plus(flux_y) - wall_minus(flux_y))
    advect = advect + 0.5 * (jnp.roll(flux_z, -1, axis=2) - jnp.roll(flux_z, 1, axis=2))
    beside = extended[0, 2:] + extended[0, :-2]
    beside = beside + wall_plus(field) + wall_minus(field)
    beside = beside + jnp.roll(field, -1, axis=2) + jnp.roll(field, 1, axis=2)
    operator = advect + viscosity * (beside - 6.0 * field) - reaction * field
    residual = time_term - operator - source[0]
    updated = field - pseudo_step * residual
    wall = updated[:, 0, :] * pulse[0]
    onehot = (actuator[:, :, None] == jnp.arange(NACT, dtype=jnp.int32)[None, None, :]).astype(
        jnp.float32
    )
    partial_sum = (
        jnp.dot(
            wall.reshape(1, -1),
            onehot.reshape(-1, NACT),
            precision=lax.Precision.HIGHEST,
            preferred_element_type=jnp.float32,
        )[0]
        / count
    )
    total = lax.psum(partial_sum, ("tm", "space"))
    share = NACT // count
    gradient = lax.dynamic_slice_in_dim(total, position * share, share)
    return (updated[None], gradient)


def solution(mesh):
    in_specs = (
        P("tm", "space", None, None),
        P(None, "tm", "space", None, None),
        P("tm", "space", None, None),
        P("tm"),
        P("space", None),
    )
    out_specs = (P("tm", "space", None, None), P("tm"))
    return jax.shard_map(
        on_device, mesh=mesh, in_specs=in_specs, out_specs=out_specs, check_vma=False
    )
```

profile of v0, /device:TPU:0, one launch (start us, length us, event | category | flops | bytes accessed | tf_op | source)
XLA Modules:
  0.0 171.2 jit_solution(5157320060168919507)
XLA Ops:
  0.6 1.1 stack.18
  1.7 4.1 %collective-permute-start = (f32[2,8,64,128]{3,2,1,0:T(8,128)S(1)}, f32[2,8,64,128]{3,2,1,0:T(8,128)S(1)}, u32[]{:S(2)}, u32[]{:S(2)}) collective-permute-start(f32[2,8,64,128]{3,2,1,0:T(8,128)S(1)} %stack.18), channel_id=1, source_target_pairs={{0,16},{2,18},{4,20},{6,22},{8,24},{10,26},{12,28},{14,30},{16,0},... | collective-permute-start | bytes 1572872 | tf_op jit(solution)/shard_map/ppermute | solution.py:18
  6.0 23.0 %collective-permute-done = f32[2,8,64,128]{3,2,1,0:T(8,128)S(1)} collective-permute-done((f32[2,8,64,128]{3,2,1,0:T(8,128)S(1)}, f32[2,8,64,128]{3,2,1,0:T(8,128)S(1)}, u32[]{:S(2)}, u32[]{:S(2)}) %collective-permute-start) | collective-permute-done | bytes 524320 | tf_op jit(solution)/shard_map/ppermute | solution.py:18
  29.0 1.2 add_add_fusion.4
  31.2 12.2 %collective-permute-done.1 = f32[2,8,64,128]{3,2,1,0:T(8,128)S(1)} collective-permute-done((f32[2,8,64,128]{3,2,1,0:T(8,128)S(1)}, f32[2,8,64,128]{3,2,1,0:T(8,128)S(1)}, u32[]{:S(2)}, u32[]{:S(2)}) %collective-permute-start.1) | collective-permute-done | bytes 524320 | tf_op jit(solution)/shard_map/ppermute | solution.py:18
  43.6 1.3 collective-permute-start.2
  45.1 10.7 %collective-permute-done.2 = f32[2,8,64,128]{3,2,1,0:T(8,128)S(1)} collective-permute-done((f32[2,8,64,128]{3,2,1,0:T(8,128)S(1)}, f32[2,8,64,128]{3,2,1,0:T(8,128)S(1)}, u32[]{:S(2)}, u32[]{:S(2)}) %collective-permute-start.2) | collective-permute-done | bytes 524320 | tf_op jit(solution)/shard_map/ppermute | solution.py:18
  56.1 1.3 collective-permute-start.3
  57.4 10.5 %collective-permute-done.3 = f32[2,8,64,128]{3,2,1,0:T(8,128)S(1)} collective-permute-done((f32[2,8,64,128]{3,2,1,0:T(8,128)S(1)}, f32[2,8,64,128]{3,2,1,0:T(8,128)S(1)}, u32[]{:S(2)}, u32[]{:S(2)}) %collective-permute-start.3) | collective-permute-done | bytes 524320 | tf_op jit(solution)/shard_map/ppermute | solution.py:18
  68.1 1.3 collective-permute-start.4
  69.5 9.1 %collective-permute-done.4 = f32[2,8,64,128]{3,2,1,0:T(8,128)S(1)} collective-permute-done((f32[2,8,64,128]{3,2,1,0:T(8,128)S(1)}, f32[2,8,64,128]{3,2,1,0:T(8,128)S(1)}, u32[]{:S(2)}, u32[]{:S(2)}) %collective-permute-start.4) | collective-permute-done | bytes 524320 | tf_op jit(solution)/shard_map/ppermute | solution.py:18
  79.5 1.4 collective-permute-start.5
  81.1 8.1 %collective-permute-done.5 = f32[2,8,64,128]{3,2,1,0:T(8,128)} collective-permute-done((f32[2,8,64,128]{3,2,1,0:T(8,128)S(1)}, f32[2,8,64,128]{3,2,1,0:T(8,128)}, u32[]{:S(2)}, u32[]{:S(2)}) %collective-permute-start.5) | collective-permute-done | bytes 524320 | tf_op jit(solution)/shard_map/ppermute | solution.py:18
  89.1 1.2 add_add_fusion.1
  91.1 4.0 %collective-permute-start.6 = (f32[2,8,64,128]{3,2,1,0:T(8,128)}, f32[2,8,64,128]{3,2,1,0:T(8,128)S(1)}, u32[]{:S(2)}, u32[]{:S(2)}) collective-permute-start(f32[2,8,64,128]{3,2,1,0:T(8,128)} %pad_maximum_fusion.5), channel_id=1, source_target_pairs={{0,8},{2,10},{4,12},{6,14},{8,0},{10,2},{12,4},{14,6},{16,24},{18,... | collective-permute-start | bytes 1572872 | tf_op jit(solution)/shard_map/ppermute | solution.py:18
  95.3 1.1 bitcast_multiply_fusion.1
  96.4 1.0 fusion.39
  97.4 5.5 %collective-permute-done.6 = f32[2,8,64,128]{3,2,1,0:T(8,128)S(1)} collective-permute-done((f32[2,8,64,128]{3,2,1,0:T(8,128)}, f32[2,8,64,128]{3,2,1,0:T(8,128)S(1)}, u32[]{:S(2)}, u32[]{:S(2)}) %collective-permute-start.6) | collective-permute-done | bytes 524320 | tf_op jit(solution)/shard_map/ppermute | solution.py:18
  103.9 7.9 %collective-permute-start.7 = (f32[2,8,64,128]{3,2,1,0:T(8,128)}, f32[2,8,64,128]{3,2,1,0:T(8,128)}, u32[]{:S(2)}, u32[]{:S(2)}) collective-permute-start(f32[2,8,64,128]{3,2,1,0:T(8,128)} %pad_maximum_fusion.6), channel_id=1, source_target_pairs={{0,16},{2,18},{4,20},{6,22},{8,24},{10,26},{12,28},{14,30},{16,0},... | collective-permute-start | bytes 1572872 | tf_op jit(solution)/shard_map/ppermute | solution.py:18
  111.8 1.1 fusion.40
  114.1 1.0 fusion.37
  116.0 11.2 %collective-permute-done.7 = f32[2,8,64,128]{3,2,1,0:T(8,128)} collective-permute-done((f32[2,8,64,128]{3,2,1,0:T(8,128)}, f32[2,8,64,128]{3,2,1,0:T(8,128)}, u32[]{:S(2)}, u32[]{:S(2)}) %collective-permute-start.7) | collective-permute-done | bytes 524320 | tf_op jit(solution)/shard_map/ppermute | solution.py:18
  127.2 3.6 %fusion.14 = f32[8,64,128]{2,1,0:T(8,128)S(1)} fusion(f32[2,1,64,128]{3,2,1,0:T(8,128)S(1)} %collective-permute-done.9, f32[1,8,64,128]{3,2,1,0:T(8,128)S(1)} %get-tuple-element.32, f32[1,8,64,128]{3,2,1,0:T(8,128)S(1)} %copy-done, f32[2,1,64,128]{3,2,1,0:T(8,128)S(1)} %collective-permute-done.8, f32[2,8,64,128]{3,2,1,0:T(8,128)} %collective-permute-done.7, ...), kind=kLoop, calls=%fused_computation.24 | loop fusion | flops 8847360 | bytes 7454840 | tf_op jit(solution)/shard_map/sub | solution.py:104
  131.9 38.8 %psum.7 = f32[128]{0:T(128)S(1)} all-reduce(f32[128]{0:T(128)S(1)} %fusion), channel_id=1, replica_groups=mesh['tm'=16,'space'=2] {'tm','space'}, use_global_device_ids=true, to_apply=%region_0.1 | all-reduce | flops 128 | bytes 1024 | tf_op jit(solution)/shard_map/psum | solution.py:118
  (32 shorter events, 6.8 us)
Async XLA Ops:
  0.6 28.3 %copy-start = (f32[1,8,64,128]{3,2,1,0:T(8,128)S(1)}, f32[1,8,64,128]{3,2,1,0:T(8,128)}, u32[]{:S(2)}) copy-start(f32[1,8,64,128]{3,2,1,0:T(8,128)} %param.5) | copy-start | bytes 786436
  1.7 27.3 %collective-permute-start = (f32[2,8,64,128]{3,2,1,0:T(8,128)S(1)}, f32[2,8,64,128]{3,2,1,0:T(8,128)S(1)}, u32[]{:S(2)}, u32[]{:S(2)}) collective-permute-start(f32[2,8,64,128]{3,2,1,0:T(8,128)S(1)} %stack.18), channel_id=1, source_target_pairs={{0,16},{2,18},{4,20},{6,22},{8,24},{10,26},{12,28},{14,30},{16,0},... | collective-permute-start | bytes 1572872 | tf_op jit(solution)/shard_map/ppermute | solution.py:18
  29.0 1.3 copy-start.1
  30.3 13.2 %collective-permute-start.1 = (f32[2,8,64,128]{3,2,1,0:T(8,128)S(1)}, f32[2,8,64,128]{3,2,1,0:T(8,128)S(1)}, u32[]{:S(2)}, u32[]{:S(2)}) collective-permute-start(f32[2,8,64,128]{3,2,1,0:T(8,128)S(1)} %pad_maximum_fusion), channel_id=1, source_target_pairs={{0,8},{2,10},{4,12},{6,14},{8,0},{10,2},{12,4},{14,6},{16,24},{18,... | collective-permute-start | bytes 1572872 | tf_op jit(solution)/shard_map/ppermute | solution.py:18
  43.6 12.3 %collective-permute-start.2 = (f32[2,8,64,128]{3,2,1,0:T(8,128)S(1)}, f32[2,8,64,128]{3,2,1,0:T(8,128)S(1)}, u32[]{:S(2)}, u32[]{:S(2)}) collective-permute-start(f32[2,8,64,128]{3,2,1,0:T(8,128)S(1)} %pad_maximum_fusion.1), channel_id=1, source_target_pairs={{0,4},{2,6},{4,0},{6,2},{8,12},{10,14},{12,8},{14,10},{16,20},{18,... | collective-permute-start | bytes 1572872 | tf_op jit(solution)/shard_map/ppermute | solution.py:18
  56.1 11.9 %collective-permute-start.3 = (f32[2,8,64,128]{3,2,1,0:T(8,128)S(1)}, f32[2,8,64,128]{3,2,1,0:T(8,128)S(1)}, u32[]{:S(2)}, u32[]{:S(2)}) collective-permute-start(f32[2,8,64,128]{3,2,1,0:T(8,128)S(1)} %pad_maximum_fusion.2), channel_id=1, source_target_pairs={{0,2},{2,0},{4,6},{6,4},{8,10},{10,8},{12,14},{14,12},{16,18},{18,... | collective-permute-start | bytes 1572872 | tf_op jit(solution)/shard_map/ppermute | solution.py:18
  68.1 10.5 %collective-permute-start.4 = (f32[2,8,64,128]{3,2,1,0:T(8,128)S(1)}, f32[2,8,64,128]{3,2,1,0:T(8,128)S(1)}, u32[]{:S(2)}, u32[]{:S(2)}) collective-permute-start(f32[2,8,64,128]{3,2,1,0:T(8,128)S(1)} %pad_maximum_fusion.3), channel_id=1, source_target_pairs={{0,2},{2,0},{4,6},{6,4},{8,10},{10,8},{12,14},{14,12},{16,18},{18,... | collective-permute-start | bytes 1572872 | tf_op jit(solution)/shard_map/ppermute | solution.py:18
  78.6 0.8 copy-start.3
  79.5 9.7 %collective-permute-start.5 = (f32[2,8,64,128]{3,2,1,0:T(8,128)S(1)}, f32[2,8,64,128]{3,2,1,0:T(8,128)}, u32[]{:S(2)}, u32[]{:S(2)}) collective-permute-start(f32[2,8,64,128]{3,2,1,0:T(8,128)S(1)} %pad_maximum_fusion.4), channel_id=1, source_target_pairs={{0,4},{2,6},{4,0},{6,2},{8,12},{10,14},{12,8},{14,10},{16,20},{18,... | collective-permute-start | bytes 1572872 | tf_op jit(solution)/shard_map/ppermute | solution.py:18
  91.1 11.8 %collective-permute-start.6 = (f32[2,8,64,128]{3,2,1,0:T(8,128)}, f32[2,8,64,128]{3,2,1,0:T(8,128)S(1)}, u32[]{:S(2)}, u32[]{:S(2)}) collective-permute-start(f32[2,8,64,128]{3,2,1,0:T(8,128)} %pad_maximum_fusion.5), channel_id=1, source_target_pairs={{0,8},{2,10},{4,12},{6,14},{8,0},{10,2},{12,4},{14,6},{16,24},{18,... | collective-permute-start | bytes 1572872 | tf_op jit(solution)/shard_map/ppermute | solution.py:18
  103.9 23.3 %collective-permute-start.7 = (f32[2,8,64,128]{3,2,1,0:T(8,128)}, f32[2,8,64,128]{3,2,1,0:T(8,128)}, u32[]{:S(2)}, u32[]{:S(2)}) collective-permute-start(f32[2,8,64,128]{3,2,1,0:T(8,128)} %pad_maximum_fusion.6), channel_id=1, source_target_pairs={{0,16},{2,18},{4,20},{6,22},{8,24},{10,26},{12,28},{14,30},{16,0},... | collective-permute-start | bytes 1572872 | tf_op jit(solution)/shard_map/ppermute | solution.py:18
  113.6 2.4 %collective-permute-start.9 = (f32[2,1,64,128]{3,2,1,0:T(8,128)}, f32[2,1,64,128]{3,2,1,0:T(8,128)S(1)}, u32[]{:S(2)}, u32[]{:S(2)}) collective-permute-start(f32[2,1,64,128]{3,2,1,0:T(8,128)} %get-tuple-element.19), channel_id=1, source_target_pairs={{0,1},{1,0},{2,3},{3,2},{4,5},{5,4},{6,7},{7,6},{8,9},{9,8},{10,11... | collective-permute-start | bytes 196616 | tf_op jit(solution)/shard_map/ppermute | solution.py:28
  113.6 2.4 %collective-permute-start.8 = (f32[2,1,64,128]{3,2,1,0:T(8,128)}, f32[2,1,64,128]{3,2,1,0:T(8,128)S(1)}, u32[]{:S(2)}, u32[]{:S(2)}) collective-permute-start(f32[2,1,64,128]{3,2,1,0:T(8,128)} %get-tuple-element.18), channel_id=1, source_target_pairs={{1,0},{0,1},{3,2},{2,3},{5,4},{4,5},{7,6},{6,7},{9,8},{8,9},{11,10... | collective-permute-start | bytes 196616 | tf_op jit(solution)/shard_map/ppermute | solution.py:29
  114.1 13.1 %copy-start.2 = (f32[2,8,64,128]{3,2,1,0:T(8,128)S(1)}, f32[2,8,64,128]{3,2,1,0:T(8,128)}, u32[]{:S(2)}) copy-start(f32[2,8,64,128]{3,2,1,0:T(8,128)} %copy-done.1) | copy-start | bytes 1572868
  127.2 4.3 %copy-start.5 = (s32[8,128]{1,0:T(8,128)S(1)}, s32[8,128]{1,0:T(8,128)}, u32[]{:S(2)}) copy-start(s32[8,128]{1,0:T(8,128)} %param.9) | copy-start | bytes 12292
  130.8 0.7 copy-start.4
where the time goes:
time: 172 us; the launch traced here: 171 us
  waiting for transfers between devices  90.4 us (53%)
  blocking collectives  38.8 us (23%)
  starting transfers between devices  22.7 us (13%)
  other arithmetic  10.3 us (6%)
  local copies, waits for them, and re-layouts  6.19 us (4%)
  between operations  2.48 us (1%)
    ppermute x8, waiting for transfers between devices, swapped(): lax.ppermute(x, axis, [(i, i ^ 1 << bit) for i in range(lax.axis_size(axi...  90.4 us
    psum x1, blocking collectives, on_device(): total = lax.psum(partial_sum, ('tm', 'space'))  38.8 us
    ppermute x8, starting transfers between devices, swapped(): lax.ppermute(x, axis, [(i, i ^ 1 << bit) for i in range(lax.axis_size(axi...  22.2 us
    sub x1, other arithmetic, on_device(): updated = field - pseudo_step * residual  3.61 us
  transfers between devices with their start and end apart: 10, of which 8 were waited for; matrix products, arithmetic and copies ran while one was open for 3% of the time, Pallas kernels for 0%

commit v1 on v0

v1 whole, which is shorter than its diff:
```python
import math

import jax
import jax.numpy as jnp
from jax import lax
from jax.sharding import PartitionSpec as P

NACT = 128


omega_rate = 0.25
pseudo_step = 0.2
viscosity = 0.2
reaction = 0.5


def spectral_matrix(count):
    steps = jnp.arange(count, dtype=jnp.int32)
    offset = steps[:, None] - steps[None, :]
    theta = math.pi * offset.astype(jnp.float32) / count
    parity = jnp.where(offset % 2 == 0, 1.0, -1.0).astype(jnp.float32)
    skipped = (offset == 0) | (jnp.abs(offset) == count // 2)
    safe_tan = jnp.where(skipped, jnp.float32(1.0), jnp.tan(theta))
    return jnp.where(skipped, jnp.float32(0.0), 0.5 * parity / safe_tan).astype(jnp.float32)


def padded(x, sides, width):
    for axis, dim in sides:
        count, length = (lax.axis_size(axis), x.shape[dim])
        up = [(i, (i + 1) % count) for i in range(count)]
        down = [(j, i) for i, j in up]
        last = lax.slice_in_dim(x, length - width, length, axis=dim)
        initial = lax.slice_in_dim(x, 0, width, axis=dim)
        before = lax.ppermute(last, axis, up)
        after = lax.ppermute(initial, axis, down)
        x = jnp.concatenate([before, x, after], axis=dim)
    return x


def wall_plus(field):
    zeros = jnp.zeros_like(field[:, :1])
    return jnp.concatenate([field[:, 1:], zeros], axis=1)


def wall_minus(field):
    zeros = jnp.zeros_like(field[:, :1])
    return jnp.concatenate([zeros, field[:, :-1]], axis=1)


def time_derivative(adjoint):
    count = lax.axis_size("tm")
    nt_loc, nx, cy, cz = adjoint.shape
    total = count * nt_loc
    rows = nx * cy
    chunk = rows // count
    dmat = spectral_matrix(total)
    blocks = adjoint.reshape(nt_loc, count, chunk, cz)
    gathered = lax.all_to_all(blocks, "tm", 1, 0, tiled=False)
    gathered = gathered.reshape(total, chunk * cz)
    derived = omega_rate * jnp.einsum(
        "ji,jp->ip", dmat, gathered, precision=lax.Precision.HIGHEST
    )
    derived = derived.reshape(count, nt_loc, chunk, cz)
    back = lax.all_to_all(derived, "tm", 0, 1, tiled=False)
    return back.reshape(nt_loc, nx, cy, cz)


def on_device(adjoint, base_flow, source, pulse, actuator):
    count = lax.axis_size("tm")
    position = lax.axis_index("tm")
    total = count * adjoint.shape[0]
    time_term = time_derivative(adjoint)[0]
    field = adjoint[0]
    flux_x = base_flow[0, 0] * field
    flux_y = base_flow[1, 0] * field
    flux_z = base_flow[2, 0] * field
    extended = padded(jnp.stack([field, flux_x]), (("space", 1),), 1)
    advect = 0.5 * (extended[1, 2:] - extended[1, :-2])
    advect = advect + 0.5 * (wall_plus(flux_y) - wall_minus(flux_y))
    advect = advect + 0.5 * (jnp.roll(flux_z, -1, axis=2) - jnp.roll(flux_z, 1, axis=2))
    beside = extended[0, 2:] + extended[0, :-2]
    beside = beside + wall_plus(field) + wall_minus(field)
    beside = beside + jnp.roll(field, -1, axis=2) + jnp.roll(field, 1, axis=2)
    operator = advect + viscosity * (beside - 6.0 * field) - reaction * field
    residual = time_term - operator - source[0]
    updated = field - pseudo_step * residual
    wall = updated[:, 0, :] * pulse[0]
    onehot = (actuator[:, :, None] == jnp.arange(NACT, dtype=jnp.int32)[None, None, :]).astype(
        jnp.float32
    )
    partial_sum = (
        jnp.dot(
            wall.reshape(1, -1),
            onehot.reshape(-1, NACT),
            precision=lax.Precision.HIGHEST,
            preferred_element_type=jnp.float32,
        )[0]
        / total
    )
    share = lax.psum_scatter(partial_sum, "tm", scatter_dimension=0, tiled=True)
    gradient = lax.psum(share, "space")
    return (updated[None], gradient)


def solution(mesh):
    in_specs = (
        P("tm", "space", None, None),
        P(None, "tm", "space", None, None),
        P("tm", "space", None, None),
        P("tm"),
        P("space", None),
    )
    out_specs = (P("tm", "space", None, None), P("tm"))
    return jax.shard_map(
        on_device, mesh=mesh, in_specs=in_specs, out_specs=out_specs, check_vma=False
    )
```

time: 172 us -> 77.4 us (0.45)
  waiting for transfers between devices: 90.4 us -> 12 us
  starting transfers between devices: 22.7 us -> 12.5 us
  other arithmetic: 10.3 us -> 3.41 us
  blocking collectives: 38.8 us -> 41.7 us
  local copies, waits for them, and re-layouts: 6.19 us -> 4.25 us
    ppermute x8 -> x0, waiting for transfers between devices: 90.4 us -> none  [swapped(): lax.ppermute(x, axis, [(i, i ^ 1 << bit) for i in range(lax.axis_size(axi...]
    unnamed x0 -> x1, blocking collectives: none -> 38.8 us
    psum x1, blocking collectives: 38.8 us -> 2.95 us  [on_device(): gradient = lax.psum(share, 'space')]
    ppermute x8 -> x0, starting transfers between devices: 22.2 us -> none  [swapped(): lax.ppermute(x, axis, [(i, i ^ 1 << bit) for i in range(lax.axis_size(axi...]
    all_to_all x0 -> x2, waiting for transfers between devices: none -> 12 us  [the longest x1 7.14 us: time_derivative(): gathered = lax.all_to_all(blocks, 'tm', 1, 0, tiled=False)]
    all_to_all x0 -> x2, starting transfers between devices: none -> 12 us  [the longest x1 8.46 us: time_derivative(): gathered = lax.all_to_all(blocks, 'tm', 1, 0, tiled=False)]
    add x3 -> x0, other arithmetic: 2.53 us -> none  [butterfly_term(): own_re * imag_part + own_im * real_part + oth_re * other[1]]
    sub x1, other arithmetic: 3.61 us -> 1.64 us  [on_device(): updated = field - pseudo_step * residual]
  transfers between devices with their start and end apart: 10 -> 4, of which waited for: 8 -> 2; matrix products, arithmetic and copies ran while one was open for 3% -> 8% of each run, Pallas kernels for 0% -> 0%
where the time goes in v1:
time: 77.4 us; the launch traced here: 76.9 us
  blocking collectives  41.7 us (54%)
  starting transfers between devices  12.5 us (16%)
  waiting for transfers between devices  12 us (16%)
  local copies, waits for them, and re-layouts  4.25 us (5%)
  other arithmetic  3.41 us (4%)
  between operations  2.04 us (3%)
  matrix products  0.91 us (1%)
    unnamed x1, blocking collectives  38.8 us
    all_to_all x1, starting transfers between devices, time_derivative(): gathered = lax.all_to_all(blocks, 'tm', 1, 0, tiled=False)  8.46 us
    all_to_all x1, waiting for transfers between devices, time_derivative(): gathered = lax.all_to_all(blocks, 'tm', 1, 0, tiled=False)  7.14 us
    all_to_all x1, waiting for transfers between devices, time_derivative(): back = lax.all_to_all(derived, 'tm', 0, 1, tiled=False)  4.9 us
    all_to_all x1, starting transfers between devices, time_derivative(): back = lax.all_to_all(derived, 'tm', 0, 1, tiled=False)  3.55 us
    psum x1, blocking collectives, on_device(): gradient = lax.psum(share, 'space')  2.95 us
    unnamed x13, local copies, waits for them, and re-layouts  2.15 us
    sub x1, other arithmetic, on_device(): updated = field - pseudo_step * residual  1.64 us
  transfers between devices with their start and end apart: 4, of which 2 were waited for; matrix products, arithmetic and copies ran while one was open for 8% of the time, Pallas kernels for 0%

profile of v1, /device:TPU:0, one launch (start us, length us, event | category | flops | bytes accessed | tf_op | source)
XLA Modules:
  0.0 76.9 jit_solution(1893989870560593265)
XLA Ops:
  0.6 8.5 %all-to-all-start = ((f32[1,1,16,32,128]{4,3,1,0,2:T(8,128)}), f32[1,1,16,32,128]{4,3,1,0,2:T(8,128)S(1)}, u32[]{:S(2)}, u32[]{:S(2)}) async-start(f32[1,1,16,32,128]{4,3,1,0,2:T(8,128)} %bitcast.77), calls=%async_computation | async-start | bytes 524288 | tf_op jit(solution)/shard_map/all_to_all | solution.py:58
  9.1 1.1 %bitcast_multiply_fusion.2 = f32[1,8,64,128]{3,2,1,0:T(8,128)S(1)} fusion(f32[1,8,64,128]{3,2,1,0:T(8,128)S(1)} %copy-done, f32[3,1,8,64,128]{4,3,2,1,0:T(8,128)} %param.6), kind=kLoop, calls=%fused_computation.33 | loop fusion | flops 65536 | bytes 786432 | tf_op jit(solution)/shard_map/mul | solution.py:74
  10.2 0.7 pad_maximum_fusion.5
  10.8 0.5 collective-permute-start
  11.4 0.1 bitcast_multiply_fusion.1
  11.4 0.1 fusion.68
  11.5 0.1 fusion.69
  11.7 0.1 fusion.66
  11.8 7.1 %all-to-all-done = f32[1,1,16,32,128]{4,3,1,0,2:T(8,128)S(1)} async-done(((f32[1,1,16,32,128]{4,3,1,0,2:T(8,128)}), f32[1,1,16,32,128]{4,3,1,0,2:T(8,128)S(1)}, u32[]{:S(2)}, u32[]{:S(2)}) %all-to-all-start) | async-done | bytes 262176 | tf_op jit(solution)/shard_map/all_to_all | solution.py:58
  19.0 0.5 fusion
  19.5 0.8 copy.9
  20.3 3.5 %all-to-all-start.1 = ((f32[16,1,1,32,128]{4,3,2,1,0:T(8,128)}), f32[16,1,1,32,128]{4,3,2,1,0:T(8,128)S(1)}, u32[]{:S(2)}, u32[]{:S(2)}) async-start(f32[16,1,1,32,128]{4,3,2,1,0:T(8,128)} %bitcast.2), calls=%async_computation.1 | async-start | bytes 524288 | tf_op jit(solution)/shard_map/all_to_all | solution.py:64
  23.8 0.1 fusion.67
  24.0 0.7 fusion.65
  24.7 0.8 %fusion.64 = (f32[8,63,128]{2,1,0:T(8,128)}, f32[8,63,128]{2,1,0:T(8,128)}) fusion(f32[8,64,128]{2,1,0:T(8,128)S(1)} %get-tuple-element.2), kind=kLoop, calls=%fused_computation.78 | loop fusion | bytes 1032192 | tf_op jit(solution)/shard_map/slice | solution.py:42
  26.2 0.0 copy-start.4
  26.2 0.6 copy-done.4
  26.9 0.6 dynamic-slice
  28.2 4.9 %all-to-all-done.1 = f32[16,1,1,32,128]{4,3,2,1,0:T(8,128)S(1)} async-done(((f32[16,1,1,32,128]{4,3,2,1,0:T(8,128)}), f32[16,1,1,32,128]{4,3,2,1,0:T(8,128)S(1)}, u32[]{:S(2)}, u32[]{:S(2)}) %all-to-all-start.1) | async-done | bytes 262176 | tf_op jit(solution)/shard_map/all_to_all | solution.py:64
  33.1 1.6 %fusion.17 = f32[8,64,128]{2,1,0:T(8,128)S(1)} fusion(f32[8,64,128]{2,1,0:T(8,128)S(1)} %bitcast.81, f32[2,1,64,128]{3,2,1,0:T(8,128)S(1)} %collective-permute-done.1, f32[1,8,64,128]{3,2,1,0:T(8,128)S(1)} %bitcast_multiply_fusion.2, f32[1,8,64,128]{3,2,1,0:T(8,128)S(1)} %copy-done, f32[2,1,64,128]{3,2,1,0:T(8,128)S(1)} %collective-permute-done, ...), kind=kLoop, calls=%fused_computation.21 | loop fusion | flops 2162688 | bytes 3522560 | tf_op jit(solution)/shard_map/sub | solution.py:86
  34.7 0.4 fusion.1
  35.1 38.8 %all-reduce.4 = f32[128]{0:T(128)S(1)} all-reduce(f32[128]{0:T(128)S(1)} %fusion.1), channel_id=2, replica_groups=mesh['tm'=16,'space'=2] {'tm'}, use_global_device_ids=true, to_apply=%region_0.1.clone | all-reduce | flops 128 | bytes 1024
  73.9 0.1 dynamic-slice.1
  73.9 2.9 %psum.7 = f32[8]{0:T(128)} all-reduce(f32[8]{0:T(128)S(1)} %dynamic-slice.1), channel_id=1, replica_groups=mesh['tm'=16,'space'=2] {'space'}, use_global_device_ids=true, to_apply=%region_1.2 | all-reduce | flops 8 | bytes 64 | tf_op jit(solution)/shard_map/psum | solution.py:101
  (11 shorter events, 0.0 us)
Async XLA Ops:
  0.6 8.5 %copy-start = (f32[1,8,64,128]{3,2,1,0:T(8,128)S(1)}, f32[1,8,64,128]{3,2,1,0:T(8,128)}, u32[]{:S(2)}) copy-start(f32[1,8,64,128]{3,2,1,0:T(8,128)} %param.5) | copy-start | bytes 786436
  0.6 18.3 %all-to-all-start = ((f32[1,1,16,32,128]{4,3,1,0,2:T(8,128)}), f32[1,1,16,32,128]{4,3,1,0,2:T(8,128)S(1)}, u32[]{:S(2)}, u32[]{:S(2)}) async-start(f32[1,1,16,32,128]{4,3,1,0,2:T(8,128)} %bitcast.77), calls=%async_computation | async-start | bytes 524288 | tf_op jit(solution)/shard_map/all_to_all | solution.py:58
  9.1 2.2 %copy-start.1 = (f32[3,1,8,64,128]{4,3,2,1,0:T(8,128)S(1)}, f32[3,1,8,64,128]{4,3,2,1,0:T(8,128)}, u32[]{:S(2)}) copy-start(f32[3,1,8,64,128]{4,3,2,1,0:T(8,128)} %param.6) | copy-start | bytes 2359300
  10.8 17.3 %collective-permute-start.1 = (f32[2,1,64,128]{3,2,1,0:T(8,128)}, f32[2,1,64,128]{3,2,1,0:T(8,128)S(1)}, u32[]{:S(2)}, u32[]{:S(2)}) collective-permute-start(f32[2,1,64,128]{3,2,1,0:T(8,128)} %get-tuple-element.5), channel_id=1, source_target_pairs={{0,1},{1,0},{2,3},{3,2},{4,5},{5,4},{6,7},{7,6},{8,9},{9,8},{10,11... | collective-permute-start | bytes 196616 | tf_op jit(solution)/shard_map/ppermute | solution.py:34
  10.8 17.3 %collective-permute-start = (f32[2,1,64,128]{3,2,1,0:T(8,128)}, f32[2,1,64,128]{3,2,1,0:T(8,128)S(1)}, u32[]{:S(2)}, u32[]{:S(2)}) collective-permute-start(f32[2,1,64,128]{3,2,1,0:T(8,128)} %get-tuple-element.4), channel_id=1, source_target_pairs={{1,0},{0,1},{3,2},{2,3},{5,4},{4,5},{7,6},{6,7},{9,8},{8,9},{11,10... | collective-permute-start | bytes 196616 | tf_op jit(solution)/shard_map/ppermute | solution.py:35
  20.3 12.8 %all-to-all-start.1 = ((f32[16,1,1,32,128]{4,3,2,1,0:T(8,128)}), f32[16,1,1,32,128]{4,3,2,1,0:T(8,128)S(1)}, u32[]{:S(2)}, u32[]{:S(2)}) async-start(f32[16,1,1,32,128]{4,3,2,1,0:T(8,128)} %bitcast.2), calls=%async_computation.1 | async-start | bytes 524288 | tf_op jit(solution)/shard_map/all_to_all | solution.py:64
  26.2 0.7 copy-start.4
  33.1 1.7 %copy-start.3 = (s32[8,128]{1,0:T(8,128)S(1)}, s32[8,128]{1,0:T(8,128)}, u32[]{:S(2)}) copy-start(s32[8,128]{1,0:T(8,128)} %param.9) | copy-start | bytes 12292
  34.7 42.2 %copy-start.2 = (f32[8,64,128]{2,1,0:T(8,128)}, f32[8,64,128]{2,1,0:T(8,128)S(1)}, u32[]{:S(2)}) copy-start(f32[8,64,128]{2,1,0:T(8,128)S(1)} %fusion.17) | copy-start | bytes 786436

commit v2 on v1

--- a/solution.py
+++ b/solution.py
@@ -97,8 +97,12 @@
         )[0]
         / total
     )
-    share = lax.psum_scatter(partial_sum, "tm", scatter_dimension=0, tiled=True)
-    gradient = lax.psum(share, "space")
+    share = NACT // count
+    groups = lax.axis_size("space")
+    blocks = jnp.repeat(partial_sum.reshape(count, 1, share), groups, axis=1)
+    blocks = blocks.reshape(count * groups, share)
+    gathered = lax.all_to_all(blocks, ("tm", "space"), 0, 0, tiled=True)
+    gradient = jnp.sum(gathered, axis=0)
     return (updated[None], gradient)
 
 

time: 77.4 us -> 47.1 us (0.61)
  blocking collectives: 41.7 us -> 9.48 us
  waiting for transfers between devices: 12 us -> 14 us
  matrix products: 0.91 us -> 2.44 us
  local copies, waits for them, and re-layouts: 4.25 us -> 2.9 us
    unnamed x1 -> x0, blocking collectives: 38.8 us -> none
    all_to_all x0 -> x1, blocking collectives: none -> 9.48 us  [on_device(): gathered = lax.all_to_all(blocks, ('tm', 'space'), 0, 0, tiled=True)]
    psum x1 -> x0, blocking collectives: 2.95 us -> none  [on_device(): gradient = lax.psum(share, 'space')]
    all_to_all x1, waiting for transfers between devices: 4.9 us -> 7.61 us  [time_derivative(): back = lax.all_to_all(derived, 'tm', 0, 1, tiled=False)]
    dot_general x1, matrix products: 0.37 us -> 1.9 us  [on_device(): jnp.dot(wall.reshape(1, -1), onehot.reshape(-1, NACT), precision=lax.Prec...]
    unnamed x13 -> x9, local copies, waits for them, and re-layouts: 2.15 us -> 0.77 us
    all_to_all x1, waiting for transfers between devices: 7.14 us -> 6.35 us  [time_derivative(): gathered = lax.all_to_all(blocks, 'tm', 1, 0, tiled=False)]
  transfers between devices with their start and end apart: 4 -> 4, of which waited for: 2 -> 2; matrix products, arithmetic and copies ran while one was open for 8% -> 11% of each run, Pallas kernels for 0% -> 0%
where the time goes in v2:
time: 47.1 us; the launch traced here: 46.7 us
  waiting for transfers between devices  14 us (30%)
  starting transfers between devices  12.5 us (27%)
  blocking collectives  9.48 us (20%)
  other arithmetic  3.97 us (8%)
  local copies, waits for them, and re-layouts  2.9 us (6%)
  matrix products  2.44 us (5%)
  between operations  1.41 us (3%)
    all_to_all x1, blocking collectives, on_device(): gathered = lax.all_to_all(blocks, ('tm', 'space'), 0, 0, tiled=True)  9.48 us
    all_to_all x1, starting transfers between devices, time_derivative(): gathered = lax.all_to_all(blocks, 'tm', 1, 0, tiled=False)  8.46 us
    all_to_all x1, waiting for transfers between devices, time_derivative(): back = lax.all_to_all(derived, 'tm', 0, 1, tiled=False)  7.61 us
    all_to_all x1, waiting for transfers between devices, time_derivative(): gathered = lax.all_to_all(blocks, 'tm', 1, 0, tiled=False)  6.35 us
    all_to_all x1, starting transfers between devices, time_derivative(): back = lax.all_to_all(derived, 'tm', 0, 1, tiled=False)  3.55 us
    dot_general x1, matrix products, on_device(): jnp.dot(wall.reshape(1, -1), onehot.reshape(-1, NACT), precision=lax.Prec...  1.9 us
    sub x1, other arithmetic, on_device(): updated = field - pseudo_step * residual  1.64 us
    slice x2, local copies, waits for them, and re-layouts, wall_plus(): return jnp.concatenate([field[:, 1:], zeros], axis=1)  1.58 us
  transfers between devices with their start and end apart: 4, of which 2 were waited for; matrix products, arithmetic and copies ran while one was open for 11% of the time, Pallas kernels for 0%

profile of v2, /device:TPU:0, one launch (start us, length us, event | category | flops | bytes accessed | tf_op | source)
XLA Modules:
  0.0 46.7 jit_solution(8733008964079224648)
XLA Ops:
  0.6 8.5 %all-to-all-start = ((f32[1,1,16,32,128]{4,3,1,0,2:T(8,128)}), f32[1,1,16,32,128]{4,3,1,0,2:T(8,128)S(1)}, u32[]{:S(2)}, u32[]{:S(2)}) async-start(f32[1,1,16,32,128]{4,3,1,0,2:T(8,128)} %bitcast.75), calls=%async_computation | async-start | bytes 524288 | tf_op jit(solution)/shard_map/all_to_all | solution.py:58
  9.1 0.0 copy-start.1
  9.1 1.1 %bitcast_multiply_fusion.2 = f32[1,8,64,128]{3,2,1,0:T(8,128)S(1)} fusion(f32[1,8,64,128]{3,2,1,0:T(8,128)S(1)} %copy-done, f32[3,1,8,64,128]{4,3,2,1,0:T(8,128)} %param.6), kind=kLoop, calls=%fused_computation.32 | loop fusion | flops 65536 | bytes 786432 | tf_op jit(solution)/shard_map/mul | solution.py:74
  10.2 0.7 %pad_maximum_fusion.5 = (f32[2,1,64,128]{3,2,1,0:T(8,128)}, f32[2,1,64,128]{3,2,1,0:T(8,128)}) fusion(f32[1,8,64,128]{3,2,1,0:T(8,128)S(1)} %bitcast_multiply_fusion.2, f32[1,8,64,128]{3,2,1,0:T(8,128)S(1)} %copy-done), kind=kLoop, calls=%fused_computation.36 | loop fusion | flops 32768 | bytes 655360 | tf_op jit(solution)/shard_map/slice | solution.py:33
  10.8 0.0 collective-permute-start.1
  10.8 0.5 %collective-permute-start = (f32[2,1,64,128]{3,2,1,0:T(8,128)}, f32[2,1,64,128]{3,2,1,0:T(8,128)S(1)}, u32[]{:S(2)}, u32[]{:S(2)}) collective-permute-start(f32[2,1,64,128]{3,2,1,0:T(8,128)} %get-tuple-element.4), channel_id=1, source_target_pairs={{1,0},{0,1},{3,2},{2,3},{5,4},{4,5},{7,6},{6,7},{9,8},{8,9},{11,10... | collective-permute-start | bytes 196616 | tf_op jit(solution)/shard_map/ppermute | solution.py:35
  11.3 0.1 bitcast_multiply_fusion.1
  11.4 0.1 fusion.70
  11.5 0.1 fusion.71
  12.3 0.1 fusion.68
  12.5 0.1 fusion.69
  12.6 6.4 %all-to-all-done = f32[1,1,16,32,128]{4,3,1,0,2:T(8,128)S(1)} async-done(((f32[1,1,16,32,128]{4,3,1,0,2:T(8,128)}), f32[1,1,16,32,128]{4,3,1,0,2:T(8,128)S(1)}, u32[]{:S(2)}, u32[]{:S(2)}) %all-to-all-start) | async-done | bytes 262176 | tf_op jit(solution)/shard_map/all_to_all | solution.py:58
  19.0 0.5 %fusion = f32[2,8,32,128]{3,1,2,0:T(8,128)S(1)} fusion(f32[2,8,32,128]{3,2,1,0:T(8,128)S(1)} %bitcast.80), kind=kOutput, calls=%fused_computation.1 | convolution fusion | flops 12654592 | bytes 524288 | tf_op jit(solution)/shard_map/ji,jp->ip/dot_general | solution.py:60
  19.5 0.8 %copy.10 = f32[2,8,32,128]{3,2,1,0:T(8,128)} copy(f32[2,8,32,128]{3,1,2,0:T(8,128)S(1)} %fusion) | data formatting | bytes 524288
  20.3 3.5 %all-to-all-start.1 = ((f32[16,1,1,32,128]{4,3,2,1,0:T(8,128)}), f32[16,1,1,32,128]{4,3,2,1,0:T(8,128)S(1)}, u32[]{:S(2)}, u32[]{:S(2)}) async-start(f32[16,1,1,32,128]{4,3,2,1,0:T(8,128)} %bitcast.2), calls=%async_computation.1 | async-start | bytes 524288 | tf_op jit(solution)/shard_map/all_to_all | solution.py:64
  23.8 0.7 %fusion.67 = (f32[8,63,128]{2,1,0:T(8,128)S(1)}, f32[8,63,128]{2,1,0:T(8,128)}) fusion(f32[8,64,128]{2,1,0:T(8,128)S(1)} %bitcast.78), kind=kLoop, calls=%fused_computation.81 | loop fusion | bytes 1032192 | tf_op jit(solution)/shard_map/slice | solution.py:42
  24.6 0.9 %fusion.66 = (f32[8,63,128]{2,1,0:T(8,128)}, f32[8,63,128]{2,1,0:T(8,128)}) fusion(f32[8,64,128]{2,1,0:T(8,128)S(1)} %get-tuple-element.2), kind=kLoop, calls=%fused_computation.80 | loop fusion | bytes 1032192 | tf_op jit(solution)/shard_map/slice | solution.py:42
  25.4 0.0 collective-permute-done.1
  25.4 7.6 %all-to-all-done.1 = f32[16,1,1,32,128]{4,3,2,1,0:T(8,128)S(1)} async-done(((f32[16,1,1,32,128]{4,3,2,1,0:T(8,128)}), f32[16,1,1,32,128]{4,3,2,1,0:T(8,128)S(1)}, u32[]{:S(2)}, u32[]{:S(2)}) %all-to-all-start.1) | async-done | bytes 262176 | tf_op jit(solution)/shard_map/all_to_all | solution.py:64
  33.1 1.6 %fusion.18 = f32[8,64,128]{2,1,0:T(8,128)S(1)} fusion(f32[8,64,128]{2,1,0:T(8,128)S(1)} %bitcast.79, f32[2,1,64,128]{3,2,1,0:T(8,128)S(1)} %collective-permute-done.1, f32[1,8,64,128]{3,2,1,0:T(8,128)S(1)} %bitcast_multiply_fusion.2, f32[1,8,64,128]{3,2,1,0:T(8,128)S(1)} %copy-done, f32[2,1,64,128]{3,2,1,0:T(8,128)S(1)} %collective-permute-done, ...), kind=kLoop, calls=%fused_computation.20 | loop fusion | flops 2162688 | bytes 3522560 | tf_op jit(solution)/shard_map/sub | solution.py:86
  34.7 0.0 copy-start.2
  34.7 1.9 %fusion.1 = f32[1,16,8]{2,0,1:T(1,128)S(1)} fusion(s32[16,8]{1,0:T(8,128)S(1)} %multiply_add_fusion, s32[1024]{0:T(1024)S(1)} %bitcast.84, f32[8,64,128]{2,1,0:T(8,128)S(1)} %fusion.18, f32[]{:T(128)} %bitcast.74), kind=kOutput, calls=%fused_computation.2 | convolution fusion | flops 1704960 | bytes 16900 | tf_op jit(solution)/shard_map/dot_general | solution.py:92
  36.6 9.5 %all_to_all.27 = f32[32,1,8]{2,1,0:T(1,128)S(1)} all-to-all(f32[32,1,8]{2,1,0:T(1,128)S(1)} %bitcast.82), channel_id=1, replica_groups=mesh['tm'=16,'space'=2] {'tm','space'}, dimensions={0} | all-to-all | bytes 2048 | tf_op jit(solution)/shard_map/all_to_all | solution.py:104
  46.1 0.6 %reduce_sum.9 = f32[8]{0:T(128)} reduce(f32[32,1,8]{2,1,0:T(1,128)S(1)} %all_to_all.27, f32[]{:T(128)} %constant.15.clone.1), dimensions={0,1}, to_apply=%region_0.1 | reduce | flops 248 | bytes 1060 | tf_op jit(solution)/shard_map/reduce_sum | solution.py:105
  (10 shorter events, 0.0 us)
Async XLA Ops:
  0.6 8.5 %copy-start = (f32[1,8,64,128]{3,2,1,0:T(8,128)S(1)}, f32[1,8,64,128]{3,2,1,0:T(8,128)}, u32[]{:S(2)}) copy-start(f32[1,8,64,128]{3,2,1,0:T(8,128)} %param.5) | copy-start | bytes 786436
  0.6 18.3 %all-to-all-start = ((f32[1,1,16,32,128]{4,3,1,0,2:T(8,128)}), f32[1,1,16,32,128]{4,3,1,0,2:T(8,128)S(1)}, u32[]{:S(2)}, u32[]{:S(2)}) async-start(f32[1,1,16,32,128]{4,3,1,0,2:T(8,128)} %bitcast.75), calls=%async_computation | async-start | bytes 524288 | tf_op jit(solution)/shard_map/all_to_all | solution.py:58
  9.1 2.2 %copy-start.1 = (f32[3,1,8,64,128]{4,3,2,1,0:T(8,128)S(1)}, f32[3,1,8,64,128]{4,3,2,1,0:T(8,128)}, u32[]{:S(2)}) copy-start(f32[3,1,8,64,128]{4,3,2,1,0:T(8,128)} %param.6) | copy-start | bytes 2359300
  10.8 14.6 %collective-permute-start.1 = (f32[2,1,64,128]{3,2,1,0:T(8,128)}, f32[2,1,64,128]{3,2,1,0:T(8,128)S(1)}, u32[]{:S(2)}, u32[]{:S(2)}) collective-permute-start(f32[2,1,64,128]{3,2,1,0:T(8,128)} %get-tuple-element.5), channel_id=1, source_target_pairs={{0,1},{1,0},{2,3},{3,2},{4,5},{5,4},{6,7},{7,6},{8,9},{9,8},{10,11... | collective-permute-start | bytes 196616 | tf_op jit(solution)/shard_map/ppermute | solution.py:34
  10.8 14.6 %collective-permute-start = (f32[2,1,64,128]{3,2,1,0:T(8,128)}, f32[2,1,64,128]{3,2,1,0:T(8,128)S(1)}, u32[]{:S(2)}, u32[]{:S(2)}) collective-permute-start(f32[2,1,64,128]{3,2,1,0:T(8,128)} %get-tuple-element.4), channel_id=1, source_target_pairs={{1,0},{0,1},{3,2},{2,3},{5,4},{4,5},{7,6},{6,7},{9,8},{8,9},{11,10... | collective-permute-start | bytes 196616 | tf_op jit(solution)/shard_map/ppermute | solution.py:35
  20.3 12.8 %all-to-all-start.1 = ((f32[16,1,1,32,128]{4,3,2,1,0:T(8,128)}), f32[16,1,1,32,128]{4,3,2,1,0:T(8,128)S(1)}, u32[]{:S(2)}, u32[]{:S(2)}) async-start(f32[16,1,1,32,128]{4,3,2,1,0:T(8,128)} %bitcast.2), calls=%async_computation.1 | async-start | bytes 524288 | tf_op jit(solution)/shard_map/all_to_all | solution.py:64
  33.1 1.7 %copy-start.3 = (s32[8,128]{1,0:T(8,128)S(1)}, s32[8,128]{1,0:T(8,128)}, u32[]{:S(2)}) copy-start(s32[8,128]{1,0:T(8,128)} %param.9) | copy-start | bytes 12292
  34.7 12.0 %copy-start.2 = (f32[8,64,128]{2,1,0:T(8,128)}, f32[8,64,128]{2,1,0:T(8,128)S(1)}, u32[]{:S(2)}) copy-start(f32[8,64,128]{2,1,0:T(8,128)S(1)} %fusion.18) | copy-start | bytes 786436

commit v3 on v1

--- a/solution.py
+++ b/solution.py
@@ -47,29 +47,34 @@
     return jnp.concatenate([zeros, field[:, :-1]], axis=1)
 
 
-def time_derivative(adjoint):
-    count = lax.axis_size("tm")
-    nt_loc, nx, cy, cz = adjoint.shape
-    total = count * nt_loc
-    rows = nx * cy
-    chunk = rows // count
-    dmat = spectral_matrix(total)
-    blocks = adjoint.reshape(nt_loc, count, chunk, cz)
-    gathered = lax.all_to_all(blocks, "tm", 1, 0, tiled=False)
-    gathered = gathered.reshape(total, chunk * cz)
-    derived = omega_rate * jnp.einsum(
-        "ji,jp->ip", dmat, gathered, precision=lax.Precision.HIGHEST
-    )
-    derived = derived.reshape(count, nt_loc, chunk, cz)
-    back = lax.all_to_all(derived, "tm", 0, 1, tiled=False)
-    return back.reshape(nt_loc, nx, cy, cz)
+def butterfly_sum(x, axis):
+    groups = lax.axis_size(axis)
+    bit = 1
+    while bit < groups:
+        x = x + lax.ppermute(x, axis, [(i, i ^ bit) for i in range(groups)])
+        bit *= 2
+    return x
 
 
 def on_device(adjoint, base_flow, source, pulse, actuator):
     count = lax.axis_size("tm")
     position = lax.axis_index("tm")
-    total = count * adjoint.shape[0]
-    time_term = time_derivative(adjoint)[0]
+    nt_loc, nx, cy, cz = adjoint.shape
+    total = count * nt_loc
+    chunk = nx * cy // count
+    share = NACT // count
+    dmat = spectral_matrix(total)
+
+    blocks = adjoint.reshape(nt_loc, count, chunk, cz)
+    pulse_row = jnp.broadcast_to(pulse.reshape(nt_loc, 1, 1, 1), (nt_loc, count, 1, cz))
+    outgoing = jnp.concatenate([blocks, pulse_row], axis=2)
+    incoming = lax.all_to_all(outgoing, "tm", 1, 0, tiled=False)
+    pulses = incoming[:, :, chunk, 0].reshape(total)
+    gathered = incoming[:, :, :chunk].reshape(total, chunk * cz)
+    derived = omega_rate * jnp.einsum(
+        "ji,jp->ip", dmat, gathered, precision=lax.Precision.HIGHEST
+    )
+
     field = adjoint[0]
     flux_x = base_flow[0, 0] * field
     flux_y = base_flow[1, 0] * field
@@ -82,23 +87,32 @@
     beside = beside + wall_plus(field) + wall_minus(field)
     beside = beside + jnp.roll(field, -1, axis=2) + jnp.roll(field, 1, axis=2)
     operator = advect + viscosity * (beside - 6.0 * field) - reaction * field
-    residual = time_term - operator - source[0]
-    updated = field - pseudo_step * residual
-    wall = updated[:, 0, :] * pulse[0]
+
+    kept = field + pseudo_step * (operator + source[0])
+    walls = jnp.stack([pulse[0] * kept[:, 0, :], field[:, 0, :]]).reshape(2, -1)
     onehot = (actuator[:, :, None] == jnp.arange(NACT, dtype=jnp.int32)[None, None, :]).astype(
         jnp.float32
     )
-    partial_sum = (
-        jnp.dot(
-            wall.reshape(1, -1),
-            onehot.reshape(-1, NACT),
-            precision=lax.Precision.HIGHEST,
-            preferred_element_type=jnp.float32,
-        )[0]
-        / total
+    terms = jnp.dot(
+        walls,
+        onehot.reshape(-1, NACT),
+        precision=lax.Precision.HIGHEST,
+        preferred_element_type=jnp.float32,
     )
-    share = lax.psum_scatter(partial_sum, "tm", scatter_dimension=0, tiled=True)
-    gradient = lax.psum(share, "space")
+    terms = butterfly_sum(terms, "space")
+    weights = jnp.dot(dmat, pulses, precision=lax.Precision.HIGHEST)
+    own_weight = lax.dynamic_index_in_dim(weights, position, keepdims=False)
+    partial_sum = (terms[0] - pseudo_step * omega_rate * own_weight * terms[1]) / total
+    grad_row = jnp.pad(partial_sum.reshape(count, 1, 1, share), ((0, 0), (0, 0), (0, 0), (0, cz - share)))
+
+    derived = derived.reshape(count, nt_loc, chunk, cz)
+    outgoing = jnp.concatenate([derived, grad_row], axis=2)
+    incoming = lax.all_to_all(outgoing, "tm", 0, 1, tiled=False)
+    time_term = incoming[:, :, :chunk].reshape(nt_loc, nx, cy, cz)[0]
+    gradient = jnp.sum(incoming[0, :, chunk, :share], axis=0)
+
+    residual = time_term - operator - source[0]
+    updated = field - pseudo_step * residual
     return (updated[None], gradient)
 
 

time: 77.4 us -> 41.4 us (0.53)
  blocking collectives: 41.7 us -> 12.9 us
  waiting for transfers between devices: 12 us -> 6.58 us
  starting transfers between devices: 12.5 us -> 8.96 us
  local copies, waits for them, and re-layouts: 4.25 us -> 6.76 us
    unnamed x1 -> x0, blocking collectives: 38.8 us -> none
    all_to_all x0 -> x1, blocking collectives: none -> 12.9 us  [on_device(): incoming = lax.all_to_all(outgoing, 'tm', 0, 1, tiled=False)]
    all_to_all x2 -> x1, waiting for transfers between devices: 12 us -> 5.45 us  [on_device(): incoming = lax.all_to_all(outgoing, 'tm', 1, 0, tiled=False)]
    all_to_all x2 -> x1, starting transfers between devices: 12 us -> 8.29 us  [on_device(): incoming = lax.all_to_all(outgoing, 'tm', 1, 0, tiled=False)]
    psum x1 -> x0, blocking collectives: 2.95 us -> none  [on_device(): gradient = lax.psum(share, 'space')]
    slice x2 -> x5, local copies, waits for them, and re-layouts: 0.26 us -> 2.17 us  [the longest x1 1.2 us: on_device(): flux_y = base_flow[1, 0] * field]
    slice x2 -> x1, local copies, waits for them, and re-layouts: 1.58 us -> 0.07 us  [wall_plus(): return jnp.concatenate([field[:, 1:], zeros], axis=1)]
    ppermute x0 -> x1, waiting for transfers between devices: none -> 1.12 us  [butterfly_sum(): x = x + lax.ppermute(x, axis, [(i, i ^ bit) for i in range(groups)])]
  transfers between devices with their start and end apart: 4 -> 4, of which waited for: 2 -> 2; matrix products, arithmetic and copies ran while one was open for 8% -> 7% of each run, Pallas kernels for 0% -> 0%
where the time goes in v3:
time: 41.4 us; the launch traced here: 41.1 us
  blocking collectives  12.9 us (31%)
  starting transfers between devices  8.96 us (22%)
  local copies, waits for them, and re-layouts  6.76 us (16%)
  waiting for transfers between devices  6.58 us (16%)
  other arithmetic  2.65 us (6%)
  between operations  2.1 us (5%)
  matrix products  1.12 us (3%)
    all_to_all x1, blocking collectives, on_device(): incoming = lax.all_to_all(outgoing, 'tm', 0, 1, tiled=False)  12.9 us
    all_to_all x1, starting transfers between devices, on_device(): incoming = lax.all_to_all(outgoing, 'tm', 1, 0, tiled=False)  8.29 us
    all_to_all x1, waiting for transfers between devices, on_device(): incoming = lax.all_to_all(outgoing, 'tm', 1, 0, tiled=False)  5.45 us
    unnamed x9, local copies, waits for them, and re-layouts  2.52 us
    slice x1, local copies, waits for them, and re-layouts, on_device(): flux_y = base_flow[1, 0] * field  1.2 us
    ppermute x1, waiting for transfers between devices, butterfly_sum(): x = x + lax.ppermute(x, axis, [(i, i ^ bit) for i in range(groups)])  1.12 us
    broadcast_in_dim x1, local copies, waits for them, and re-layouts, on_device(): incoming = lax.all_to_all(outgoing, 'tm', 1, 0, tiled=False)  0.89 us
  transfers between devices with their start and end apart: 4, of which 2 were waited for; matrix products, arithmetic and copies ran while one was open for 7% of the time, Pallas kernels for 0%

profile of v3, /device:TPU:0, one launch (start us, length us, event | category | flops | bytes accessed | tf_op | source)
XLA Modules:
  0.0 41.1 jit_solution(4664880379909792156)
XLA Ops:
  0.6 1.2 %fusion.58 = (f32[1,1,8,64,128]{4,3,2,1,0:T(8,128)S(1)}, f32[1,1,8,64,128]{4,3,2,1,0:T(8,128)S(1)}, f32[1,1,8,64,128]{4,3,2,1,0:T(8,128)S(1)}) fusion(f32[3,1,8,64,128]{4,3,2,1,0:T(8,128)} %param.6), kind=kLoop, calls=%fused_computation.90 | loop fusion | bytes 1572864 | tf_op jit(solution)/shard_map/slice | solution.py:80
  1.9 0.3 copy_bitcast_fusion.5
  2.3 0.5 %collective-permute-start = (f32[2,1,64,128]{3,1,2,0:T(1,128)S(1)}, f32[2,1,64,128]{3,1,2,0:T(1,128)S(1)}, u32[]{:S(2)}, u32[]{:S(2)}) collective-permute-start(f32[2,1,64,128]{3,1,2,0:T(1,128)S(1)} %get-tuple-element.13), channel_id=1, source_target_pairs={{1,0},{0,1},{3,2},{2,3},{5,4},{4,5},{7,6},{6,7},{9,8},{8,9},{11,10... | collective-permute-start | bytes 196616 | tf_op jit(solution)/shard_map/ppermute | solution.py:35
  3.5 0.9 %pad_bitcast_fusion = f32[1,1,16,33,128]{4,1,3,0,2:T(1,128)} fusion(f32[1,16,32,128]{3,0,2,1:T(1,128)S(1)} %bitcast.90, f32[]{:T(128)} %bitcast.88), kind=kLoop, calls=%fused_computation.7 | loop fusion | bytes 532484 | tf_op jit(solution)/shard_map/broadcast_in_dim | solution.py:71
  4.4 8.3 %all-to-all-start = ((f32[1,1,16,33,128]{4,1,3,0,2:T(1,128)}), f32[1,1,16,33,128]{4,1,3,0,2:T(1,128)S(1)}, u32[]{:S(2)}, u32[]{:S(2)}) async-start(f32[1,1,16,33,128]{4,1,3,0,2:T(1,128)} %pad_bitcast_fusion), calls=%async_computation | async-start | bytes 540672 | tf_op jit(solution)/shard_map/all_to_all | solution.py:71
  12.7 0.4 %fusion.18 = (f32[8,64,128]{2,0,1:T(8,128)S(1)}, f32[8,64,128]{2,0,1:T(8,128)S(1)}) fusion(f32[1,1,8,64,128]{4,3,2,1,0:T(8,128)S(1)} %get-tuple-element.10, f32[1,8,64,128]{3,2,1,0:T(8,128)S(1)} %copy-done, f32[1,1,8,64,128]{4,3,2,1,0:T(8,128)S(1)} %get-tuple-element.12), kind=kLoop, calls=%fused_computation.34 | loop fusion | flops 131072 | bytes 1310720 | tf_op jit(solution)/shard_map/mul | solution.py:80
  13.2 0.2 fusion.62
  13.4 0.2 fusion.61
  13.6 0.9 %copy-done.1 = f32[1,8,64,128]{3,2,1,0:T(8,128)S(1)} copy-done((f32[1,8,64,128]{3,2,1,0:T(8,128)S(1)}, f32[1,8,64,128]{3,2,1,0:T(8,128)}, u32[]{:S(2)}) %copy-start.1) | copy-done | bytes 262168
  14.7 0.5 %fusion.12 = f32[8,64,128]{2,0,1:T(8,128)S(1)} fusion(f32[2,1,64,128]{3,1,2,0:T(1,128)S(1)} %collective-permute-done.1, f32[1,8,64,128]{3,1,2,0:T(8,128)S(1)} %get-tuple-element.28, f32[1,8,64,128]{3,1,2,0:T(8,128)S(1)} %get-tuple-element.29, f32[2,1,64,128]{3,1,2,0:T(1,128)S(1)} %collective-permute-done, f32[8,64,1]{2,0,1:T(8,128)S(1)} %get-tuple-element.36, ...), kind=kLoop, calls=%fused_computation.20 | loop fusion | flops 1900544 | bytes 2998272 | tf_op jit(solution)/shard_map/sub | solution.py:89
  15.3 0.7 %copy-done.2 = s32[8,128]{1,0:T(8,128)S(1)} copy-done((s32[8,128]{1,0:T(8,128)S(1)}, s32[8,128]{1,0:T(8,128)}, u32[]{:S(2)}) %copy-start.2) | copy-done | bytes 4120
  15.9 0.4 convolution_bitcast_fusion
  16.4 1.1 %collective-permute-done.2 = f32[2,128]{1,0:T(2,128)S(1)} collective-permute-done((f32[2,128]{1,0:T(2,128)S(1)}, f32[2,128]{1,0:T(2,128)S(1)}, u32[]{:S(2)}, u32[]{:S(2)}) %collective-permute-start.2) | collective-permute-done | bytes 1056 | tf_op jit(solution)/shard_map/ppermute | solution.py:54
  17.5 5.4 %all-to-all-done = f32[1,1,16,33,128]{4,1,3,0,2:T(1,128)S(1)} async-done(((f32[1,1,16,33,128]{4,1,3,0,2:T(1,128)}), f32[1,1,16,33,128]{4,1,3,0,2:T(1,128)S(1)}, u32[]{:S(2)}, u32[]{:S(2)}) %all-to-all-start) | async-done | bytes 270368 | tf_op jit(solution)/shard_map/all_to_all | solution.py:71
  23.0 0.2 slice_reduce_fusion.2
  23.2 0.7 %slice_reduce_fusion = f32[16,32,128]{2,1,0:T(8,128)S(1)} fusion(f32[16,1,33,128]{3,1,2,0:T(1,128)S(1)} %bitcast.92), kind=kLoop, calls=%fused_computation.29 | loop fusion | bytes 524288 | tf_op jit(solution)/shard_map/slice | solution.py:73
  23.8 0.2 convolution_bitcast_fusion.1
  24.0 0.6 %dynamic_slice.4 = f32[1]{0:T(128)} dynamic-slice(f32[16]{0:T(128)S(1)} %convolution_bitcast_fusion.1, s32[]{:T(128)S(6)} %select_n.34), dynamic_slice_sizes={1} | dynamic-slice | bytes 12 | tf_op jit(solution)/shard_map/jit(dynamic_index_in_dim)/dynamic_slice | solution.py:104
  25.4 0.6 %fusion = f32[2,8,32,128]{3,1,2,0:T(8,128)S(1)} fusion(f32[2,8,32,128]{3,2,1,0:T(8,128)S(1)} %bitcast.96), kind=kOutput, calls=%fused_computation.1 | convolution fusion | flops 12654592 | bytes 524288 | tf_op jit(solution)/shard_map/ji,jp->ip/dot_general | solution.py:74
  26.0 0.3 maximum_bitcast_fusion
  26.3 12.9 %all_to_all.8 = f32[16,1,1,33,128]{4,2,3,1,0:T(1,128)S(1)} all-to-all(f32[16,1,1,33,128]{4,2,3,1,0:T(1,128)S(1)} %maximum_bitcast_fusion), channel_id=1, replica_groups=mesh['tm'=16,'space'=2] {'tm'}, dimensions={0} | all-to-all | bytes 540672 | tf_op jit(solution)/shard_map/all_to_all | solution.py:110
  39.2 0.5 %slice_reduce_fusion.1 = f32[8]{0:T(128)} fusion(f32[1,16,33,128]{3,1,2,0:T(8,128)S(1)} %bitcast.94), kind=kLoop, calls=%fused_computation.51 | loop fusion | flops 120 | bytes 544 | tf_op jit(solution)/shard_map/reduce_sum | solution.py:112
  39.9 0.5 %fusion.23 = f32[1,8,64,128]{3,1,2,0:T(8,128)S(1)} fusion(f32[8,64,128]{2,0,1:T(8,128)S(1)} %fusion.12, f32[8,64,128]{2,1,0:T(8,128)S(1)} %bitcast.95, f32[1,8,64,128]{3,2,1,0:T(8,128)S(1)} %copy-done.1, f32[1,8,64,128]{3,2,1,0:T(8,128)S(1)} %copy-done), kind=kLoop, calls=%fused_computation.41 | loop fusion | flops 262144 | bytes 1310720 | tf_op jit(solution)/shard_map/broadcast_in_dim | solution.py:116
  40.3 0.8 %copy.55 = f32[1,8,64,128]{3,2,1,0:T(8,128)} copy(f32[1,8,64,128]{3,1,2,0:T(8,128)S(1)} %fusion.23) | data formatting | bytes 524288
  (20 shorter events, 0.8 us)
Async XLA Ops:
  0.6 1.2 %copy-start = (f32[1,8,64,128]{3,2,1,0:T(8,128)S(1)}, f32[1,8,64,128]{3,2,1,0:T(8,128)}, u32[]{:S(2)}) copy-start(f32[1,8,64,128]{3,2,1,0:T(8,128)} %param.5) | copy-start | bytes 786436
  2.3 12.4 %collective-permute-start = (f32[2,1,64,128]{3,1,2,0:T(1,128)S(1)}, f32[2,1,64,128]{3,1,2,0:T(1,128)S(1)}, u32[]{:S(2)}, u32[]{:S(2)}) collective-permute-start(f32[2,1,64,128]{3,1,2,0:T(1,128)S(1)} %get-tuple-element.13), channel_id=1, source_target_pairs={{1,0},{0,1},{3,2},{2,3},{5,4},{4,5},{7,6},{6,7},{9,8},{8,9},{11,10... | collective-permute-start | bytes 196616 | tf_op jit(solution)/shard_map/ppermute | solution.py:35
  2.8 11.9 %collective-permute-start.1 = (f32[2,1,64,128]{3,1,2,0:T(1,128)S(1)}, f32[2,1,64,128]{3,1,2,0:T(1,128)S(1)}, u32[]{:S(2)}, u32[]{:S(2)}) collective-permute-start(f32[2,1,64,128]{3,1,2,0:T(1,128)S(1)} %get-tuple-element.14), channel_id=1, source_target_pairs={{0,1},{1,0},{2,3},{3,2},{4,5},{5,4},{6,7},{7,6},{8,9},{9,8},{10,11... | collective-permute-start | bytes 196616 | tf_op jit(solution)/shard_map/ppermute | solution.py:34
  4.4 18.6 %all-to-all-start = ((f32[1,1,16,33,128]{4,1,3,0,2:T(1,128)}), f32[1,1,16,33,128]{4,1,3,0,2:T(1,128)S(1)}, u32[]{:S(2)}, u32[]{:S(2)}) async-start(f32[1,1,16,33,128]{4,1,3,0,2:T(1,128)} %pad_bitcast_fusion), calls=%async_computation | async-start | bytes 540672 | tf_op jit(solution)/shard_map/all_to_all | solution.py:71
  13.6 1.0 %copy-start.1 = (f32[1,8,64,128]{3,2,1,0:T(8,128)S(1)}, f32[1,8,64,128]{3,2,1,0:T(8,128)}, u32[]{:S(2)}) copy-start(f32[1,8,64,128]{3,2,1,0:T(8,128)} %param.7) | copy-start | bytes 786436
  15.2 0.7 %copy-start.2 = (s32[8,128]{1,0:T(8,128)S(1)}, s32[8,128]{1,0:T(8,128)}, u32[]{:S(2)}) copy-start(s32[8,128]{1,0:T(8,128)} %param.9) | copy-start | bytes 12292
  16.3 1.2 %collective-permute-start.2 = (f32[2,128]{1,0:T(2,128)S(1)}, f32[2,128]{1,0:T(2,128)S(1)}, u32[]{:S(2)}, u32[]{:S(2)}) collective-permute-start(f32[2,128]{1,0:T(2,128)S(1)} %convolution_bitcast_fusion), channel_id=1, source_target_pairs={{0,1},{1,0},{2,3},{3,2},{4,5},{5,4},{6,7},{7,6},{8,9},{9,8},{10,11... | collective-permute-start | bytes 3080 | tf_op jit(solution)/shard_map/ppermute | solution.py:54

commit v4 on v3

--- a/solution.py
+++ b/solution.py
@@ -56,6 +56,16 @@
     return x
 
 
+def spectral_row(position, count):
+    steps = jnp.arange(count, dtype=jnp.int32)
+    offset = position - steps
+    theta = math.pi * offset.astype(jnp.float32) / count
+    parity = jnp.where(offset % 2 == 0, 1.0, -1.0).astype(jnp.float32)
+    skipped = (offset == 0) | (jnp.abs(offset) == count // 2)
+    safe_tan = jnp.where(skipped, jnp.float32(1.0), jnp.tan(theta))
+    return jnp.where(skipped, jnp.float32(0.0), 0.5 * parity / safe_tan).astype(jnp.float32)
+
+
 def on_device(adjoint, base_flow, source, pulse, actuator):
     count = lax.axis_size("tm")
     position = lax.axis_index("tm")
@@ -63,14 +73,15 @@
     total = count * nt_loc
     chunk = nx * cy // count
     share = NACT // count
+    pad = 8
     dmat = spectral_matrix(total)
 
-    blocks = adjoint.reshape(nt_loc, count, chunk, cz)
-    pulse_row = jnp.broadcast_to(pulse.reshape(nt_loc, 1, 1, 1), (nt_loc, count, 1, cz))
-    outgoing = jnp.concatenate([blocks, pulse_row], axis=2)
-    incoming = lax.all_to_all(outgoing, "tm", 1, 0, tiled=False)
-    pulses = incoming[:, :, chunk, 0].reshape(total)
-    gathered = incoming[:, :, :chunk].reshape(total, chunk * cz)
+    blocks = adjoint.reshape(count, chunk, cz)
+    pulse_rows = jnp.broadcast_to(pulse.reshape(1, 1, 1), (count, pad, cz))
+    outgoing = jnp.concatenate([blocks, pulse_rows], axis=1)
+    incoming = lax.all_to_all(outgoing, "tm", 0, 0, tiled=True)
+    pulses = incoming[:, chunk, 0]
+    gathered = incoming[:, :chunk].reshape(total, chunk * cz)
     derived = omega_rate * jnp.einsum(
         "ji,jp->ip", dmat, gathered, precision=lax.Precision.HIGHEST
     )
@@ -87,8 +98,9 @@
     beside = beside + wall_plus(field) + wall_minus(field)
     beside = beside + jnp.roll(field, -1, axis=2) + jnp.roll(field, 1, axis=2)
     operator = advect + viscosity * (beside - 6.0 * field) - reaction * field
+    forcing = operator + source[0]
 
-    kept = field + pseudo_step * (operator + source[0])
+    kept = field + pseudo_step * forcing
     walls = jnp.stack([pulse[0] * kept[:, 0, :], field[:, 0, :]]).reshape(2, -1)
     onehot = (actuator[:, :, None] == jnp.arange(NACT, dtype=jnp.int32)[None, None, :]).astype(
         jnp.float32
@@ -100,19 +112,17 @@
         preferred_element_type=jnp.float32,
     )
     terms = butterfly_sum(terms, "space")
-    weights = jnp.dot(dmat, pulses, precision=lax.Precision.HIGHEST)
-    own_weight = lax.dynamic_index_in_dim(weights, position, keepdims=False)
+    forcing, terms = lax.optimization_barrier((forcing, terms))
+    own_weight = jnp.sum(spectral_row(position, total) * pulses)
     partial_sum = (terms[0] - pseudo_step * omega_rate * own_weight * terms[1]) / total
-    grad_row = jnp.pad(partial_sum.reshape(count, 1, 1, share), ((0, 0), (0, 0), (0, 0), (0, cz - share)))
+    grad_rows = jnp.pad(partial_sum.reshape(count, 1, share), ((0, 0), (0, pad - 1), (0, cz - share)))
 
-    derived = derived.reshape(count, nt_loc, chunk, cz)
-    outgoing = jnp.concatenate([derived, grad_row], axis=2)
-    incoming = lax.all_to_all(outgoing, "tm", 0, 1, tiled=False)
-    time_term = incoming[:, :, :chunk].reshape(nt_loc, nx, cy, cz)[0]
-    gradient = jnp.sum(incoming[0, :, chunk, :share], axis=0)
+    outgoing = jnp.concatenate([derived.reshape(count, chunk, cz), grad_rows], axis=1)
+    incoming = lax.all_to_all(outgoing, "tm", 0, 0, tiled=True)
+    time_term = incoming[:, :chunk].reshape(nx, cy, cz)
+    gradient = jnp.sum(incoming[:, chunk, :share], axis=0)
 
-    residual = time_term - operator - source[0]
-    updated = field - pseudo_step * residual
+    updated = field - pseudo_step * (time_term - forcing)
     return (updated[None], gradient)
 
 

time: 41.4 us -> 42.5 us (1.027)
  local copies, waits for them, and re-layouts: 6.76 us -> 5.08 us
  waiting for transfers between devices: 6.58 us -> 7.94 us
  blocking collectives: 12.9 us -> 14.1 us
    all_to_all x1, waiting for transfers between devices: 5.45 us -> 6.82 us  [on_device(): incoming = lax.all_to_all(outgoing, 'tm', 0, 0, tiled=True)]
    all_to_all x1, blocking collectives: 12.9 us -> 14.1 us  [on_device(): incoming = lax.all_to_all(outgoing, 'tm', 0, 0, tiled=True)]
    broadcast_in_dim x1 -> x0, local copies, waits for them, and re-layouts: 0.89 us -> none  [on_device(): incoming = lax.all_to_all(outgoing, 'tm', 1, 0, tiled=False)]
    concatenate x0 -> x1, local copies, waits for them, and re-layouts: none -> 0.74 us  [on_device(): outgoing = jnp.concatenate([blocks, pulse_rows], axis=1)]
    slice x4 -> x3, local copies, waits for them, and re-layouts: 0.96 us -> 0.25 us  [the longest x1 0.2 us: on_device(): pulses = incoming[:, chunk, 0]]
    reduce_sum x1 -> x2, other arithmetic: 0.53 us -> 1.2 us  [the longest x1 0.66 us: on_device(): own_weight = jnp.sum(spectral_row(position, total) * pulses)]
    add x0 -> x1, other arithmetic: none -> 0.64 us  [on_device(): forcing = operator + source[0]]
    dynamic_slice x1 -> x0, local copies, waits for them, and re-layouts: 0.6 us -> none  [on_device(): own_weight = lax.dynamic_index_in_dim(weights, position, keepdims=False)]
  transfers between devices with their start and end apart: 4 -> 4, of which waited for: 2 -> 2; matrix products, arithmetic and copies ran while one was open for 7% -> 6% of each run, Pallas kernels for 0% -> 0%
where the time goes in v4:
time: 42.5 us; the launch traced here: 42.2 us
  blocking collectives  14.1 us (33%)
  starting transfers between devices  8.96 us (21%)
  waiting for transfers between devices  7.94 us (19%)
  local copies, waits for them, and re-layouts  5.08 us (12%)
  other arithmetic  3.06 us (7%)
  between operations  2.09 us (5%)
  matrix products  0.92 us (2%)
    all_to_all x1, blocking collectives, on_device(): incoming = lax.all_to_all(outgoing, 'tm', 0, 0, tiled=True)  14.1 us
    all_to_all x1, starting transfers between devices, on_device(): incoming = lax.all_to_all(outgoing, 'tm', 0, 0, tiled=True)  8.29 us
    all_to_all x1, waiting for transfers between devices, on_device(): incoming = lax.all_to_all(outgoing, 'tm', 0, 0, tiled=True)  6.82 us
    unnamed x8, local copies, waits for them, and re-layouts  2.34 us
    slice x1, local copies, waits for them, and re-layouts, on_device(): flux_y = base_flow[1, 0] * field  1.2 us
    ppermute x1, waiting for transfers between devices, butterfly_sum(): x = x + lax.ppermute(x, axis, [(i, i ^ bit) for i in range(groups)])  1.12 us
  transfers between devices with their start and end apart: 4, of which 2 were waited for; matrix products, arithmetic and copies ran while one was open for 6% of the time, Pallas kernels for 0%

profile of v4, /device:TPU:0, one launch (start us, length us, event | category | flops | bytes accessed | tf_op | source)
XLA Modules:
  0.0 42.2 jit_solution(12316335506607184110)
XLA Ops:
  0.6 1.2 %fusion.73 = (f32[1,1,8,64,128]{4,3,2,1,0:T(8,128)S(1)}, f32[1,1,8,64,128]{4,3,2,1,0:T(8,128)S(1)}, f32[1,1,8,64,128]{4,3,2,1,0:T(8,128)S(1)}) fusion(f32[3,1,8,64,128]{4,3,2,1,0:T(8,128)} %param.6), kind=kLoop, calls=%fused_computation.101 | loop fusion | bytes 1572864 | tf_op jit(solution)/shard_map/slice | solution.py:91
  1.9 0.3 copy_bitcast_fusion.3
  2.2 0.1 pad_maximum_fusion.5
  2.3 0.5 %collective-permute-start = (f32[2,1,64,128]{3,1,2,0:T(1,128)S(1)}, f32[2,1,64,128]{3,1,2,0:T(1,128)S(1)}, u32[]{:S(2)}, u32[]{:S(2)}) collective-permute-start(f32[2,1,64,128]{3,1,2,0:T(1,128)S(1)} %get-tuple-element.17), channel_id=1, source_target_pairs={{1,0},{0,1},{3,2},{2,3},{5,4},{4,5},{7,6},{6,7},{9,8},{8,9},{11,10... | collective-permute-start | bytes 196616 | tf_op jit(solution)/shard_map/ppermute | solution.py:35
  2.8 0.1 collective-permute-start.1
  3.5 0.7 %concatenate.41 = f32[16,40,128]{2,1,0:T(8,128)} pad(f32[16,32,128]{2,1,0:T(8,128)S(1)} %bitcast.71, f32[]{:T(128)} %bitcast.69), padding=0_0x0_8x0_0 | pad | bytes 589828 | tf_op jit(solution)/shard_map/concatenate | solution.py:81
  4.2 8.3 %all-to-all-start = ((f32[16,40,128]{2,1,0:T(8,128)}), f32[16,40,128]{2,1,0:T(8,128)S(1)}, u32[]{:S(2)}, u32[]{:S(2)}) async-start(f32[16,40,128]{2,1,0:T(8,128)} %concatenate.41), calls=%async_computation | async-start | bytes 655360 | tf_op jit(solution)/shard_map/all_to_all | solution.py:82
  12.5 0.4 %fusion.19 = (f32[8,64,128]{2,0,1:T(8,128)S(1)}, f32[8,64,128]{2,0,1:T(8,128)S(1)}) fusion(f32[1,1,8,64,128]{4,3,2,1,0:T(8,128)S(1)} %get-tuple-element.14, f32[1,8,64,128]{3,2,1,0:T(8,128)S(1)} %copy-done, f32[1,1,8,64,128]{4,3,2,1,0:T(8,128)S(1)} %get-tuple-element.16), kind=kLoop, calls=%fused_computation.32 | loop fusion | flops 131072 | bytes 1310720 | tf_op jit(solution)/shard_map/mul | solution.py:91
  13.0 0.2 fusion.77
  13.2 0.2 fusion.76
  13.5 0.8 %copy-done.1 = f32[1,8,64,128]{3,2,1,0:T(8,128)S(1)} copy-done((f32[1,8,64,128]{3,2,1,0:T(8,128)S(1)}, f32[1,8,64,128]{3,2,1,0:T(8,128)}, u32[]{:S(2)}) %copy-start.1) | copy-done | bytes 262168
  14.4 0.6 %fusion.13 = f32[8,64,128]{2,0,1:T(8,128)S(1)} fusion(f32[2,1,64,128]{3,1,2,0:T(1,128)S(1)} %collective-permute-done.1, f32[1,8,64,128]{3,1,2,0:T(8,128)S(1)} %get-tuple-element.32, f32[1,8,64,128]{3,1,2,0:T(8,128)S(1)} %get-tuple-element.33, f32[2,1,64,128]{3,1,2,0:T(1,128)S(1)} %collective-permute-done, f32[8,64,1]{2,0,1:T(8,128)S(1)} %get-tuple-element.40, ...), kind=kLoop, calls=%fused_computation.19 | loop fusion | flops 1966080 | bytes 3260416 | tf_op jit(solution)/shard_map/add | solution.py:101
  15.0 0.7 %copy-done.2 = s32[8,128]{1,0:T(8,128)S(1)} copy-done((s32[8,128]{1,0:T(8,128)S(1)}, s32[8,128]{1,0:T(8,128)}, u32[]{:S(2)}) %copy-start.2) | copy-done | bytes 4120
  15.7 0.4 convolution_bitcast_fusion
  16.2 1.1 %collective-permute-done.2 = f32[2,128]{1,0:T(2,128)S(1)} collective-permute-done((f32[2,128]{1,0:T(2,128)S(1)}, f32[2,128]{1,0:T(2,128)S(1)}, u32[]{:S(2)}, u32[]{:S(2)}) %collective-permute-start.2) | collective-permute-done | bytes 1056 | tf_op jit(solution)/shard_map/ppermute | solution.py:54
  17.3 6.8 %all-to-all-done = f32[16,40,128]{2,1,0:T(8,128)S(1)} async-done(((f32[16,40,128]{2,1,0:T(8,128)}), f32[16,40,128]{2,1,0:T(8,128)S(1)}, u32[]{:S(2)}, u32[]{:S(2)}) %all-to-all-start) | async-done | bytes 327712 | tf_op jit(solution)/shard_map/all_to_all | solution.py:82
  24.1 0.2 slice_reduce_fusion.1
  24.3 0.7 %multiply_reduce_fusion.1 = f32[]{:T(128)} fusion(f32[16]{0:T(128)S(1)} %slice_reduce_fusion.1, s32[]{:T(128)S(6)} %axis_index.15), kind=kLoop, calls=%fused_computation.89 | loop fusion | flops 415 | bytes 72 | tf_op jit(solution)/shard_map/reduce_sum | solution.py:116
  25.6 0.1 div.33
  25.8 0.5 %fusion = f32[2,8,32,128]{3,1,2,0:T(8,128)S(1)} fusion(f32[2,8,32,128]{3,2,1,0:T(8,128)S(1)} %bitcast.73), kind=kOutput, calls=%fused_computation.1 | convolution fusion | flops 12654592 | bytes 524288 | tf_op jit(solution)/shard_map/ji,jp->ip/dot_general | solution.py:85
  26.4 14.1 %all_to_all.10 = f32[16,40,128]{2,1,0:T(8,128)S(1)} all-to-all(f32[16,40,128]{2,1,0:T(8,128)S(1)} %select_maximum_fusion), channel_id=1, replica_groups=mesh['tm'=16,'space'=2] {'tm'}, dimensions={0} | all-to-all | bytes 655360 | tf_op jit(solution)/shard_map/all_to_all | solution.py:121
  40.6 0.3 fusion.23
  40.9 0.8 %copy.51 = f32[1,8,64,128]{3,2,1,0:T(8,128)} copy(f32[1,8,64,128]{3,1,2,0:T(8,128)S(1)} %fusion.23) | data formatting | bytes 524288
  41.6 0.5 %slice_reduce_fusion = f32[8]{0:T(128)} fusion(f32[16,40,128]{2,1,0:T(8,128)S(1)} %all_to_all.10), kind=kLoop, calls=%fused_computation.47 | loop fusion | flops 120 | bytes 544 | tf_op jit(solution)/shard_map/reduce_sum | solution.py:123
  (15 shorter events, 0.3 us)
Async XLA Ops:
  0.6 1.2 %copy-start = (f32[1,8,64,128]{3,2,1,0:T(8,128)S(1)}, f32[1,8,64,128]{3,2,1,0:T(8,128)}, u32[]{:S(2)}) copy-start(f32[1,8,64,128]{3,2,1,0:T(8,128)} %param.5) | copy-start | bytes 786436
  2.3 11.2 %collective-permute-start = (f32[2,1,64,128]{3,1,2,0:T(1,128)S(1)}, f32[2,1,64,128]{3,1,2,0:T(1,128)S(1)}, u32[]{:S(2)}, u32[]{:S(2)}) collective-permute-start(f32[2,1,64,128]{3,1,2,0:T(1,128)S(1)} %get-tuple-element.17), channel_id=1, source_target_pairs={{1,0},{0,1},{3,2},{2,3},{5,4},{4,5},{7,6},{6,7},{9,8},{8,9},{11,10... | collective-permute-start | bytes 196616 | tf_op jit(solution)/shard_map/ppermute | solution.py:35
  2.8 10.7 %collective-permute-start.1 = (f32[2,1,64,128]{3,1,2,0:T(1,128)S(1)}, f32[2,1,64,128]{3,1,2,0:T(1,128)S(1)}, u32[]{:S(2)}, u32[]{:S(2)}) collective-permute-start(f32[2,1,64,128]{3,1,2,0:T(1,128)S(1)} %get-tuple-element.18), channel_id=1, source_target_pairs={{0,1},{1,0},{2,3},{3,2},{4,5},{5,4},{6,7},{7,6},{8,9},{9,8},{10,11... | collective-permute-start | bytes 196616 | tf_op jit(solution)/shard_map/ppermute | solution.py:34
  4.2 19.9 %all-to-all-start = ((f32[16,40,128]{2,1,0:T(8,128)}), f32[16,40,128]{2,1,0:T(8,128)S(1)}, u32[]{:S(2)}, u32[]{:S(2)}) async-start(f32[16,40,128]{2,1,0:T(8,128)} %concatenate.41), calls=%async_computation | async-start | bytes 655360 | tf_op jit(solution)/shard_map/all_to_all | solution.py:82
  13.4 1.0 %copy-start.1 = (f32[1,8,64,128]{3,2,1,0:T(8,128)S(1)}, f32[1,8,64,128]{3,2,1,0:T(8,128)}, u32[]{:S(2)}) copy-start(f32[1,8,64,128]{3,2,1,0:T(8,128)} %param.7) | copy-start | bytes 786436
  15.0 0.7 %copy-start.2 = (s32[8,128]{1,0:T(8,128)S(1)}, s32[8,128]{1,0:T(8,128)}, u32[]{:S(2)}) copy-start(s32[8,128]{1,0:T(8,128)} %param.9) | copy-start | bytes 12292
  16.1 1.2 %collective-permute-start.2 = (f32[2,128]{1,0:T(2,128)S(1)}, f32[2,128]{1,0:T(2,128)S(1)}, u32[]{:S(2)}, u32[]{:S(2)}) collective-permute-start(f32[2,128]{1,0:T(2,128)S(1)} %convolution_bitcast_fusion), channel_id=1, source_target_pairs={{0,1},{1,0},{2,3},{3,2},{4,5},{5,4},{6,7},{7,6},{8,9},{9,8},{10,11... | collective-permute-start | bytes 3080 | tf_op jit(solution)/shard_map/ppermute | solution.py:54

commit v5 on v4

v5 whole, which is shorter than its diff:
```python
import math

import jax
import jax.numpy as jnp
from jax import lax
from jax.sharding import PartitionSpec as P

NACT = 128


omega_rate = 0.25
pseudo_step = 0.2
viscosity = 0.2
reaction = 0.5


def spectral_matrix(count):
    steps = jnp.arange(count, dtype=jnp.int32)
    offset = steps[:, None] - steps[None, :]
    theta = math.pi * offset.astype(jnp.float32) / count
    parity = jnp.where(offset % 2 == 0, 1.0, -1.0).astype(jnp.float32)
    skipped = (offset == 0) | (jnp.abs(offset) == count // 2)
    safe_tan = jnp.where(skipped, jnp.float32(1.0), jnp.tan(theta))
    return jnp.where(skipped, jnp.float32(0.0), 0.5 * parity / safe_tan).astype(jnp.float32)


def wall_plus(field):
    zeros = jnp.zeros_like(field[:, :1])
    return jnp.concatenate([field[:, 1:], zeros], axis=1)


def wall_minus(field):
    zeros = jnp.zeros_like(field[:, :1])
    return jnp.concatenate([zeros, field[:, :-1]], axis=1)


def butterfly_sum(x, axis):
    groups = lax.axis_size(axis)
    bit = 1
    while bit < groups:
        x = x + lax.ppermute(x, axis, [(i, i ^ bit) for i in range(groups)])
        bit *= 2
    return x


def halo(ends, axis):
    count = lax.axis_size(axis)
    up = [(i, (i + 1) % count) for i in range(count)]
    down = [(j, i) for i, j in up]
    before = lax.ppermute(ends[1], axis, up)
    after = lax.ppermute(ends[0], axis, down)
    return before, after


def on_device(adjoint, base_flow, source, pulse, actuator):
    count = lax.axis_size("tm")
    nt_loc, nx, cy, cz = adjoint.shape
    total = count * nt_loc
    chunk = nx * cy // count
    share = NACT // count
    pad = 8
    dmat = spectral_matrix(total)

    incoming = lax.all_to_all(adjoint.reshape(count, chunk, cz), "tm", 0, 0, tiled=True)
    derived = omega_rate * jnp.einsum(
        "ji,jp->ip", dmat, incoming.reshape(total, chunk * cz), precision=lax.Precision.HIGHEST
    )

    field = adjoint[0]
    velocity = base_flow[:, 0]
    ends = [jnp.stack([field[k], velocity[0, k] * field[k]]) for k in (0, nx - 1)]
    before, after = halo(ends, "space")
    flux_x = velocity[0] * field
    flux_y = velocity[1] * field
    flux_z = velocity[2] * field
    ahead_x = jnp.concatenate([flux_x[1:], after[1][None]], axis=0)
    behind_x = jnp.concatenate([before[1][None], flux_x[:-1]], axis=0)
    ahead = jnp.concatenate([field[1:], after[0][None]], axis=0)
    behind = jnp.concatenate([before[0][None], field[:-1]], axis=0)
    advect = 0.5 * (ahead_x - behind_x)
    advect = advect + 0.5 * (wall_plus(flux_y) - wall_minus(flux_y))
    advect = advect + 0.5 * (jnp.roll(flux_z, -1, axis=2) - jnp.roll(flux_z, 1, axis=2))
    beside = ahead + behind
    beside = beside + wall_plus(field) + wall_minus(field)
    beside = beside + jnp.roll(field, -1, axis=2) + jnp.roll(field, 1, axis=2)
    operator = advect + viscosity * (beside - 6.0 * field) - reaction * field
    forcing = operator + source[0]

    kept = field + pseudo_step * forcing
    walls = jnp.stack([pulse[0] * kept[:, 0, :], field[:, 0, :]]).reshape(2, -1)
    onehot = (actuator[:, :, None] == jnp.arange(NACT, dtype=jnp.int32)[None, None, :]).astype(
        jnp.float32
    )
    terms = jnp.dot(
        walls,
        onehot.reshape(-1, NACT),
        precision=lax.Precision.HIGHEST,
        preferred_element_type=jnp.float32,
    )
    terms = butterfly_sum(terms, "space")
    slices = jnp.transpose(terms.reshape(2, count, share), (1, 0, 2))
    slices = jnp.pad(slices, ((0, 0), (0, 0), (0, cz - share)))
    pulse_row = jnp.broadcast_to(pulse.reshape(1, 1, 1), (count, 1, cz))
    grad_rows = jnp.concatenate([slices, pulse_row, jnp.zeros((count, pad - 3, cz), jnp.float32)], axis=1)
    forcing, grad_rows = lax.optimization_barrier((forcing, grad_rows))

    outgoing = jnp.concatenate([derived.reshape(count, chunk, cz), grad_rows], axis=1)
    incoming = lax.all_to_all(outgoing, "tm", 0, 0, tiled=True)
    time_term = incoming[:, :chunk].reshape(nx, cy, cz)
    weights = jnp.dot(dmat, incoming[:, chunk + 2, 0], precision=lax.Precision.HIGHEST)
    parts = incoming[:, chunk, :share] - pseudo_step * omega_rate * weights[:, None] * incoming[:, chunk + 1, :share]
    gradient = jnp.sum(parts, axis=0) / total

    updated = field - pseudo_step * (time_term - forcing)
    return (updated[None], gradient)


def solution(mesh):
    in_specs = (
        P("tm", "space", None, None),
        P(None, "tm", "space", None, None),
        P("tm", "space", None, None),
        P("tm"),
        P("space", None),
    )
    out_specs = (P("tm", "space", None, None), P("tm"))
    return jax.shard_map(
        on_device, mesh=mesh, in_specs=in_specs, out_specs=out_specs, check_vma=False
    )
```

time: 42.5 us -> 43.5 us (1.024)
  waiting for transfers between devices: 7.94 us -> 2.52 us
  other arithmetic: 3.06 us -> 6.23 us
  blocking collectives: 14.1 us -> 16.8 us
  local copies, waits for them, and re-layouts: 5.08 us -> 5.68 us
  between operations: 2.09 us -> 1.51 us
    all_to_all x1, waiting for transfers between devices: 6.82 us -> 1.54 us  [on_device(): lax.all_to_all(adjoint.reshape(count, chunk, cz), 'tm', 0, 0, tiled=True)]
    all_to_all x1, blocking collectives: 14.1 us -> 16.8 us  [on_device(): incoming = lax.all_to_all(outgoing, 'tm', 0, 0, tiled=True)]
    mul x1 -> x3, other arithmetic: 0.44 us -> 2.36 us  [the longest x1 1.55 us: on_device(): flux_y = velocity[1] * field]
    add x1, other arithmetic: 0.64 us -> 1.76 us  [on_device(): forcing = operator + source[0]]
    reduce_sum x2 -> x1, other arithmetic: 1.2 us -> 0.12 us  [on_device(): gradient = jnp.sum(parts, axis=0) / total]
    broadcast_in_dim x1, other arithmetic: 0.32 us -> 1.28 us  [on_device(): return (updated[None], gradient)]
    slice x3 -> x11, local copies, waits for them, and re-layouts: 1.43 us -> 2.15 us  [the longest x1 0.86 us: on_device(): field[k]]
    concatenate x1 -> x2, local copies, waits for them, and re-layouts: 0.74 us -> 0.15 us  [on_device(): jnp.concatenate([slices, pulse_row, jnp.zeros((count, pad - 3, cz), jnp.f...]
  transfers between devices with their start and end apart: 4 -> 4, of which waited for: 2 -> 2; matrix products, arithmetic and copies ran while one was open for 6% -> 15% of each run, Pallas kernels for 0% -> 0%
where the time goes in v5:
time: 43.5 us; the launch traced here: 42.9 us
  blocking collectives  16.8 us (39%)
  starting transfers between devices  9.02 us (21%)
  other arithmetic  6.23 us (14%)
  local copies, waits for them, and re-layouts  5.68 us (13%)
  waiting for transfers between devices  2.52 us (6%)
  between operations  1.51 us (3%)
  matrix products  1.12 us (3%)
    all_to_all x1, blocking collectives, on_device(): incoming = lax.all_to_all(outgoing, 'tm', 0, 0, tiled=True)  16.8 us
    all_to_all x1, starting transfers between devices, on_device(): lax.all_to_all(adjoint.reshape(count, chunk, cz), 'tm', 0, 0, tiled=True)  8.31 us
    unnamed x10, local copies, waits for them, and re-layouts  2.79 us
    add x1, other arithmetic, on_device(): forcing = operator + source[0]  1.76 us
    mul x1, other arithmetic, on_device(): flux_y = velocity[1] * field  1.55 us
    all_to_all x1, waiting for transfers between devices, on_device(): lax.all_to_all(adjoint.reshape(count, chunk, cz), 'tm', 0, 0, tiled=True)  1.54 us
    broadcast_in_dim x1, other arithmetic, on_device(): return (updated[None], gradient)  1.28 us
    ppermute x1, waiting for transfers between devices, butterfly_sum(): x = x + lax.ppermute(x, axis, [(i, i ^ bit) for i in range(groups)])  0.97 us
  transfers between devices with their start and end apart: 4, of which 2 were waited for; matrix products, arithmetic and copies ran while one was open for 15% of the time, Pallas kernels for 0%

profile of v5, /device:TPU:0, one launch (start us, length us, event | category | flops | bytes accessed | tf_op | source)
XLA Modules:
  0.0 42.9 jit_solution(15004866498846017244)
XLA Ops:
  0.6 0.9 %fusion.67 = (f32[1,1,64,128]{3,2,1,0:T(8,128)S(1)}, f32[1,64,128]{2,1,0:T(8,128)S(1)}) fusion(f32[1,8,64,128]{3,2,1,0:T(8,128)} %param.5), kind=kLoop, calls=%fused_computation.98 | loop fusion | bytes 131072 | tf_op jit(solution)/shard_map/slice | solution.py:71
  1.5 0.8 %slice.160 = f32[1,1,64,128]{3,2,1,0:T(8,128)S(1)} slice(f32[3,8,64,128]{3,2,1,0:T(8,128)} %bitcast.81), slice={[0:1], [7:8], [0:64], [0:128]} | slice | bytes 65536 | tf_op jit(solution)/shard_map/slice | solution.py:71
  2.4 0.5 %collective-permute-start.1 = (f32[2,64,128]{2,0,1:T(2,128)S(1)}, f32[2,64,128]{2,0,1:T(2,128)S(1)}, u32[]{:S(2)}, u32[]{:S(2)}) collective-permute-start(f32[2,64,128]{2,0,1:T(2,128)S(1)} %pad_maximum_fusion.2), channel_id=1, source_target_pairs={{0,1},{1,0},{2,3},{3,2},{4,5},{5,4},{6,7},{7,6},{8,9},{9,8},{10,11... | collective-permute-start | bytes 196616 | tf_op jit(solution)/shard_map/ppermute | solution.py:50
  2.9 0.8 %fusion.24 = f32[1,64,128]{2,1,0:T(8,128)S(1)} fusion(f32[3,8,64,128]{3,2,1,0:T(8,128)} %bitcast.82, f32[1,8,64,128]{3,2,1,0:T(8,128)} %param.5), kind=kLoop, calls=%fused_computation.43 | loop fusion | flops 8192 | bytes 98304 | tf_op jit(solution)/shard_map/mul | solution.py:71
  3.7 0.1 collective-permute-start
  3.8 8.3 %all-to-all-start = ((f32[16,32,128]{2,1,0:T(8,128)}), f32[16,32,128]{2,1,0:T(8,128)S(1)}, u32[]{:S(2)}, u32[]{:S(2)}) async-start(f32[16,32,128]{2,1,0:T(8,128)} %bitcast.1), calls=%async_computation | async-start | bytes 524288 | tf_op jit(solution)/shard_map/all_to_all | solution.py:64
  12.2 1.1 %copy.84 = f32[1,8,64,128]{3,1,2,0:T(8,128)S(1)} copy(f32[1,8,64,128]{3,2,1,0:T(8,128)} %param.5) | data formatting | bytes 524288 | tf_op args[0]
  13.3 1.5 %fusion.17 = (f32[8,64,128]{2,0,1:T(8,128)S(1)}, f32[8,64,128]{2,0,1:T(8,128)S(1)}, f32[8,64,128]{2,0,1:T(8,128)S(1)}) fusion(f32[1,1,8,64,128]{4,3,2,1,0:T(8,128)S(1)} %get-tuple-element.12, f32[1,8,64,128]{3,2,1,0:T(8,128)} %param.5, f32[1,1,8,64,128]{4,3,2,1,0:T(8,128)S(1)} %get-tuple-element.14, f32[1,1,8,64,128]{4,3,2,1,0:T(8,128)S(1)} %get-tuple-element.13), kind=kLoop, calls=%fused_computation.29 | loop fusion | flops 196608 | bytes 1835008 | tf_op jit(solution)/shard_map/mul | solution.py:74
  14.9 0.2 fusion.63
  15.1 0.2 fusion.64
  16.2 0.2 copy-done.1
  16.4 1.8 %fusion.9 = f32[8,64,128]{2,0,1:T(8,128)S(1)} fusion(f32[1,64,128]{2,0,1:T(1,128)S(1)} %bitcast.86, f32[7,64,128]{2,0,1:T(8,128)S(1)} %get-tuple-element.41, f32[7,64,128]{2,0,1:T(8,128)S(1)} %get-tuple-element.40, f32[1,64,128]{2,0,1:T(1,128)S(1)} %get-tuple-element.43, f32[8,64,1]{2,0,1:T(8,128)S(1)} %get-tuple-element.48, ...), kind=kLoop, calls=%fused_computation.17 | loop fusion | flops 1703936 | bytes 3915776 | tf_op jit(solution)/shard_map/add | solution.py:87
  18.2 0.7 %copy-done.2 = s32[8,128]{1,0:T(8,128)S(1)} copy-done((s32[8,128]{1,0:T(8,128)S(1)}, s32[8,128]{1,0:T(8,128)}, u32[]{:S(2)}) %copy-start.2) | copy-done | bytes 4120
  18.9 0.4 convolution_bitcast_fusion
  19.5 1.0 %collective-permute-done.2 = f32[2,128]{1,0:T(2,128)S(1)} collective-permute-done((f32[2,128]{1,0:T(2,128)S(1)}, f32[2,128]{1,0:T(2,128)S(1)}, u32[]{:S(2)}, u32[]{:S(2)}) %collective-permute-start.2) | collective-permute-done | bytes 1056 | tf_op jit(solution)/shard_map/ppermute | solution.py:41
  20.6 1.5 %all-to-all-done = f32[16,32,128]{2,1,0:T(8,128)S(1)} async-done(((f32[16,32,128]{2,1,0:T(8,128)}), f32[16,32,128]{2,1,0:T(8,128)S(1)}, u32[]{:S(2)}, u32[]{:S(2)}) %all-to-all-start) | async-done | bytes 262176 | tf_op jit(solution)/shard_map/all_to_all | solution.py:64
  22.2 0.5 %fusion = f32[2,8,32,128]{3,1,2,0:T(8,128)S(1)} fusion(f32[2,8,32,128]{3,2,1,0:T(8,128)S(1)} %bitcast.78), kind=kOutput, calls=%fused_computation.1 | convolution fusion | flops 12654592 | bytes 524288 | tf_op jit(solution)/shard_map/ji,jp->ip/dot_general | solution.py:65
  22.8 16.8 %all_to_all.10 = f32[16,40,128]{2,1,0:T(8,128)S(1)} all-to-all(f32[16,40,128]{2,1,0:T(8,128)S(1)} %pad_maximum_fusion), channel_id=1, replica_groups=mesh['tm'=16,'space'=2] {'tm'}, dimensions={0} | all-to-all | bytes 655360 | tf_op jit(solution)/shard_map/all_to_all | solution.py:108
  39.8 0.2 slice_reduce_fusion
  40.0 0.2 fusion.1
  40.2 0.1 fusion.38
  40.3 0.5 %broadcast_multiply_fusion = f32[8]{0:T(128)} fusion(f32[8]{0:T(128)S(1)} %fusion.38), kind=kLoop, calls=%fused_computation.69 | loop fusion | flops 8 | bytes 64 | tf_op jit(solution)/shard_map/div | solution.py:112
  40.9 1.3 %fusion.21 = f32[1,8,64,128]{3,1,2,0:T(8,128)S(1)} fusion(f32[8,64,128]{2,0,1:T(8,128)S(1)} %fusion.9, f32[8,64,128]{2,1,0:T(8,128)S(1)} %bitcast.80, f32[1,8,64,128]{3,2,1,0:T(8,128)} %param.5), kind=kLoop, calls=%fused_computation.35 | loop fusion | flops 196608 | bytes 1048576 | tf_op jit(solution)/shard_map/broadcast_in_dim | solution.py:115
  42.2 0.8 %copy.49 = f32[1,8,64,128]{3,2,1,0:T(8,128)} copy(f32[1,8,64,128]{3,1,2,0:T(8,128)S(1)} %fusion.21) | data formatting | bytes 524288
  (30 shorter events, 1.0 us)
Async XLA Ops:
  0.6 11.5 %copy-start = (f32[3,1,8,64,128]{4,3,2,1,0:T(8,128)S(1)}, f32[3,1,8,64,128]{4,3,2,1,0:T(8,128)}, u32[]{:S(2)}) copy-start(f32[3,1,8,64,128]{4,3,2,1,0:T(8,128)} %param.6) | copy-start | bytes 2359300
  2.4 13.8 %collective-permute-start.1 = (f32[2,64,128]{2,0,1:T(2,128)S(1)}, f32[2,64,128]{2,0,1:T(2,128)S(1)}, u32[]{:S(2)}, u32[]{:S(2)}) collective-permute-start(f32[2,64,128]{2,0,1:T(2,128)S(1)} %pad_maximum_fusion.2), channel_id=1, source_target_pairs={{0,1},{1,0},{2,3},{3,2},{4,5},{5,4},{6,7},{7,6},{8,9},{9,8},{10,11... | collective-permute-start | bytes 196616 | tf_op jit(solution)/shard_map/ppermute | solution.py:50
  3.7 12.5 %collective-permute-start = (f32[2,64,128]{2,1,0:T(8,128)S(1)}, f32[2,64,128]{2,1,0:T(8,128)S(1)}, u32[]{:S(2)}, u32[]{:S(2)}) collective-permute-start(f32[2,64,128]{2,1,0:T(8,128)S(1)} %pad_maximum_fusion.1), channel_id=1, source_target_pairs={{1,0},{0,1},{3,2},{2,3},{5,4},{4,5},{7,6},{6,7},{9,8},{8,9},{11,10... | collective-permute-start | bytes 196616 | tf_op jit(solution)/shard_map/ppermute | solution.py:51
  3.8 18.4 %all-to-all-start = ((f32[16,32,128]{2,1,0:T(8,128)}), f32[16,32,128]{2,1,0:T(8,128)S(1)}, u32[]{:S(2)}, u32[]{:S(2)}) async-start(f32[16,32,128]{2,1,0:T(8,128)} %bitcast.1), calls=%async_computation | async-start | bytes 524288 | tf_op jit(solution)/shard_map/all_to_all | solution.py:64
  15.4 1.0 %copy-start.1 = (f32[1,8,64,128]{3,2,1,0:T(8,128)S(1)}, f32[1,8,64,128]{3,2,1,0:T(8,128)}, u32[]{:S(2)}) copy-start(f32[1,8,64,128]{3,2,1,0:T(8,128)} %param.7) | copy-start | bytes 786436
  18.2 0.7 %copy-start.2 = (s32[8,128]{1,0:T(8,128)S(1)}, s32[8,128]{1,0:T(8,128)}, u32[]{:S(2)}) copy-start(s32[8,128]{1,0:T(8,128)} %param.9) | copy-start | bytes 12292
  19.2 1.2 %collective-permute-start.2 = (f32[2,128]{1,0:T(2,128)S(1)}, f32[2,128]{1,0:T(2,128)S(1)}, u32[]{:S(2)}, u32[]{:S(2)}) collective-permute-start(f32[2,128]{1,0:T(2,128)S(1)} %convolution_bitcast_fusion), channel_id=1, source_target_pairs={{0,1},{1,0},{2,3},{3,2},{4,5},{5,4},{6,7},{7,6},{8,9},{9,8},{10,11... | collective-permute-start | bytes 3080 | tf_op jit(solution)/shard_map/ppermute | solution.py:41

commit v6 on v5

--- a/solution.py
+++ b/solution.py
@@ -3,6 +3,8 @@
 import jax
 import jax.numpy as jnp
 from jax import lax
+from jax.experimental import pallas as pl
+from jax.experimental.pallas import tpu as pltpu
 from jax.sharding import PartitionSpec as P
 
 NACT = 128
@@ -52,6 +54,90 @@
     return before, after
 
 
+def stencil_kernel(pulse_ref, field_ref, vel_ref, src_ref, before_ref, after_ref, forcing_ref, walls_ref):
+    nx, cy, cz = field_ref.shape
+    row = lax.broadcasted_iota(jnp.int32, (cy, cz), 0)
+
+    def wall_up(a):
+        return jnp.where(row == cy - 1, 0.0, pltpu.roll(a, cy - 1, 0))
+
+    def wall_down(a):
+        return jnp.where(row == 0, 0.0, pltpu.roll(a, 1, 0))
+
+    def span_up(a):
+        return pltpu.roll(a, cz - 1, 1)
+
+    def span_down(a):
+        return pltpu.roll(a, 1, 1)
+
+    for x in range(nx):
+        f = field_ref[x]
+        if x + 1 < nx:
+            ahead, ahead_x = field_ref[x + 1], vel_ref[0, x + 1] * field_ref[x + 1]
+        else:
+            ahead, ahead_x = after_ref[0], after_ref[1]
+        if x > 0:
+            behind, behind_x = field_ref[x - 1], vel_ref[0, x - 1] * field_ref[x - 1]
+        else:
+            behind, behind_x = before_ref[0], before_ref[1]
+        flux_y = vel_ref[1, x] * f
+        flux_z = vel_ref[2, x] * f
+        advect = 0.5 * (ahead_x - behind_x)
+        advect = advect + 0.5 * (wall_up(flux_y) - wall_down(flux_y))
+        advect = advect + 0.5 * (span_up(flux_z) - span_down(flux_z))
+        beside = ahead + behind
+        beside = beside + wall_up(f) + wall_down(f)
+        beside = beside + span_up(f) + span_down(f)
+        operator = advect + viscosity * (beside - 6.0 * f) - reaction * f
+        forcing = operator + src_ref[x]
+        forcing_ref[x] = forcing
+        walls_ref[0, x : x + 1, :] = pulse_ref[0] * (f[0:1] + pseudo_step * forcing[0:1])
+        walls_ref[1, x : x + 1, :] = f[0:1]
+
+
+def stencil(pulse, field, velocity, source, before, after):
+    nx, cy, cz = field.shape
+    vmem = pl.BlockSpec(memory_space=pltpu.VMEM)
+    return pl.pallas_call(
+        stencil_kernel,
+        out_shape=(
+            jax.ShapeDtypeStruct((nx, cy, cz), jnp.float32),
+            jax.ShapeDtypeStruct((2, nx, cz), jnp.float32),
+        ),
+        in_specs=[pl.BlockSpec(memory_space=pltpu.SMEM)] + [vmem] * 5,
+        out_specs=(vmem, vmem),
+    )(pulse, field, velocity, source, before, after)
+
+
+def update_kernel(dmat_ref, buf_ref, field_ref, forcing_ref, out_ref, grad_ref):
+    count = buf_ref.shape[0]
+    chunk = buf_ref.shape[1] - 8
+    for k in range(count):
+        rows = slice(k * chunk, (k + 1) * chunk)
+        out_ref[rows, :] = field_ref[rows, :] - pseudo_step * (buf_ref[k, :chunk, :] - forcing_ref[rows, :])
+    weights = jnp.zeros((count, buf_ref.shape[2]), jnp.float32)
+    for i in range(count):
+        weights = weights + dmat_ref[:, i : i + 1] * buf_ref[i, chunk + 2 : chunk + 3, :]
+    kept = buf_ref[:, chunk, :]
+    plain = buf_ref[:, chunk + 1, :]
+    parts = kept - pseudo_step * omega_rate * weights * plain
+    grad_ref[...] = jnp.sum(parts, axis=0, keepdims=True) / count
+
+
+def update(dmat, incoming, field, forcing):
+    rows, cz = field.shape
+    vmem = pl.BlockSpec(memory_space=pltpu.VMEM)
+    return pl.pallas_call(
+        update_kernel,
+        out_shape=(
+            jax.ShapeDtypeStruct((rows, cz), jnp.float32),
+            jax.ShapeDtypeStruct((1, cz), jnp.float32),
+        ),
+        in_specs=[vmem] * 4,
+        out_specs=(vmem, vmem),
+    )(dmat, incoming, field, forcing)
+
+
 def on_device(adjoint, base_flow, source, pulse, actuator):
     count = lax.axis_size("tm")
     nt_loc, nx, cy, cz = adjoint.shape
@@ -70,29 +156,13 @@
     velocity = base_flow[:, 0]
     ends = [jnp.stack([field[k], velocity[0, k] * field[k]]) for k in (0, nx - 1)]
     before, after = halo(ends, "space")
-    flux_x = velocity[0] * field
-    flux_y = velocity[1] * field
-    flux_z = velocity[2] * field
-    ahead_x = jnp.concatenate([flux_x[1:], after[1][None]], axis=0)
-    behind_x = jnp.concatenate([before[1][None], flux_x[:-1]], axis=0)
-    ahead = jnp.concatenate([field[1:], after[0][None]], axis=0)
-    behind = jnp.concatenate([before[0][None], field[:-1]], axis=0)
-    advect = 0.5 * (ahead_x - behind_x)
-    advect = advect + 0.5 * (wall_plus(flux_y) - wall_minus(flux_y))
-    advect = advect + 0.5 * (jnp.roll(flux_z, -1, axis=2) - jnp.roll(flux_z, 1, axis=2))
-    beside = ahead + behind
-    beside = beside + wall_plus(field) + wall_minus(field)
-    beside = beside + jnp.roll(field, -1, axis=2) + jnp.roll(field, 1, axis=2)
-    operator = advect + viscosity * (beside - 6.0 * field) - reaction * field
-    forcing = operator + source[0]
+    forcing, walls = stencil(pulse, field, velocity, source[0], before, after)
 
-    kept = field + pseudo_step * forcing
-    walls = jnp.stack([pulse[0] * kept[:, 0, :], field[:, 0, :]]).reshape(2, -1)
     onehot = (actuator[:, :, None] == jnp.arange(NACT, dtype=jnp.int32)[None, None, :]).astype(
         jnp.float32
     )
     terms = jnp.dot(
-        walls,
+        walls.reshape(2, -1),
         onehot.reshape(-1, NACT),
         precision=lax.Precision.HIGHEST,
         preferred_element_type=jnp.float32,
@@ -106,13 +176,8 @@
 
     outgoing = jnp.concatenate([derived.reshape(count, chunk, cz), grad_rows], axis=1)
     incoming = lax.all_to_all(outgoing, "tm", 0, 0, tiled=True)
-    time_term = incoming[:, :chunk].reshape(nx, cy, cz)
-    weights = jnp.dot(dmat, incoming[:, chunk + 2, 0], precision=lax.Precision.HIGHEST)
-    parts = incoming[:, chunk, :share] - pseudo_step * omega_rate * weights[:, None] * incoming[:, chunk + 1, :share]
-    gradient = jnp.sum(parts, axis=0) / total
-
-    updated = field - pseudo_step * (time_term - forcing)
-    return (updated[None], gradient)
+    updated, gradient = update(dmat, incoming, field.reshape(nx * cy, cz), forcing.reshape(nx * cy, cz))
+    return (updated.reshape(1, nx, cy, cz), gradient[0, :share])
 
 
 def solution(mesh):

time: 43.5 us -> 41.7 us (0.959)
  blocking collectives: 16.8 us -> 0 us
  waiting for transfers between devices: 2.52 us -> 15.5 us
  Pallas kernels: 0 us -> 4.27 us
  other arithmetic: 6.23 us -> 2.32 us
  starting transfers between devices: 9.02 us -> 12.5 us
  local copies, waits for them, and re-layouts: 5.68 us -> 3.59 us
  matrix products: 1.12 us -> 1.62 us
    all_to_all x1 -> x0, blocking collectives: 16.8 us -> none  [on_device(): incoming = lax.all_to_all(outgoing, 'tm', 0, 0, tiled=True)]
    all_to_all x0 -> x1, waiting for transfers between devices: none -> 10.6 us  [on_device(): incoming = lax.all_to_all(outgoing, 'tm', 0, 0, tiled=True)]
    pallas_call x0 -> x2, Pallas kernels: none -> 4.27 us  [the longest x1 2.35 us: stencil(): pl.pallas_call(stencil_kernel, out_shape=(jax.ShapeDtypeStruct((nx, cy, c...]
    all_to_all x0 -> x1, starting transfers between devices: none -> 3.55 us  [on_device(): incoming = lax.all_to_all(outgoing, 'tm', 0, 0, tiled=True)]
    all_to_all x1, waiting for transfers between devices: 1.54 us -> 3.75 us  [on_device(): lax.all_to_all(adjoint.reshape(count, chunk, cz), 'tm', 0, 0, tiled=True)]
    slice x14 -> x0, local copies, waits for them, and re-layouts: 1.8 us -> none  [the longest x1 0.76 us: on_device(): velocity[0, k] * field[k]]
    add x1 -> x0, other arithmetic: 1.76 us -> none  [on_device(): forcing = operator + source[0]]
    mul x2 -> x0, other arithmetic: 1.56 us -> none  [the longest x1 1.55 us: on_device(): flux_y = velocity[1] * field]
  transfers between devices with their start and end apart: 4 -> 5, of which waited for: 2 -> 4; matrix products, arithmetic and copies ran while one was open for 15% -> 5% of each run, Pallas kernels for 0% -> 6%
where the time goes in v6:
time: 41.7 us; the launch traced here: 41.2 us
  waiting for transfers between devices  15.5 us (37%)
  starting transfers between devices  12.5 us (30%)
  Pallas kernels  4.27 us (10%)
  local copies, waits for them, and re-layouts  3.59 us (9%)
  other arithmetic  2.32 us (6%)
  matrix products  1.62 us (4%)
  between operations  1.37 us (3%)
    all_to_all x1, waiting for transfers between devices, on_device(): incoming = lax.all_to_all(outgoing, 'tm', 0, 0, tiled=True)  10.6 us
    all_to_all x1, starting transfers between devices, on_device(): lax.all_to_all(adjoint.reshape(count, chunk, cz), 'tm', 0, 0, tiled=True)  7.89 us
    all_to_all x1, waiting for transfers between devices, on_device(): lax.all_to_all(adjoint.reshape(count, chunk, cz), 'tm', 0, 0, tiled=True)  3.75 us
    all_to_all x1, starting transfers between devices, on_device(): incoming = lax.all_to_all(outgoing, 'tm', 0, 0, tiled=True)  3.55 us
    pallas_call x1, Pallas kernels, stencil(): pl.pallas_call(stencil_kernel, out_shape=(jax.ShapeDtypeStruct((nx, cy, c...  2.35 us
    unnamed x11, local copies, waits for them, and re-layouts  2.05 us
    pallas_call x1, Pallas kernels, update(): pl.pallas_call(update_kernel, out_shape=(jax.ShapeDtypeStruct((rows, cz),...  1.92 us
    dot_general x1, matrix products, on_device(): jnp.dot(walls.reshape(2, -1), onehot.reshape(-1, NACT), precision=lax.Pre...  1.07 us
  transfers between devices with their start and end apart: 5, of which 4 were waited for; matrix products, arithmetic and copies ran while one was open for 5% of the time, Pallas kernels for 6%

profile of v6, /device:TPU:0, one launch (start us, length us, event | category | flops | bytes accessed | tf_op | source)
XLA Modules:
  0.0 41.2 jit_solution(12400480547840330817)
XLA Ops:
  0.6 0.8 %slice_bitcast_fusion.2 = (f32[1,64,128]{2,1,0:T(8,128)S(1)}, f32[1,64,128]{2,1,0:T(8,128)S(1)}) fusion(f32[1,8,64,128]{3,2,1,0:T(8,128)} %param.5), kind=kLoop, calls=%fused_computation.17 | loop fusion | bytes 131072 | tf_op jit(solution)/shard_map/slice | solution.py:157
  1.4 0.8 %fusion.5 = (f32[1,64,128]{2,1,0:T(8,128)S(1)}, f32[1,64,128]{2,1,0:T(8,128)S(1)}) fusion(f32[3,8,64,128]{3,2,1,0:T(8,128)} %bitcast.40, f32[1,8,64,128]{3,2,1,0:T(8,128)} %param.5), kind=kLoop, calls=%fused_computation.14 | loop fusion | flops 16384 | bytes 196608 | tf_op jit(solution)/shard_map/mul | solution.py:157
  2.2 0.5 %collective-permute-start = (f32[2,64,128]{2,1,0:T(8,128)S(1)}, f32[2,64,128]{2,1,0:T(8,128)S(1)}, u32[]{:S(2)}, u32[]{:S(2)}) collective-permute-start(f32[2,64,128]{2,1,0:T(8,128)S(1)} %pad_maximum_fusion.1), channel_id=1, source_target_pairs={{0,1},{1,0},{2,3},{3,2},{4,5},{5,4},{6,7},{7,6},{8,9},{9,8},{10,11... | collective-permute-start | bytes 196616 | tf_op jit(solution)/shard_map/ppermute | solution.py:52
  2.8 7.9 %all-to-all-start = ((f32[16,32,128]{2,1,0:T(8,128)}), f32[16,32,128]{2,1,0:T(8,128)S(1)}, u32[]{:S(2)}, u32[]{:S(2)}) async-start(f32[16,32,128]{2,1,0:T(8,128)} %bitcast), calls=%async_computation | async-start | bytes 524288 | tf_op jit(solution)/shard_map/all_to_all | solution.py:150
  10.7 0.3 collective-permute-start.1
  11.6 0.4 collective-permute-done.1.after_ref
  12.0 0.2 copy-done.1
  12.2 0.4 copy-done.2
  12.6 2.4 %shard_map.68 = (f32[8,64,128]{2,1,0:T(8,128)}, f32[2,8,128]{2,1,0:T(8,128)}) custom-call(f32[1]{0:T(128)S(6)} %copy.20.pulse_ref, f32[8,64,128]{2,1,0:T(8,128)} %bitcast.1.field_ref, f32[3,8,64,128]{3,2,1,0:T(8,128)} %bitcast.41, f32[8,64,128]{2,1,0:T(8,128)} %bitcast.43, f32[2,64,128]{2,1,0:T(8,128)} %copy-done.1, f32[2,64,128]{2,1,0:T(8,128)} %copy-done.2), custom_call_target="tpu_custom_call" | custom-call | tf_op jit(solution)/shard_map/pallas_call | solution.py:101
  15.0 1.1 %convolution_bitcast_fusion = f32[2,128]{1,0:T(2,128)S(1)} fusion(s32[8,128]{1,0:T(8,128)S(1)} %copy-done.3, f32[2,8,128]{2,1,0:T(8,128)} %get-tuple-element.9), kind=kOutput, calls=%fused_computation.2 | convolution fusion | flops 3276800 | bytes 13312 | tf_op jit(solution)/shard_map/dot_general | solution.py:164
  16.0 0.3 collective-permute-start.2
  16.5 0.8 %collective-permute-done.2 = f32[2,128]{1,0:T(2,128)S(1)} collective-permute-done((f32[2,128]{1,0:T(2,128)S(1)}, f32[2,128]{1,0:T(2,128)S(1)}, u32[]{:S(2)}, u32[]{:S(2)}) %collective-permute-start.2) | collective-permute-done | bytes 1056 | tf_op jit(solution)/shard_map/ppermute | solution.py:43
  17.2 0.1 reshape.70
  17.3 0.1 fusion.4
  17.4 3.7 %all-to-all-done = f32[16,32,128]{2,1,0:T(8,128)S(1)} async-done(((f32[16,32,128]{2,1,0:T(8,128)}), f32[16,32,128]{2,1,0:T(8,128)S(1)}, u32[]{:S(2)}, u32[]{:S(2)}) %all-to-all-start) | async-done | bytes 262176 | tf_op jit(solution)/shard_map/all_to_all | solution.py:150
  21.2 0.6 %fusion = f32[2,8,32,128]{3,1,2,0:T(8,128)S(1)} fusion(f32[2,8,32,128]{3,2,1,0:T(8,128)S(1)} %bitcast.38), kind=kOutput, calls=%fused_computation.1 | convolution fusion | flops 12654592 | bytes 524288 | tf_op jit(solution)/shard_map/ji,jp->ip/dot_general | solution.py:151
  21.8 0.7 %pad_maximum_fusion = f32[16,40,128]{2,1,0:T(8,128)} fusion(f32[16,8,128]{2,1,0:T(8,128)S(1)} %fusion.4, f32[16,32,128]{2,1,0:T(8,128)S(1)} %bitcast.39), kind=kLoop, calls=%fused_computation.4 | loop fusion | flops 81920 | bytes 655360 | tf_op jit(solution)/shard_map/concatenate | solution.py:177
  22.5 3.5 %all-to-all-start.1 = ((f32[16,40,128]{2,1,0:T(8,128)}), f32[16,40,128]{2,1,0:T(8,128)S(1)}, u32[]{:S(2)}, u32[]{:S(2)}) async-start(f32[16,40,128]{2,1,0:T(8,128)} %pad_maximum_fusion), calls=%async_computation.1 | async-start | bytes 655360 | tf_op jit(solution)/shard_map/all_to_all | solution.py:178
  26.1 0.7 %divide_select_fusion.dmat_ref = f32[16,16]{1,0:T(8,128)} fusion(), kind=kLoop, calls=%fused_computation.26 | loop fusion | flops 6144 | bytes 1024 | tf_op jit(solution)/shard_map/jit(_where)/select_n | solution.py:26
  26.8 10.6 %all-to-all-done.1.buf_ref = f32[16,40,128]{2,1,0:T(8,128)S(1)} async-done(((f32[16,40,128]{2,1,0:T(8,128)}), f32[16,40,128]{2,1,0:T(8,128)S(1)}, u32[]{:S(2)}, u32[]{:S(2)}) %all-to-all-start.1) | async-done | bytes 327712 | tf_op jit(solution)/shard_map/all_to_all | solution.py:178
  37.4 0.7 %copy-done = f32[16,40,128]{2,1,0:T(8,128)} copy-done((f32[16,40,128]{2,1,0:T(8,128)}, f32[16,40,128]{2,1,0:T(8,128)S(1)}, u32[]{:S(2)}) %copy-start) | copy-done | bytes 327704
  38.1 1.9 %shard_map.69 = (f32[512,128]{1,0:T(8,128)}, f32[1,128]{1,0:T(1,128)}) custom-call(f32[16,16]{1,0:T(8,128)} %divide_select_fusion.dmat_ref, f32[16,40,128]{2,1,0:T(8,128)} %copy-done, f32[512,128]{1,0:T(8,128)} %bitcast.11.field_ref, f32[512,128]{1,0:T(8,128)} %bitcast.42), custom_call_target="tpu_custom_call" | custom-call | tf_op jit(solution)/shard_map/pallas_call | solution.py:130
  40.0 0.7 %copy-done.4 = f32[1,128]{1,0:T(1,128)S(1)} copy-done((f32[1,128]{1,0:T(1,128)S(1)}, f32[1,128]{1,0:T(1,128)}, u32[]{:S(2)}) %copy-start.4) | copy-done | bytes 536
  40.7 0.5 %slice_bitcast_fusion.4 = f32[8]{0:T(128)} fusion(f32[1,128]{1,0:T(1,128)S(1)} %copy-done.4), kind=kLoop, calls=%fused_computation.34 | loop fusion | bytes 64 | tf_op jit(solution)/shard_map/squeeze | solution.py:180
  (15 shorter events, 0.3 us)
Async XLA Ops:
  2.2 9.4 %collective-permute-start = (f32[2,64,128]{2,1,0:T(8,128)S(1)}, f32[2,64,128]{2,1,0:T(8,128)S(1)}, u32[]{:S(2)}, u32[]{:S(2)}) collective-permute-start(f32[2,64,128]{2,1,0:T(8,128)S(1)} %pad_maximum_fusion.1), channel_id=1, source_target_pairs={{0,1},{1,0},{2,3},{3,2},{4,5},{5,4},{6,7},{7,6},{8,9},{9,8},{10,11... | collective-permute-start | bytes 196616 | tf_op jit(solution)/shard_map/ppermute | solution.py:52
  2.8 18.4 %all-to-all-start = ((f32[16,32,128]{2,1,0:T(8,128)}), f32[16,32,128]{2,1,0:T(8,128)S(1)}, u32[]{:S(2)}, u32[]{:S(2)}) async-start(f32[16,32,128]{2,1,0:T(8,128)} %bitcast), calls=%async_computation | async-start | bytes 524288 | tf_op jit(solution)/shard_map/all_to_all | solution.py:150
  10.7 1.3 %collective-permute-start.1 = (f32[2,64,128]{2,1,0:T(8,128)S(1)}, f32[2,64,128]{2,1,0:T(8,128)S(1)}, u32[]{:S(2)}, u32[]{:S(2)}) collective-permute-start(f32[2,64,128]{2,1,0:T(8,128)S(1)} %pad_maximum_fusion.2), channel_id=1, source_target_pairs={{1,0},{0,1},{3,2},{2,3},{5,4},{4,5},{7,6},{6,7},{9,8},{8,9},{11,10... | collective-permute-start | bytes 196616 | tf_op jit(solution)/shard_map/ppermute | solution.py:53
  11.6 0.6 %copy-start.1 = (f32[2,64,128]{2,1,0:T(8,128)}, f32[2,64,128]{2,1,0:T(8,128)S(1)}, u32[]{:S(2)}) copy-start(f32[2,64,128]{2,1,0:T(8,128)S(1)} %collective-permute-done.before_ref) | copy-start | bytes 196612
  12.0 0.6 %copy-start.2 = (f32[2,64,128]{2,1,0:T(8,128)}, f32[2,64,128]{2,1,0:T(8,128)S(1)}, u32[]{:S(2)}) copy-start(f32[2,64,128]{2,1,0:T(8,128)S(1)} %collective-permute-done.1.after_ref) | copy-start | bytes 196612
  12.6 2.4 %copy-start.3 = (s32[8,128]{1,0:T(8,128)S(1)}, s32[8,128]{1,0:T(8,128)}, u32[]{:S(2)}) copy-start(s32[8,128]{1,0:T(8,128)} %param.9) | copy-start | bytes 12292
  16.0 1.2 %collective-permute-start.2 = (f32[2,128]{1,0:T(2,128)S(1)}, f32[2,128]{1,0:T(2,128)S(1)}, u32[]{:S(2)}, u32[]{:S(2)}) collective-permute-start(f32[2,128]{1,0:T(2,128)S(1)} %convolution_bitcast_fusion), channel_id=1, source_target_pairs={{0,1},{1,0},{2,3},{3,2},{4,5},{5,4},{6,7},{7,6},{8,9},{9,8},{10,11... | collective-permute-start | bytes 3080 | tf_op jit(solution)/shard_map/ppermute | solution.py:43
  22.5 14.8 %all-to-all-start.1 = ((f32[16,40,128]{2,1,0:T(8,128)}), f32[16,40,128]{2,1,0:T(8,128)S(1)}, u32[]{:S(2)}, u32[]{:S(2)}) async-start(f32[16,40,128]{2,1,0:T(8,128)} %pad_maximum_fusion), calls=%async_computation.1 | async-start | bytes 655360 | tf_op jit(solution)/shard_map/all_to_all | solution.py:178
  37.4 0.7 %copy-start = (f32[16,40,128]{2,1,0:T(8,128)}, f32[16,40,128]{2,1,0:T(8,128)S(1)}, u32[]{:S(2)}) copy-start(f32[16,40,128]{2,1,0:T(8,128)S(1)} %all-to-all-done.1.buf_ref) | copy-start | bytes 983044
  40.0 0.7 %copy-start.4 = (f32[1,128]{1,0:T(1,128)S(1)}, f32[1,128]{1,0:T(1,128)}, u32[]{:S(2)}) copy-start(f32[1,128]{1,0:T(1,128)} %get-tuple-element.13) | copy-start | bytes 1540

commit v7 on v6

--- a/solution.py
+++ b/solution.py
@@ -47,6 +47,9 @@
 
 def halo(ends, axis):
     count = lax.axis_size(axis)
+    if count == 2:
+        swapped = lax.ppermute(ends, axis, [(0, 1), (1, 0)])
+        return swapped[1], swapped[0]
     up = [(i, (i + 1) % count) for i in range(count)]
     down = [(j, i) for i, j in up]
     before = lax.ppermute(ends[1], axis, up)
@@ -109,35 +112,6 @@
     )(pulse, field, velocity, source, before, after)
 
 
-def update_kernel(dmat_ref, buf_ref, field_ref, forcing_ref, out_ref, grad_ref):
-    count = buf_ref.shape[0]
-    chunk = buf_ref.shape[1] - 8
-    for k in range(count):
-        rows = slice(k * chunk, (k + 1) * chunk)
-        out_ref[rows, :] = field_ref[rows, :] - pseudo_step * (buf_ref[k, :chunk, :] - forcing_ref[rows, :])
-    weights = jnp.zeros((count, buf_ref.shape[2]), jnp.float32)
-    for i in range(count):
-        weights = weights + dmat_ref[:, i : i + 1] * buf_ref[i, chunk + 2 : chunk + 3, :]
-    kept = buf_ref[:, chunk, :]
-    plain = buf_ref[:, chunk + 1, :]
-    parts = kept - pseudo_step * omega_rate * weights * plain
-    grad_ref[...] = jnp.sum(parts, axis=0, keepdims=True) / count
-
-
-def update(dmat, incoming, field, forcing):
-    rows, cz = field.shape
-    vmem = pl.BlockSpec(memory_space=pltpu.VMEM)
-    return pl.pallas_call(
-        update_kernel,
-        out_shape=(
-            jax.ShapeDtypeStruct((rows, cz), jnp.float32),
-            jax.ShapeDtypeStruct((1, cz), jnp.float32),
-        ),
-        in_specs=[vmem] * 4,
-        out_specs=(vmem, vmem),
-    )(dmat, incoming, field, forcing)
-
-
 def on_device(adjoint, base_flow, source, pulse, actuator):
     count = lax.axis_size("tm")
     nt_loc, nx, cy, cz = adjoint.shape
@@ -154,7 +128,7 @@
 
     field = adjoint[0]
     velocity = base_flow[:, 0]
-    ends = [jnp.stack([field[k], velocity[0, k] * field[k]]) for k in (0, nx - 1)]
+    ends = jnp.stack([jnp.stack([field[k], velocity[0, k] * field[k]]) for k in (0, nx - 1)])
     before, after = halo(ends, "space")
     forcing, walls = stencil(pulse, field, velocity, source[0], before, after)
 
@@ -176,8 +150,12 @@
 
     outgoing = jnp.concatenate([derived.reshape(count, chunk, cz), grad_rows], axis=1)
     incoming = lax.all_to_all(outgoing, "tm", 0, 0, tiled=True)
-    updated, gradient = update(dmat, incoming, field.reshape(nx * cy, cz), forcing.reshape(nx * cy, cz))
-    return (updated.reshape(1, nx, cy, cz), gradient[0, :share])
+    time_term = incoming[:, :chunk].reshape(nx, cy, cz)
+    weights = jnp.dot(dmat, incoming[:, chunk + 2, 0], precision=lax.Precision.HIGHEST)
+    parts = incoming[:, chunk, :share] - pseudo_step * omega_rate * weights[:, None] * incoming[:, chunk + 1, :share]
+    gradient = jnp.sum(parts, axis=0) / total
+    updated = field - pseudo_step * (time_term - forcing)
+    return (updated[None], gradient)
 
 
 def solution(mesh):

time: 41.7 us -> 40.5 us (0.971)
  blocking collectives: 0 us -> 14.3 us
  waiting for transfers between devices: 15.5 us -> 5.16 us
  starting transfers between devices: 12.5 us -> 8.67 us
  Pallas kernels: 4.27 us -> 2.36 us
  other arithmetic: 2.32 us -> 3.29 us
  local copies, waits for them, and re-layouts: 3.59 us -> 3.05 us
    all_to_all x0 -> x1, blocking collectives: none -> 14.3 us  [on_device(): incoming = lax.all_to_all(outgoing, 'tm', 0, 0, tiled=True)]
    all_to_all x1 -> x0, waiting for transfers between devices: 10.6 us -> none  [on_device(): incoming = lax.all_to_all(outgoing, 'tm', 0, 0, tiled=True)]
    all_to_all x1 -> x0, starting transfers between devices: 3.55 us -> none  [on_device(): incoming = lax.all_to_all(outgoing, 'tm', 0, 0, tiled=True)]
    pallas_call x1 -> x0, Pallas kernels: 1.92 us -> none  [update(): pl.pallas_call(update_kernel, out_shape=(jax.ShapeDtypeStruct((rows, cz),...]
    broadcast_in_dim x0 -> x1, other arithmetic: none -> 1.71 us  [on_device(): return (updated[None], gradient)]
    unnamed x11 -> x8, local copies, waits for them, and re-layouts: 2.05 us -> 1.13 us
    concatenate x1, other arithmetic: 0.74 us -> 0.03 us  [on_device(): jnp.concatenate([derived.reshape(count, chunk, cz), grad_rows], axis=1)]
    select_n x1 -> x0, other arithmetic: 0.66 us -> none  [spectral_matrix(): jnp.where(skipped, jnp.float32(0.0), 0.5 * parity / safe_tan)]
  transfers between devices with their start and end apart: 5 -> 3, of which waited for: 4 -> 2; matrix products, arithmetic and copies ran while one was open for 5% -> 5% of each run, Pallas kernels for 6% -> 6%
where the time goes in v7:
time: 40.5 us; the launch traced here: 40 us
  blocking collectives  14.3 us (35%)
  starting transfers between devices  8.67 us (21%)
  waiting for transfers between devices  5.16 us (13%)
  other arithmetic  3.29 us (8%)
  local copies, waits for them, and re-layouts  3.05 us (8%)
  Pallas kernels  2.36 us (6%)
  matrix products  1.8 us (4%)
  between operations  1.37 us (3%)
    all_to_all x1, blocking collectives, on_device(): incoming = lax.all_to_all(outgoing, 'tm', 0, 0, tiled=True)  14.3 us
    all_to_all x1, starting transfers between devices, on_device(): lax.all_to_all(adjoint.reshape(count, chunk, cz), 'tm', 0, 0, tiled=True)  7.89 us
    all_to_all x1, waiting for transfers between devices, on_device(): lax.all_to_all(adjoint.reshape(count, chunk, cz), 'tm', 0, 0, tiled=True)  4.37 us
    pallas_call x1, Pallas kernels, stencil(): pl.pallas_call(stencil_kernel, out_shape=(jax.ShapeDtypeStruct((nx, cy, c...  2.36 us
    broadcast_in_dim x1, other arithmetic, on_device(): return (updated[None], gradient)  1.71 us
    unnamed x8, local copies, waits for them, and re-layouts  1.13 us
    dot_general x1, matrix products, on_device(): jnp.dot(walls.reshape(2, -1), onehot.reshape(-1, NACT), precision=lax.Pre...  1.07 us
    mul x1, other arithmetic, on_device(): velocity[0, k] * field[k]  0.82 us
  transfers between devices with their start and end apart: 3, of which 2 were waited for; matrix products, arithmetic and copies ran while one was open for 5% of the time, Pallas kernels for 6%

profile of v7, /device:TPU:0, one launch (start us, length us, event | category | flops | bytes accessed | tf_op | source)
XLA Modules:
  0.0 40.0 jit_solution(13147008915237995502)
XLA Ops:
  0.6 0.8 %slice_bitcast_fusion.5 = (f32[1,64,128]{2,1,0:T(8,128)S(1)}, f32[1,64,128]{2,1,0:T(8,128)S(1)}) fusion(f32[1,8,64,128]{3,2,1,0:T(8,128)} %param.5), kind=kLoop, calls=%fused_computation.27 | loop fusion | bytes 131072 | tf_op jit(solution)/shard_map/slice | solution.py:131
  1.4 0.8 %fusion.10 = (f32[1,64,128]{2,1,0:T(8,128)S(1)}, f32[1,64,128]{2,1,0:T(8,128)S(1)}) fusion(f32[3,8,64,128]{3,2,1,0:T(8,128)} %bitcast.69, f32[1,8,64,128]{3,2,1,0:T(8,128)} %param.5), kind=kLoop, calls=%fused_computation.25 | loop fusion | flops 16384 | bytes 196608 | tf_op jit(solution)/shard_map/mul | solution.py:131
  2.3 0.5 %collective-permute-start = (f32[2,2,64,128]{3,2,1,0:T(8,128)S(1)}, f32[2,2,64,128]{3,2,1,0:T(8,128)S(1)}, u32[]{:S(2)}, u32[]{:S(2)}) collective-permute-start(f32[2,2,64,128]{3,2,1,0:T(8,128)S(1)} %pad_maximum_fusion.1), channel_id=1, source_target_pairs={{0,1},{1,0},{2,3},{3,2},{4,5},{5,4},{6,7},{7,6},{8,9},{9,8},{10,11... | collective-permute-start | bytes 393224 | tf_op jit(solution)/shard_map/ppermute | solution.py:51
  2.8 7.9 %all-to-all-start = ((f32[16,32,128]{2,1,0:T(8,128)}), f32[16,32,128]{2,1,0:T(8,128)S(1)}, u32[]{:S(2)}, u32[]{:S(2)}) async-start(f32[16,32,128]{2,1,0:T(8,128)} %bitcast.1), calls=%async_computation | async-start | bytes 524288 | tf_op jit(solution)/shard_map/all_to_all | solution.py:124
  11.3 0.7 %slice_bitcast_fusion = (f32[2,64,128]{2,1,0:T(8,128)}, f32[2,64,128]{2,1,0:T(8,128)}) fusion(f32[2,2,64,128]{3,2,1,0:T(8,128)S(1)} %collective-permute-done), kind=kLoop, calls=%fused_computation.18 | loop fusion | bytes 262144 | tf_op jit(solution)/shard_map/squeeze | solution.py:52
  12.0 2.4 %shard_map.68 = (f32[8,64,128]{2,1,0:T(8,128)}, f32[2,8,128]{2,1,0:T(8,128)}) custom-call(f32[1]{0:T(128)S(6)} %copy.34.pulse_ref, f32[8,64,128]{2,1,0:T(8,128)} %bitcast.field_ref, f32[3,8,64,128]{3,2,1,0:T(8,128)} %bitcast.70, f32[8,64,128]{2,1,0:T(8,128)} %bitcast.71, f32[2,64,128]{2,1,0:T(8,128)} %get-tuple-element.17.before_ref, ...), custom_call_target="tpu_custom_call" | custom-call | tf_op jit(solution)/shard_map/pallas_call | solution.py:104
  14.4 1.1 %convolution_bitcast_fusion = f32[2,128]{1,0:T(2,128)S(1)} fusion(s32[8,128]{1,0:T(8,128)S(1)} %copy-done.1, f32[2,8,128]{2,1,0:T(8,128)} %get-tuple-element.7), kind=kOutput, calls=%fused_computation.2 | convolution fusion | flops 3276800 | bytes 13312 | tf_op jit(solution)/shard_map/dot_general | solution.py:138
  15.4 0.3 collective-permute-start.1
  15.7 0.1 pad.8.clone
  15.8 0.1 pad.9.clone
  15.9 0.8 %collective-permute-done.1 = f32[2,128]{1,0:T(2,128)S(1)} collective-permute-done((f32[2,128]{1,0:T(2,128)S(1)}, f32[2,128]{1,0:T(2,128)S(1)}, u32[]{:S(2)}, u32[]{:S(2)}) %collective-permute-start.1) | collective-permute-done | bytes 1056 | tf_op jit(solution)/shard_map/ppermute | solution.py:43
  16.6 0.1 reshape.69
  16.7 0.1 fusion.8
  16.8 4.4 %all-to-all-done = f32[16,32,128]{2,1,0:T(8,128)S(1)} async-done(((f32[16,32,128]{2,1,0:T(8,128)}), f32[16,32,128]{2,1,0:T(8,128)S(1)}, u32[]{:S(2)}, u32[]{:S(2)}) %all-to-all-start) | async-done | bytes 262176 | tf_op jit(solution)/shard_map/all_to_all | solution.py:124
  21.2 0.5 %fusion = f32[2,8,32,128]{3,1,2,0:T(8,128)S(1)} fusion(f32[2,8,32,128]{3,2,1,0:T(8,128)S(1)} %bitcast.66), kind=kOutput, calls=%fused_computation.1 | convolution fusion | flops 12654592 | bytes 524288 | tf_op jit(solution)/shard_map/ji,jp->ip/dot_general | solution.py:125
  21.8 14.3 %all_to_all.10 = f32[16,40,128]{2,1,0:T(8,128)S(1)} all-to-all(f32[16,40,128]{2,1,0:T(8,128)S(1)} %pad_maximum_fusion), channel_id=1, replica_groups=mesh['tm'=16,'space'=2] {'tm'}, dimensions={0} | all-to-all | bytes 655360 | tf_op jit(solution)/shard_map/all_to_all | solution.py:152
  36.1 0.2 slice_reduce_fusion
  36.3 0.2 fusion.1
  36.6 0.1 copy.23
  36.6 0.1 copy.24
  36.7 0.1 fusion.20
  36.8 0.5 %broadcast_multiply_fusion = f32[8]{0:T(128)} fusion(f32[8]{0:T(128)S(1)} %fusion.20), kind=kLoop, calls=%fused_computation.47 | loop fusion | flops 8 | bytes 64 | tf_op jit(solution)/shard_map/div | solution.py:156
  37.4 0.9 %copy-done = f32[8,64,128]{2,1,0:T(8,128)S(1)} copy-done((f32[8,64,128]{2,1,0:T(8,128)S(1)}, f32[8,64,128]{2,1,0:T(8,128)}, u32[]{:S(2)}) %copy-start) | copy-done | bytes 262168
  38.3 1.7 %fusion.6 = f32[1,8,64,128]{3,2,1,0:T(8,128)} fusion(f32[8,64,128]{2,1,0:T(8,128)S(1)} %copy-done, f32[1,8,64,128]{3,2,1,0:T(8,128)} %param.5, f32[8,64,128]{2,1,0:T(8,128)S(1)} %bitcast.68), kind=kLoop, calls=%fused_computation.12 | loop fusion | flops 196608 | bytes 1048576 | tf_op jit(solution)/shard_map/broadcast_in_dim | solution.py:158
  (13 shorter events, 0.2 us)
Async XLA Ops:
  2.3 9.1 %collective-permute-start = (f32[2,2,64,128]{3,2,1,0:T(8,128)S(1)}, f32[2,2,64,128]{3,2,1,0:T(8,128)S(1)}, u32[]{:S(2)}, u32[]{:S(2)}) collective-permute-start(f32[2,2,64,128]{3,2,1,0:T(8,128)S(1)} %pad_maximum_fusion.1), channel_id=1, source_target_pairs={{0,1},{1,0},{2,3},{3,2},{4,5},{5,4},{6,7},{7,6},{8,9},{9,8},{10,11... | collective-permute-start | bytes 393224 | tf_op jit(solution)/shard_map/ppermute | solution.py:51
  2.8 18.4 %all-to-all-start = ((f32[16,32,128]{2,1,0:T(8,128)}), f32[16,32,128]{2,1,0:T(8,128)S(1)}, u32[]{:S(2)}, u32[]{:S(2)}) async-start(f32[16,32,128]{2,1,0:T(8,128)} %bitcast.1), calls=%async_computation | async-start | bytes 524288 | tf_op jit(solution)/shard_map/all_to_all | solution.py:124
  12.0 2.4 %copy-start.1 = (s32[8,128]{1,0:T(8,128)S(1)}, s32[8,128]{1,0:T(8,128)}, u32[]{:S(2)}) copy-start(s32[8,128]{1,0:T(8,128)} %param.9) | copy-start | bytes 12292
  15.4 1.2 %collective-permute-start.1 = (f32[2,128]{1,0:T(2,128)S(1)}, f32[2,128]{1,0:T(2,128)S(1)}, u32[]{:S(2)}, u32[]{:S(2)}) collective-permute-start(f32[2,128]{1,0:T(2,128)S(1)} %convolution_bitcast_fusion), channel_id=1, source_target_pairs={{0,1},{1,0},{2,3},{3,2},{4,5},{5,4},{6,7},{7,6},{8,9},{9,8},{10,11... | collective-permute-start | bytes 3080 | tf_op jit(solution)/shard_map/ppermute | solution.py:43
  37.3 0.9 %copy-start = (f32[8,64,128]{2,1,0:T(8,128)S(1)}, f32[8,64,128]{2,1,0:T(8,128)}, u32[]{:S(2)}) copy-start(f32[8,64,128]{2,1,0:T(8,128)} %get-tuple-element.9) | copy-start | bytes 786436

commit v8 on v7

--- a/solution.py
+++ b/solution.py
@@ -45,19 +45,17 @@
     return x
 
 
-def halo(ends, axis):
+def neighbours(slab, axis):
     count = lax.axis_size(axis)
-    if count == 2:
-        swapped = lax.ppermute(ends, axis, [(0, 1), (1, 0)])
-        return swapped[1], swapped[0]
     up = [(i, (i + 1) % count) for i in range(count)]
     down = [(j, i) for i, j in up]
-    before = lax.ppermute(ends[1], axis, up)
-    after = lax.ppermute(ends[0], axis, down)
-    return before, after
+    prev = lax.ppermute(slab, axis, up)
+    if count == 2:
+        return prev, prev
+    return prev, lax.ppermute(slab, axis, down)
 
 
-def stencil_kernel(pulse_ref, field_ref, vel_ref, src_ref, before_ref, after_ref, forcing_ref, walls_ref):
+def stencil_kernel(pulse_ref, field_ref, vel_ref, src_ref, prev_ref, prev_u_ref, next_ref, next_u_ref, kept_ref, walls_ref):
     nx, cy, cz = field_ref.shape
     row = lax.broadcasted_iota(jnp.int32, (cy, cz), 0)
 
@@ -78,11 +76,11 @@
         if x + 1 < nx:
             ahead, ahead_x = field_ref[x + 1], vel_ref[0, x + 1] * field_ref[x + 1]
         else:
-            ahead, ahead_x = after_ref[0], after_ref[1]
+            ahead, ahead_x = next_ref[0, 0], next_u_ref[0, 0] * next_ref[0, 0]
         if x > 0:
             behind, behind_x = field_ref[x - 1], vel_ref[0, x - 1] * field_ref[x - 1]
         else:
-            behind, behind_x = before_ref[0], before_ref[1]
+            behind, behind_x = prev_ref[0, nx - 1], prev_u_ref[0, nx - 1] * prev_ref[0, nx - 1]
         flux_y = vel_ref[1, x] * f
         flux_z = vel_ref[2, x] * f
         advect = 0.5 * (ahead_x - behind_x)
@@ -92,13 +90,13 @@
         beside = beside + wall_up(f) + wall_down(f)
         beside = beside + span_up(f) + span_down(f)
         operator = advect + viscosity * (beside - 6.0 * f) - reaction * f
-        forcing = operator + src_ref[x]
-        forcing_ref[x] = forcing
-        walls_ref[0, x : x + 1, :] = pulse_ref[0] * (f[0:1] + pseudo_step * forcing[0:1])
+        kept = f + pseudo_step * (operator + src_ref[x])
+        kept_ref[x] = kept
+        walls_ref[0, x : x + 1, :] = pulse_ref[0] * kept[0:1]
         walls_ref[1, x : x + 1, :] = f[0:1]
 
 
-def stencil(pulse, field, velocity, source, before, after):
+def stencil(pulse, field, velocity, source, prev, nxt):
     nx, cy, cz = field.shape
     vmem = pl.BlockSpec(memory_space=pltpu.VMEM)
     return pl.pallas_call(
@@ -107,9 +105,9 @@
             jax.ShapeDtypeStruct((nx, cy, cz), jnp.float32),
             jax.ShapeDtypeStruct((2, nx, cz), jnp.float32),
         ),
-        in_specs=[pl.BlockSpec(memory_space=pltpu.SMEM)] + [vmem] * 5,
+        in_specs=[pl.BlockSpec(memory_space=pltpu.SMEM)] + [vmem] * 7,
         out_specs=(vmem, vmem),
-    )(pulse, field, velocity, source, before, after)
+    )(pulse, field, velocity, source, *prev, *nxt)
 
 
 def on_device(adjoint, base_flow, source, pulse, actuator):
@@ -128,9 +126,8 @@
 
     field = adjoint[0]
     velocity = base_flow[:, 0]
-    ends = jnp.stack([jnp.stack([field[k], velocity[0, k] * field[k]]) for k in (0, nx - 1)])
-    before, after = halo(ends, "space")
-    forcing, walls = stencil(pulse, field, velocity, source[0], before, after)
+    prev, nxt = neighbours((adjoint, base_flow[0]), "space")
+    kept, walls = stencil(pulse, field, velocity, source[0], prev, nxt)
 
     onehot = (actuator[:, :, None] == jnp.arange(NACT, dtype=jnp.int32)[None, None, :]).astype(
         jnp.float32
@@ -146,7 +143,7 @@
     slices = jnp.pad(slices, ((0, 0), (0, 0), (0, cz - share)))
     pulse_row = jnp.broadcast_to(pulse.reshape(1, 1, 1), (count, 1, cz))
     grad_rows = jnp.concatenate([slices, pulse_row, jnp.zeros((count, pad - 3, cz), jnp.float32)], axis=1)
-    forcing, grad_rows = lax.optimization_barrier((forcing, grad_rows))
+    kept, grad_rows = lax.optimization_barrier((kept, grad_rows))
 
     outgoing = jnp.concatenate([derived.reshape(count, chunk, cz), grad_rows], axis=1)
     incoming = lax.all_to_all(outgoing, "tm", 0, 0, tiled=True)
@@ -154,7 +151,7 @@
     weights = jnp.dot(dmat, incoming[:, chunk + 2, 0], precision=lax.Precision.HIGHEST)
     parts = incoming[:, chunk, :share] - pseudo_step * omega_rate * weights[:, None] * incoming[:, chunk + 1, :share]
     gradient = jnp.sum(parts, axis=0) / total
-    updated = field - pseudo_step * (time_term - forcing)
+    updated = kept - pseudo_step * time_term
     return (updated[None], gradient)
 
 

time: 40.5 us -> 39.4 us (0.973)
  other arithmetic: 3.29 us -> 1.51 us
  waiting for transfers between devices: 5.16 us -> 4.52 us
  blocking collectives: 14.3 us -> 14.8 us
    broadcast_in_dim x1, other arithmetic: 1.71 us -> 0.73 us  [on_device(): return (updated[None], gradient)]
    all_to_all x1, waiting for transfers between devices: 4.37 us -> 3.55 us  [on_device(): lax.all_to_all(adjoint.reshape(count, chunk, cz), 'tm', 0, 0, tiled=True)]
    slice x2 -> x0, local copies, waits for them, and re-layouts: 0.8 us -> none  [the longest x1 0.78 us: on_device(): field[k]]
    mul x1, other arithmetic: 0.82 us -> 0.03 us  [on_device(): updated = kept - pseudo_step * time_term]
    unnamed x8 -> x12, local copies, waits for them, and re-layouts: 1.13 us -> 1.89 us
    all_to_all x1, blocking collectives: 14.3 us -> 14.8 us  [on_device(): incoming = lax.all_to_all(outgoing, 'tm', 0, 0, tiled=True)]
    all_to_all x1, starting transfers between devices: 7.89 us -> 8.29 us  [on_device(): lax.all_to_all(adjoint.reshape(count, chunk, cz), 'tm', 0, 0, tiled=True)]
  transfers between devices with their start and end apart: 3 -> 4, of which waited for: 2 -> 2; matrix products, arithmetic and copies ran while one was open for 5% -> 4% of each run, Pallas kernels for 6% -> 7%
where the time goes in v8:
time: 39.4 us; the launch traced here: 39 us
  blocking collectives  14.8 us (38%)
  starting transfers between devices  8.96 us (23%)
  waiting for transfers between devices  4.52 us (11%)
  local copies, waits for them, and re-layouts  3.31 us (8%)
  Pallas kernels  2.65 us (7%)
  matrix products  1.81 us (5%)
  other arithmetic  1.51 us (4%)
  between operations  1.39 us (4%)
    all_to_all x1, blocking collectives, on_device(): incoming = lax.all_to_all(outgoing, 'tm', 0, 0, tiled=True)  14.8 us
    all_to_all x1, starting transfers between devices, on_device(): lax.all_to_all(adjoint.reshape(count, chunk, cz), 'tm', 0, 0, tiled=True)  8.29 us
    all_to_all x1, waiting for transfers between devices, on_device(): lax.all_to_all(adjoint.reshape(count, chunk, cz), 'tm', 0, 0, tiled=True)  3.55 us
    pallas_call x1, Pallas kernels, stencil(): pl.pallas_call(stencil_kernel, out_shape=(jax.ShapeDtypeStruct((nx, cy, c...  2.65 us
    unnamed x12, local copies, waits for them, and re-layouts  1.89 us
    dot_general x1, matrix products, on_device(): jnp.dot(walls.reshape(2, -1), onehot.reshape(-1, NACT), precision=lax.Pre...  1.07 us
    ppermute x1, waiting for transfers between devices, butterfly_sum(): x = x + lax.ppermute(x, axis, [(i, i ^ bit) for i in range(groups)])  0.97 us
    squeeze x1, local copies, waits for them, and re-layouts, on_device(): prev, nxt = neighbours((adjoint, base_flow[0]), 'space')  0.97 us
  transfers between devices with their start and end apart: 4, of which 2 were waited for; matrix products, arithmetic and copies ran while one was open for 4% of the time, Pallas kernels for 7%

profile of v8, /device:TPU:0, one launch (start us, length us, event | category | flops | bytes accessed | tf_op | source)
XLA Modules:
  0.0 39.0 jit_solution(14691447421097261733)
XLA Ops:
  0.6 1.0 %slice_bitcast_fusion = f32[1,8,64,128]{3,2,1,0:T(8,128)S(1)} fusion(f32[3,1,8,64,128]{4,3,2,1,0:T(8,128)} %param.6), kind=kLoop, calls=%fused_computation.13 | loop fusion | bytes 524288 | tf_op jit(solution)/shard_map/squeeze | solution.py:129
  1.6 0.5 %collective-permute-start.1 = (f32[1,8,64,128]{3,2,1,0:T(8,128)S(1)}, f32[1,8,64,128]{3,2,1,0:T(8,128)S(1)}, u32[]{:S(2)}, u32[]{:S(2)}) collective-permute-start(f32[1,8,64,128]{3,2,1,0:T(8,128)S(1)} %slice_bitcast_fusion), channel_id=1, source_target_pairs={{0,1},{1,0},{2,3},{3,2},{4,5},{5,4},{6,7},{7,6},{8,9},{9,8},{10,11... | collective-permute-start | bytes 786440 | tf_op jit(solution)/shard_map/ppermute | solution.py:52
  2.1 0.1 collective-permute-start
  2.2 8.3 %all-to-all-start = ((f32[16,32,128]{2,1,0:T(8,128)}), f32[16,32,128]{2,1,0:T(8,128)S(1)}, u32[]{:S(2)}, u32[]{:S(2)}) async-start(f32[16,32,128]{2,1,0:T(8,128)} %bitcast.7), calls=%async_computation | async-start | bytes 524288 | tf_op jit(solution)/shard_map/all_to_all | solution.py:122
  11.2 0.7 %copy-done = f32[1,8,64,128]{3,2,1,0:T(8,128)} copy-done((f32[1,8,64,128]{3,2,1,0:T(8,128)}, f32[1,8,64,128]{3,2,1,0:T(8,128)S(1)}, u32[]{:S(2)}) %copy-start) | copy-done | bytes 262168
  11.9 0.1 copy-done.1
  11.9 2.7 %shard_map.68 = (f32[8,64,128]{2,1,0:T(8,128)}, f32[2,8,128]{2,1,0:T(8,128)}) custom-call(f32[1]{0:T(128)S(6)} %copy.34.pulse_ref, f32[8,64,128]{2,1,0:T(8,128)} %bitcast.field_ref, f32[3,8,64,128]{3,2,1,0:T(8,128)} %bitcast.39, f32[8,64,128]{2,1,0:T(8,128)} %bitcast.43, f32[1,8,64,128]{3,2,1,0:T(8,128)} %copy-done.1, f32[1,8,64,128]{3,2,1,0:T(8,128)} %copy-done, ...), custom_call_target="tpu_custom_call" | custom-call | tf_op jit(solution)/shard_map/pallas_call | solution.py:102
  14.6 1.1 %convolution_bitcast_fusion = f32[2,128]{1,0:T(2,128)S(1)} fusion(s32[8,128]{1,0:T(8,128)S(1)} %copy-done.3, f32[2,8,128]{2,1,0:T(8,128)} %get-tuple-element.7), kind=kOutput, calls=%fused_computation.2 | convolution fusion | flops 3276800 | bytes 13312 | tf_op jit(solution)/shard_map/dot_general | solution.py:135
  15.7 0.1 collective-permute-start.2
  15.8 0.1 pad.8.clone
  15.8 0.1 pad.9.clone
  15.9 1.0 %collective-permute-done.2 = f32[2,128]{1,0:T(2,128)S(1)} collective-permute-done((f32[2,128]{1,0:T(2,128)S(1)}, f32[2,128]{1,0:T(2,128)S(1)}, u32[]{:S(2)}, u32[]{:S(2)}) %collective-permute-start.2) | collective-permute-done | bytes 1056 | tf_op jit(solution)/shard_map/ppermute | solution.py:43
  16.9 0.1 reshape.28
  17.0 0.1 fusion.6
  17.1 3.5 %all-to-all-done = f32[16,32,128]{2,1,0:T(8,128)S(1)} async-done(((f32[16,32,128]{2,1,0:T(8,128)}), f32[16,32,128]{2,1,0:T(8,128)S(1)}, u32[]{:S(2)}, u32[]{:S(2)}) %all-to-all-start) | async-done | bytes 262176 | tf_op jit(solution)/shard_map/all_to_all | solution.py:122
  20.6 0.5 %fusion = f32[2,8,32,128]{3,1,2,0:T(8,128)S(1)} fusion(f32[2,8,32,128]{3,2,1,0:T(8,128)S(1)} %bitcast.41), kind=kOutput, calls=%fused_computation.1 | convolution fusion | flops 12654592 | bytes 524288 | tf_op jit(solution)/shard_map/ji,jp->ip/dot_general | solution.py:123
  21.3 14.8 %all_to_all.10 = f32[16,40,128]{2,1,0:T(8,128)S(1)} all-to-all(f32[16,40,128]{2,1,0:T(8,128)S(1)} %pad_maximum_fusion), channel_id=1, replica_groups=mesh['tm'=16,'space'=2] {'tm'}, dimensions={0} | all-to-all | bytes 655360 | tf_op jit(solution)/shard_map/all_to_all | solution.py:149
  36.1 0.1 copy.23
  36.3 0.2 slice_reduce_fusion
  36.5 0.2 fusion.1
  36.7 0.1 fusion.16
  36.8 0.5 %broadcast_multiply_fusion = f32[8]{0:T(128)} fusion(f32[8]{0:T(128)S(1)} %fusion.16), kind=kLoop, calls=%fused_computation.36 | loop fusion | flops 8 | bytes 64 | tf_op jit(solution)/shard_map/div | solution.py:153
  37.3 0.9 %copy-done.2 = f32[8,64,128]{2,1,0:T(8,128)S(1)} copy-done((f32[8,64,128]{2,1,0:T(8,128)S(1)}, f32[8,64,128]{2,1,0:T(8,128)}, u32[]{:S(2)}) %copy-start.2) | copy-done | bytes 262168
  38.3 0.7 %fusion.4 = f32[1,8,64,128]{3,2,1,0:T(8,128)} fusion(f32[8,64,128]{2,1,0:T(8,128)S(1)} %copy-done.2, f32[8,64,128]{2,1,0:T(8,128)S(1)} %bitcast.40), kind=kLoop, calls=%fused_computation.11 | loop fusion | flops 65536 | bytes 786432 | tf_op jit(solution)/shard_map/broadcast_in_dim | solution.py:155
  (15 shorter events, 0.2 us)
Async XLA Ops:
  1.6 9.5 %collective-permute-start.1 = (f32[1,8,64,128]{3,2,1,0:T(8,128)S(1)}, f32[1,8,64,128]{3,2,1,0:T(8,128)S(1)}, u32[]{:S(2)}, u32[]{:S(2)}) collective-permute-start(f32[1,8,64,128]{3,2,1,0:T(8,128)S(1)} %slice_bitcast_fusion), channel_id=1, source_target_pairs={{0,1},{1,0},{2,3},{3,2},{4,5},{5,4},{6,7},{7,6},{8,9},{9,8},{10,11... | collective-permute-start | bytes 786440 | tf_op jit(solution)/shard_map/ppermute | solution.py:52
  2.1 9.0 %collective-permute-start = (f32[1,8,64,128]{3,2,1,0:T(8,128)}, f32[1,8,64,128]{3,2,1,0:T(8,128)S(1)}, u32[]{:S(2)}, u32[]{:S(2)}) collective-permute-start(f32[1,8,64,128]{3,2,1,0:T(8,128)} %param.5), channel_id=1, source_target_pairs={{0,1},{1,0},{2,3},{3,2},{4,5},{5,4},{6,7},{7,6},{8,9},{9,8},{10,11... | collective-permute-start | bytes 786440 | tf_op jit(solution)/shard_map/ppermute | solution.py:52
  2.2 18.4 %all-to-all-start = ((f32[16,32,128]{2,1,0:T(8,128)}), f32[16,32,128]{2,1,0:T(8,128)S(1)}, u32[]{:S(2)}, u32[]{:S(2)}) async-start(f32[16,32,128]{2,1,0:T(8,128)} %bitcast.7), calls=%async_computation | async-start | bytes 524288 | tf_op jit(solution)/shard_map/all_to_all | solution.py:122
  11.2 0.7 %copy-start = (f32[1,8,64,128]{3,2,1,0:T(8,128)}, f32[1,8,64,128]{3,2,1,0:T(8,128)S(1)}, u32[]{:S(2)}) copy-start(f32[1,8,64,128]{3,2,1,0:T(8,128)S(1)} %collective-permute-done.1.prev_u_ref.next_u_ref) | copy-start | bytes 786436
  11.2 0.8 %copy-start.1 = (f32[1,8,64,128]{3,2,1,0:T(8,128)}, f32[1,8,64,128]{3,2,1,0:T(8,128)S(1)}, u32[]{:S(2)}) copy-start(f32[1,8,64,128]{3,2,1,0:T(8,128)S(1)} %collective-permute-done.prev_ref.next_ref) | copy-start | bytes 786436
  11.9 2.7 %copy-start.3 = (s32[8,128]{1,0:T(8,128)S(1)}, s32[8,128]{1,0:T(8,128)}, u32[]{:S(2)}) copy-start(s32[8,128]{1,0:T(8,128)} %param.9) | copy-start | bytes 12292
  15.7 1.2 %collective-permute-start.2 = (f32[2,128]{1,0:T(2,128)S(1)}, f32[2,128]{1,0:T(2,128)S(1)}, u32[]{:S(2)}, u32[]{:S(2)}) collective-permute-start(f32[2,128]{1,0:T(2,128)S(1)} %convolution_bitcast_fusion), channel_id=1, source_target_pairs={{0,1},{1,0},{2,3},{3,2},{4,5},{5,4},{6,7},{7,6},{8,9},{9,8},{10,11... | collective-permute-start | bytes 3080 | tf_op jit(solution)/shard_map/ppermute | solution.py:43
  37.3 0.9 %copy-start.2 = (f32[8,64,128]{2,1,0:T(8,128)S(1)}, f32[8,64,128]{2,1,0:T(8,128)}, u32[]{:S(2)}) copy-start(f32[8,64,128]{2,1,0:T(8,128)} %get-tuple-element.8) | copy-start | bytes 786436

commit v9 on v8

--- a/solution.py
+++ b/solution.py
@@ -120,8 +120,11 @@
     dmat = spectral_matrix(total)
 
     incoming = lax.all_to_all(adjoint.reshape(count, chunk, cz), "tm", 0, 0, tiled=True)
-    derived = omega_rate * jnp.einsum(
-        "ji,jp->ip", dmat, incoming.reshape(total, chunk * cz), precision=lax.Precision.HIGHEST
+    derived = jnp.einsum(
+        "ji,jp->ip",
+        (-pseudo_step * omega_rate) * dmat,
+        incoming.reshape(total, chunk * cz),
+        precision=lax.Precision.HIGHEST,
     )
 
     field = adjoint[0]
@@ -147,11 +150,12 @@
 
     outgoing = jnp.concatenate([derived.reshape(count, chunk, cz), grad_rows], axis=1)
     incoming = lax.all_to_all(outgoing, "tm", 0, 0, tiled=True)
-    time_term = incoming[:, :chunk].reshape(nx, cy, cz)
-    weights = jnp.dot(dmat, incoming[:, chunk + 2, 0], precision=lax.Precision.HIGHEST)
-    parts = incoming[:, chunk, :share] - pseudo_step * omega_rate * weights[:, None] * incoming[:, chunk + 1, :share]
+    scaled_term = incoming[:, :chunk].reshape(nx, cy, cz)
+    tile = incoming[:, chunk : chunk + 3, :share]
+    weights = jnp.sum(dmat * tile[None, :, 2, 0], axis=1)
+    parts = tile[:, 0] - pseudo_step * omega_rate * weights[:, None] * tile[:, 1]
     gradient = jnp.sum(parts, axis=0) / total
-    updated = kept - pseudo_step * time_term
+    updated = kept + scaled_term
     return (updated[None], gradient)
 
 

time: 39.4 us -> 39.3 us (level)
    unnamed x12 -> x10, local copies, waits for them, and re-layouts: 1.89 us -> 1.83 us
where the time goes in v9:
time: 39.3 us; the launch traced here: 38.9 us
  blocking collectives  14.9 us (38%)
  starting transfers between devices  8.96 us (23%)
  waiting for transfers between devices  4.51 us (11%)
  local copies, waits for them, and re-layouts  3.37 us (9%)
  Pallas kernels  2.66 us (7%)
  other arithmetic  1.58 us (4%)
  matrix products  1.57 us (4%)
  between operations  1.39 us (4%)
    all_to_all x1, blocking collectives, on_device(): incoming = lax.all_to_all(outgoing, 'tm', 0, 0, tiled=True)  14.9 us
    all_to_all x1, starting transfers between devices, on_device(): lax.all_to_all(adjoint.reshape(count, chunk, cz), 'tm', 0, 0, tiled=True)  8.29 us
    all_to_all x1, waiting for transfers between devices, on_device(): lax.all_to_all(adjoint.reshape(count, chunk, cz), 'tm', 0, 0, tiled=True)  3.54 us
    pallas_call x1, Pallas kernels, stencil(): pl.pallas_call(stencil_kernel, out_shape=(jax.ShapeDtypeStruct((nx, cy, c...  2.66 us
    unnamed x10, local copies, waits for them, and re-layouts  1.83 us
    dot_general x1, matrix products, on_device(): jnp.dot(walls.reshape(2, -1), onehot.reshape(-1, NACT), precision=lax.Pre...  1.07 us
    ppermute x1, waiting for transfers between devices, butterfly_sum(): x = x + lax.ppermute(x, axis, [(i, i ^ bit) for i in range(groups)])  0.97 us
    squeeze x1, local copies, waits for them, and re-layouts, on_device(): prev, nxt = neighbours((adjoint, base_flow[0]), 'space')  0.97 us
  transfers between devices with their start and end apart: 4, of which 2 were waited for; matrix products, arithmetic and copies ran while one was open for 4% of the time, Pallas kernels for 7%

profile of v9, /device:TPU:0, one launch (start us, length us, event | category | flops | bytes accessed | tf_op | source)
XLA Modules:
  0.0 38.9 jit_solution(15943634231602410269)
XLA Ops:
  0.6 1.0 %slice_bitcast_fusion = f32[1,8,64,128]{3,2,1,0:T(8,128)S(1)} fusion(f32[3,1,8,64,128]{4,3,2,1,0:T(8,128)} %param.6), kind=kLoop, calls=%fused_computation.10 | loop fusion | bytes 524288 | tf_op jit(solution)/shard_map/squeeze | solution.py:132
  1.6 0.5 %collective-permute-start.1 = (f32[1,8,64,128]{3,2,1,0:T(8,128)S(1)}, f32[1,8,64,128]{3,2,1,0:T(8,128)S(1)}, u32[]{:S(2)}, u32[]{:S(2)}) collective-permute-start(f32[1,8,64,128]{3,2,1,0:T(8,128)S(1)} %slice_bitcast_fusion), channel_id=1, source_target_pairs={{0,1},{1,0},{2,3},{3,2},{4,5},{5,4},{6,7},{7,6},{8,9},{9,8},{10,11... | collective-permute-start | bytes 786440 | tf_op jit(solution)/shard_map/ppermute | solution.py:52
  2.1 0.1 collective-permute-start
  2.2 8.3 %all-to-all-start = ((f32[16,32,128]{2,1,0:T(8,128)}), f32[16,32,128]{2,1,0:T(8,128)S(1)}, u32[]{:S(2)}, u32[]{:S(2)}) async-start(f32[16,32,128]{2,1,0:T(8,128)} %bitcast.8), calls=%async_computation | async-start | bytes 524288 | tf_op jit(solution)/shard_map/all_to_all | solution.py:122
  11.2 0.7 %copy-done = f32[1,8,64,128]{3,2,1,0:T(8,128)} copy-done((f32[1,8,64,128]{3,2,1,0:T(8,128)}, f32[1,8,64,128]{3,2,1,0:T(8,128)S(1)}, u32[]{:S(2)}) %copy-start) | copy-done | bytes 262168
  11.8 0.1 copy-done.1
  11.9 2.7 %shard_map.68 = (f32[8,64,128]{2,1,0:T(8,128)}, f32[2,8,128]{2,1,0:T(8,128)}) custom-call(f32[1]{0:T(128)S(6)} %copy.34.pulse_ref, f32[8,64,128]{2,1,0:T(8,128)} %bitcast.field_ref, f32[3,8,64,128]{3,2,1,0:T(8,128)} %bitcast.41, f32[8,64,128]{2,1,0:T(8,128)} %bitcast.44, f32[1,8,64,128]{3,2,1,0:T(8,128)} %copy-done.1, f32[1,8,64,128]{3,2,1,0:T(8,128)} %copy-done, ...), custom_call_target="tpu_custom_call" | custom-call | tf_op jit(solution)/shard_map/pallas_call | solution.py:102
  14.6 1.1 %convolution_bitcast_fusion = f32[2,128]{1,0:T(2,128)S(1)} fusion(s32[8,128]{1,0:T(8,128)S(1)} %copy-done.3, f32[2,8,128]{2,1,0:T(8,128)} %get-tuple-element.7), kind=kOutput, calls=%fused_computation | convolution fusion | flops 3276800 | bytes 13312 | tf_op jit(solution)/shard_map/dot_general | solution.py:138
  15.7 0.1 collective-permute-start.2
  15.8 0.1 pad.8.clone
  15.8 0.1 pad.9.clone
  15.9 1.0 %collective-permute-done.2 = f32[2,128]{1,0:T(2,128)S(1)} collective-permute-done((f32[2,128]{1,0:T(2,128)S(1)}, f32[2,128]{1,0:T(2,128)S(1)}, u32[]{:S(2)}, u32[]{:S(2)}) %collective-permute-start.2) | collective-permute-done | bytes 1056 | tf_op jit(solution)/shard_map/ppermute | solution.py:43
  16.9 0.1 reshape.30
  17.0 0.1 fusion.5
  17.1 3.5 %all-to-all-done = f32[16,32,128]{2,1,0:T(8,128)S(1)} async-done(((f32[16,32,128]{2,1,0:T(8,128)}), f32[16,32,128]{2,1,0:T(8,128)S(1)}, u32[]{:S(2)}, u32[]{:S(2)}) %all-to-all-start) | async-done | bytes 262176 | tf_op jit(solution)/shard_map/all_to_all | solution.py:122
  20.6 0.5 %fusion = f32[16,32,128]{2,0,1:T(8,128)S(1)} fusion(f32[2,8,32,128]{3,2,1,0:T(8,128)S(1)} %bitcast.43), kind=kOutput, calls=%fused_computation.4 | convolution fusion | flops 12589312 | bytes 524288 | tf_op jit(solution)/shard_map/ji,jp->ip/dot_general | solution.py:123
  21.2 0.1 copy.18
  21.3 14.9 %all_to_all.10 = f32[16,40,128]{2,1,0:T(8,128)S(1)} all-to-all(f32[16,40,128]{2,1,0:T(8,128)S(1)} %copy.18), channel_id=1, replica_groups=mesh['tm'=16,'space'=2] {'tm'}, dimensions={0} | all-to-all | bytes 655360 | tf_op jit(solution)/shard_map/all_to_all | solution.py:152
  36.3 0.2 slice_reduce_fusion
  36.5 0.1 multiply_reduce_fusion
  36.6 0.1 fusion.17
  36.7 0.5 %broadcast_multiply_fusion = f32[8]{0:T(128)} fusion(f32[8]{0:T(128)S(1)} %fusion.17), kind=kLoop, calls=%fused_computation.36 | loop fusion | flops 8 | bytes 64 | tf_op jit(solution)/shard_map/div | solution.py:157
  37.3 0.9 %copy-done.2 = f32[8,64,128]{2,1,0:T(8,128)S(1)} copy-done((f32[8,64,128]{2,1,0:T(8,128)S(1)}, f32[8,64,128]{2,1,0:T(8,128)}, u32[]{:S(2)}) %copy-start.2) | copy-done | bytes 262168
  38.2 0.7 %fusion.3 = f32[1,8,64,128]{3,2,1,0:T(8,128)} fusion(f32[8,64,128]{2,1,0:T(8,128)S(1)} %copy-done.2, f32[8,64,128]{2,1,0:T(8,128)S(1)} %bitcast.42), kind=kLoop, calls=%fused_computation.8 | loop fusion | flops 65536 | bytes 786432 | tf_op jit(solution)/shard_map/broadcast_in_dim | solution.py:159
  (15 shorter events, 0.2 us)
Async XLA Ops:
  1.6 9.5 %collective-permute-start.1 = (f32[1,8,64,128]{3,2,1,0:T(8,128)S(1)}, f32[1,8,64,128]{3,2,1,0:T(8,128)S(1)}, u32[]{:S(2)}, u32[]{:S(2)}) collective-permute-start(f32[1,8,64,128]{3,2,1,0:T(8,128)S(1)} %slice_bitcast_fusion), channel_id=1, source_target_pairs={{0,1},{1,0},{2,3},{3,2},{4,5},{5,4},{6,7},{7,6},{8,9},{9,8},{10,11... | collective-permute-start | bytes 786440 | tf_op jit(solution)/shard_map/ppermute | solution.py:52
  2.1 9.0 %collective-permute-start = (f32[1,8,64,128]{3,2,1,0:T(8,128)}, f32[1,8,64,128]{3,2,1,0:T(8,128)S(1)}, u32[]{:S(2)}, u32[]{:S(2)}) collective-permute-start(f32[1,8,64,128]{3,2,1,0:T(8,128)} %param.5), channel_id=1, source_target_pairs={{0,1},{1,0},{2,3},{3,2},{4,5},{5,4},{6,7},{7,6},{8,9},{9,8},{10,11... | collective-permute-start | bytes 786440 | tf_op jit(solution)/shard_map/ppermute | solution.py:52
  2.2 18.4 %all-to-all-start = ((f32[16,32,128]{2,1,0:T(8,128)}), f32[16,32,128]{2,1,0:T(8,128)S(1)}, u32[]{:S(2)}, u32[]{:S(2)}) async-start(f32[16,32,128]{2,1,0:T(8,128)} %bitcast.8), calls=%async_computation | async-start | bytes 524288 | tf_op jit(solution)/shard_map/all_to_all | solution.py:122
  11.2 0.7 %copy-start = (f32[1,8,64,128]{3,2,1,0:T(8,128)}, f32[1,8,64,128]{3,2,1,0:T(8,128)S(1)}, u32[]{:S(2)}) copy-start(f32[1,8,64,128]{3,2,1,0:T(8,128)S(1)} %collective-permute-done.1.prev_u_ref.next_u_ref) | copy-start | bytes 786436
  11.2 0.8 %copy-start.1 = (f32[1,8,64,128]{3,2,1,0:T(8,128)}, f32[1,8,64,128]{3,2,1,0:T(8,128)S(1)}, u32[]{:S(2)}) copy-start(f32[1,8,64,128]{3,2,1,0:T(8,128)S(1)} %collective-permute-done.prev_ref.next_ref) | copy-start | bytes 786436
  11.9 2.7 %copy-start.3 = (s32[8,128]{1,0:T(8,128)S(1)}, s32[8,128]{1,0:T(8,128)}, u32[]{:S(2)}) copy-start(s32[8,128]{1,0:T(8,128)} %param.9) | copy-start | bytes 12292
  15.7 1.2 %collective-permute-start.2 = (f32[2,128]{1,0:T(2,128)S(1)}, f32[2,128]{1,0:T(2,128)S(1)}, u32[]{:S(2)}, u32[]{:S(2)}) collective-permute-start(f32[2,128]{1,0:T(2,128)S(1)} %convolution_bitcast_fusion), channel_id=1, source_target_pairs={{0,1},{1,0},{2,3},{3,2},{4,5},{5,4},{6,7},{7,6},{8,9},{9,8},{10,11... | collective-permute-start | bytes 3080 | tf_op jit(solution)/shard_map/ppermute | solution.py:43
  37.2 0.9 %copy-start.2 = (f32[8,64,128]{2,1,0:T(8,128)S(1)}, f32[8,64,128]{2,1,0:T(8,128)}, u32[]{:S(2)}) copy-start(f32[8,64,128]{2,1,0:T(8,128)} %get-tuple-element.8) | copy-start | bytes 786436

commit v10 on v9

--- a/solution.py
+++ b/solution.py
@@ -76,11 +76,11 @@
         if x + 1 < nx:
             ahead, ahead_x = field_ref[x + 1], vel_ref[0, x + 1] * field_ref[x + 1]
         else:
-            ahead, ahead_x = next_ref[0, 0], next_u_ref[0, 0] * next_ref[0, 0]
+            ahead, ahead_x = next_ref[0, 0], next_u_ref[0, 0, 0] * next_ref[0, 0]
         if x > 0:
             behind, behind_x = field_ref[x - 1], vel_ref[0, x - 1] * field_ref[x - 1]
         else:
-            behind, behind_x = prev_ref[0, nx - 1], prev_u_ref[0, nx - 1] * prev_ref[0, nx - 1]
+            behind, behind_x = prev_ref[0, nx - 1], prev_u_ref[0, 0, nx - 1] * prev_ref[0, nx - 1]
         flux_y = vel_ref[1, x] * f
         flux_z = vel_ref[2, x] * f
         advect = 0.5 * (ahead_x - behind_x)
@@ -129,7 +129,7 @@
 
     field = adjoint[0]
     velocity = base_flow[:, 0]
-    prev, nxt = neighbours((adjoint, base_flow[0]), "space")
+    prev, nxt = neighbours((adjoint, base_flow), "space")
     kept, walls = stencil(pulse, field, velocity, source[0], prev, nxt)
 
     onehot = (actuator[:, :, None] == jnp.arange(NACT, dtype=jnp.int32)[None, None, :]).astype(

time: 39.3 us -> 38.9 us (0.990)
  local copies, waits for them, and re-layouts: 3.37 us -> 2.61 us
    squeeze x1 -> x0, local copies, waits for them, and re-layouts: 0.97 us -> none  [on_device(): prev, nxt = neighbours((adjoint, base_flow[0]), 'space')]
    ppermute x1, waiting for transfers between devices: 0.97 us -> 0.01 us  [butterfly_sum(): x = x + lax.ppermute(x, axis, [(i, i ^ bit) for i in range(groups)])]
    ppermute x2, waiting for transfers between devices: 0.01 us -> 0.54 us  [neighbours(): prev = lax.ppermute(slab, axis, up)]
    unnamed x10 -> x12, local copies, waits for them, and re-layouts: 1.83 us -> 2.04 us
  transfers between devices with their start and end apart: 4 -> 4, of which waited for: 2 -> 2; matrix products, arithmetic and copies ran while one was open for 4% -> 4% of each run, Pallas kernels for 7% -> 8%
where the time goes in v10:
time: 38.9 us; the launch traced here: 38.5 us
  blocking collectives  15.2 us (39%)
  starting transfers between devices  9.06 us (23%)
  waiting for transfers between devices  4.14 us (11%)
  Pallas kernels  2.99 us (8%)
  local copies, waits for them, and re-layouts  2.61 us (7%)
  other arithmetic  1.59 us (4%)
  matrix products  1.57 us (4%)
  between operations  1.37 us (4%)
    all_to_all x1, blocking collectives, on_device(): incoming = lax.all_to_all(outgoing, 'tm', 0, 0, tiled=True)  15.2 us
    all_to_all x1, starting transfers between devices, on_device(): lax.all_to_all(adjoint.reshape(count, chunk, cz), 'tm', 0, 0, tiled=True)  8.03 us
    all_to_all x1, waiting for transfers between devices, on_device(): lax.all_to_all(adjoint.reshape(count, chunk, cz), 'tm', 0, 0, tiled=True)  3.6 us
    pallas_call x1, Pallas kernels, stencil(): pl.pallas_call(stencil_kernel, out_shape=(jax.ShapeDtypeStruct((nx, cy, c...  2.99 us
    unnamed x12, local copies, waits for them, and re-layouts  2.04 us
    dot_general x1, matrix products, on_device(): jnp.dot(walls.reshape(2, -1), onehot.reshape(-1, NACT), precision=lax.Pre...  1.07 us
  transfers between devices with their start and end apart: 4, of which 2 were waited for; matrix products, arithmetic and copies ran while one was open for 4% of the time, Pallas kernels for 8%

profile of v10, /device:TPU:0, one launch (start us, length us, event | category | flops | bytes accessed | tf_op | source)
XLA Modules:
  0.0 38.5 jit_solution(15521082304618800404)
XLA Ops:
  0.6 0.5 %collective-permute-start.1 = (f32[3,1,8,64,128]{4,3,2,1,0:T(8,128)}, f32[3,1,8,64,128]{4,3,2,1,0:T(8,128)S(1)}, u32[]{:S(2)}, u32[]{:S(2)}) collective-permute-start(f32[3,1,8,64,128]{4,3,2,1,0:T(8,128)} %param.6), channel_id=1, source_target_pairs={{0,1},{1,0},{2,3},{3,2},{4,5},{5,4},{6,7},{7,6},{8,9},{9,8},{10,11... | collective-permute-start | bytes 2359304 | tf_op jit(solution)/shard_map/ppermute | solution.py:52
  1.1 8.0 %all-to-all-start = ((f32[16,32,128]{2,1,0:T(8,128)}), f32[16,32,128]{2,1,0:T(8,128)S(1)}, u32[]{:S(2)}, u32[]{:S(2)}) async-start(f32[16,32,128]{2,1,0:T(8,128)} %bitcast.39), calls=%async_computation | async-start | bytes 524288 | tf_op jit(solution)/shard_map/all_to_all | solution.py:122
  9.2 0.3 collective-permute-start
  10.1 0.1 pad.8.clone
  10.2 0.1 pad.9.clone
  10.3 0.5 %collective-permute-done.prev_ref.next_ref = f32[1,8,64,128]{3,2,1,0:T(8,128)S(1)} collective-permute-done((f32[1,8,64,128]{3,2,1,0:T(8,128)S(1)}, f32[1,8,64,128]{3,2,1,0:T(8,128)S(1)}, u32[]{:S(2)}, u32[]{:S(2)}) %collective-permute-start) | collective-permute-done | bytes 262176 | tf_op jit(solution)/shard_map/ppermute | solution.py:52
  10.8 0.7 %copy-done.1 = f32[1,8,64,128]{3,2,1,0:T(8,128)} copy-done((f32[1,8,64,128]{3,2,1,0:T(8,128)}, f32[1,8,64,128]{3,2,1,0:T(8,128)S(1)}, u32[]{:S(2)}) %copy-start.1) | copy-done | bytes 262168
  11.5 0.3 copy-done
  11.8 3.0 %shard_map.68 = (f32[8,64,128]{2,1,0:T(8,128)}, f32[2,8,128]{2,1,0:T(8,128)}) custom-call(f32[1]{0:T(128)S(6)} %copy.34.pulse_ref, f32[8,64,128]{2,1,0:T(8,128)} %bitcast.40, f32[3,8,64,128]{3,2,1,0:T(8,128)} %bitcast.43, f32[8,64,128]{2,1,0:T(8,128)} %bitcast.44, f32[1,8,64,128]{3,2,1,0:T(8,128)} %copy-done.1, f32[3,1,8,64,128]{4,3,2,1,0:T(8,128)} %copy-done, ...), custom_call_target="tpu_custom_call" | custom-call | tf_op jit(solution)/shard_map/pallas_call | solution.py:102
  14.8 1.1 %convolution_bitcast_fusion = f32[2,128]{1,0:T(2,128)S(1)} fusion(s32[8,128]{1,0:T(8,128)S(1)} %copy-done.4, f32[2,8,128]{2,1,0:T(8,128)} %get-tuple-element.7), kind=kOutput, calls=%fused_computation | convolution fusion | flops 3276800 | bytes 13312 | tf_op jit(solution)/shard_map/dot_general | solution.py:138
  15.8 0.3 collective-permute-start.2
  16.1 3.6 %all-to-all-done = f32[16,32,128]{2,1,0:T(8,128)S(1)} async-done(((f32[16,32,128]{2,1,0:T(8,128)}), f32[16,32,128]{2,1,0:T(8,128)S(1)}, u32[]{:S(2)}, u32[]{:S(2)}) %all-to-all-start) | async-done | bytes 262176 | tf_op jit(solution)/shard_map/all_to_all | solution.py:122
  19.7 0.5 %fusion = f32[16,32,128]{2,0,1:T(8,128)S(1)} fusion(f32[2,8,32,128]{3,2,1,0:T(8,128)S(1)} %bitcast.42), kind=kOutput, calls=%fused_computation.4 | convolution fusion | flops 12589312 | bytes 524288 | tf_op jit(solution)/shard_map/ji,jp->ip/dot_general | solution.py:123
  20.2 0.1 reshape.30
  20.3 0.1 fusion.5
  20.4 0.1 copy.18
  20.6 15.2 %all_to_all.10 = f32[16,40,128]{2,1,0:T(8,128)S(1)} all-to-all(f32[16,40,128]{2,1,0:T(8,128)S(1)} %copy.18), channel_id=1, replica_groups=mesh['tm'=16,'space'=2] {'tm'}, dimensions={0} | all-to-all | bytes 655360 | tf_op jit(solution)/shard_map/all_to_all | solution.py:152
  35.8 0.1 copy.21
  35.9 0.2 slice_reduce_fusion
  36.1 0.1 multiply_reduce_fusion
  36.2 0.1 fusion.17
  36.3 0.5 %broadcast_multiply_fusion = f32[8]{0:T(128)} fusion(f32[8]{0:T(128)S(1)} %fusion.17), kind=kLoop, calls=%fused_computation.35 | loop fusion | flops 8 | bytes 64 | tf_op jit(solution)/shard_map/div | solution.py:157
  36.9 0.9 %copy-done.3 = f32[8,64,128]{2,1,0:T(8,128)S(1)} copy-done((f32[8,64,128]{2,1,0:T(8,128)S(1)}, f32[8,64,128]{2,1,0:T(8,128)}, u32[]{:S(2)}) %copy-start.3) | copy-done | bytes 262168
  37.8 0.7 %fusion.3 = f32[1,8,64,128]{3,2,1,0:T(8,128)} fusion(f32[8,64,128]{2,1,0:T(8,128)S(1)} %copy-done.3, f32[8,64,128]{2,1,0:T(8,128)S(1)} %bitcast.41), kind=kLoop, calls=%fused_computation.8 | loop fusion | flops 65536 | bytes 786432 | tf_op jit(solution)/shard_map/broadcast_in_dim | solution.py:159
  (16 shorter events, 0.2 us)
Async XLA Ops:
  0.6 10.2 %collective-permute-start.1 = (f32[3,1,8,64,128]{4,3,2,1,0:T(8,128)}, f32[3,1,8,64,128]{4,3,2,1,0:T(8,128)S(1)}, u32[]{:S(2)}, u32[]{:S(2)}) collective-permute-start(f32[3,1,8,64,128]{4,3,2,1,0:T(8,128)} %param.6), channel_id=1, source_target_pairs={{0,1},{1,0},{2,3},{3,2},{4,5},{5,4},{6,7},{7,6},{8,9},{9,8},{10,11... | collective-permute-start | bytes 2359304 | tf_op jit(solution)/shard_map/ppermute | solution.py:52
  1.1 8.0 %copy-start.2 = (f32[1,8,64,128]{3,2,1,0:T(8,128)S(1)}, f32[1,8,64,128]{3,2,1,0:T(8,128)}, u32[]{:S(2)}) copy-start(f32[1,8,64,128]{3,2,1,0:T(8,128)} %param.5) | copy-start | bytes 786436
  1.1 18.5 %all-to-all-start = ((f32[16,32,128]{2,1,0:T(8,128)}), f32[16,32,128]{2,1,0:T(8,128)S(1)}, u32[]{:S(2)}, u32[]{:S(2)}) async-start(f32[16,32,128]{2,1,0:T(8,128)} %bitcast.39), calls=%async_computation | async-start | bytes 524288 | tf_op jit(solution)/shard_map/all_to_all | solution.py:122
  9.2 1.6 %collective-permute-start = (f32[1,8,64,128]{3,2,1,0:T(8,128)S(1)}, f32[1,8,64,128]{3,2,1,0:T(8,128)S(1)}, u32[]{:S(2)}, u32[]{:S(2)}) collective-permute-start(f32[1,8,64,128]{3,2,1,0:T(8,128)S(1)} %copy-done.2), channel_id=1, source_target_pairs={{0,1},{1,0},{2,3},{3,2},{4,5},{5,4},{6,7},{7,6},{8,9},{9,8},{10,11... | collective-permute-start | bytes 786440 | tf_op jit(solution)/shard_map/ppermute | solution.py:52
  10.8 0.7 %copy-start.1 = (f32[1,8,64,128]{3,2,1,0:T(8,128)}, f32[1,8,64,128]{3,2,1,0:T(8,128)S(1)}, u32[]{:S(2)}) copy-start(f32[1,8,64,128]{3,2,1,0:T(8,128)S(1)} %collective-permute-done.prev_ref.next_ref) | copy-start | bytes 786436
  10.8 1.0 %copy-start = (f32[3,1,8,64,128]{4,3,2,1,0:T(8,128)}, f32[3,1,8,64,128]{4,3,2,1,0:T(8,128)S(1)}, u32[]{:S(2)}) copy-start(f32[3,1,8,64,128]{4,3,2,1,0:T(8,128)S(1)} %collective-permute-done.1.prev_u_ref.next_u_ref) | copy-start | bytes 2359300
  11.8 3.0 %copy-start.4 = (s32[8,128]{1,0:T(8,128)S(1)}, s32[8,128]{1,0:T(8,128)}, u32[]{:S(2)}) copy-start(s32[8,128]{1,0:T(8,128)} %param.9) | copy-start | bytes 12292
  15.8 4.4 %collective-permute-start.2 = (f32[2,128]{1,0:T(2,128)S(1)}, f32[2,128]{1,0:T(2,128)S(1)}, u32[]{:S(2)}, u32[]{:S(2)}) collective-permute-start(f32[2,128]{1,0:T(2,128)S(1)} %convolution_bitcast_fusion), channel_id=1, source_target_pairs={{0,1},{1,0},{2,3},{3,2},{4,5},{5,4},{6,7},{7,6},{8,9},{9,8},{10,11... | collective-permute-start | bytes 3080 | tf_op jit(solution)/shard_map/ppermute | solution.py:43
  36.9 0.9 %copy-start.3 = (f32[8,64,128]{2,1,0:T(8,128)S(1)}, f32[8,64,128]{2,1,0:T(8,128)}, u32[]{:S(2)}) copy-start(f32[8,64,128]{2,1,0:T(8,128)} %get-tuple-element.8) | copy-start | bytes 786436

commit v11 on v10

--- a/solution.py
+++ b/solution.py
@@ -142,7 +142,8 @@
         preferred_element_type=jnp.float32,
     )
     terms = butterfly_sum(terms, "space")
-    slices = jnp.transpose(terms.reshape(2, count, share), (1, 0, 2))
+    scales = jnp.array([1.0, -pseudo_step * omega_rate], jnp.float32)[:, None] / total
+    slices = jnp.transpose((terms * scales).reshape(2, count, share), (1, 0, 2))
     slices = jnp.pad(slices, ((0, 0), (0, 0), (0, cz - share)))
     pulse_row = jnp.broadcast_to(pulse.reshape(1, 1, 1), (count, 1, cz))
     grad_rows = jnp.concatenate([slices, pulse_row, jnp.zeros((count, pad - 3, cz), jnp.float32)], axis=1)
@@ -153,8 +154,7 @@
     scaled_term = incoming[:, :chunk].reshape(nx, cy, cz)
     tile = incoming[:, chunk : chunk + 3, :share]
     weights = jnp.sum(dmat * tile[None, :, 2, 0], axis=1)
-    parts = tile[:, 0] - pseudo_step * omega_rate * weights[:, None] * tile[:, 1]
-    gradient = jnp.sum(parts, axis=0) / total
+    gradient = jnp.sum(tile[:, 0] + weights[:, None] * tile[:, 1], axis=0)
     updated = kept + scaled_term
     return (updated[None], gradient)
 

time: 38.9 us -> 39 us (level)
    div x1 -> x0, other arithmetic: 0.53 us -> none  [on_device(): gradient = jnp.sum(parts, axis=0) / total]
    reduce_sum x1, other arithmetic: 0.12 us -> 0.63 us  [on_device(): gradient = jnp.sum(tile[:, 0] + weights[:, None] * tile[:, 1], axis=0)]
    unnamed x12 -> x14, local copies, waits for them, and re-layouts: 2.04 us -> 2.17 us
where the time goes in v11:
time: 39 us; the launch traced here: 38.6 us
  blocking collectives  15.1 us (39%)
  starting transfers between devices  9.06 us (23%)
  waiting for transfers between devices  4.13 us (11%)
  Pallas kernels  3 us (8%)
  local copies, waits for them, and re-layouts  2.75 us (7%)
  other arithmetic  1.63 us (4%)
  matrix products  1.57 us (4%)
  between operations  1.37 us (4%)
    all_to_all x1, blocking collectives, on_device(): incoming = lax.all_to_all(outgoing, 'tm', 0, 0, tiled=True)  15.1 us
    all_to_all x1, starting transfers between devices, on_device(): lax.all_to_all(adjoint.reshape(count, chunk, cz), 'tm', 0, 0, tiled=True)  8.03 us
    all_to_all x1, waiting for transfers between devices, on_device(): lax.all_to_all(adjoint.reshape(count, chunk, cz), 'tm', 0, 0, tiled=True)  3.59 us
    pallas_call x1, Pallas kernels, stencil(): pl.pallas_call(stencil_kernel, out_shape=(jax.ShapeDtypeStruct((nx, cy, c...  3 us
    unnamed x14, local copies, waits for them, and re-layouts  2.17 us
    dot_general x1, matrix products, on_device(): jnp.dot(walls.reshape(2, -1), onehot.reshape(-1, NACT), precision=lax.Pre...  1.07 us
  transfers between devices with their start and end apart: 4, of which 2 were waited for; matrix products, arithmetic and copies ran while one was open for 4% of the time, Pallas kernels for 8%

profile of v11, /device:TPU:0, one launch (start us, length us, event | category | flops | bytes accessed | tf_op | source)
XLA Modules:
  0.0 38.6 jit_solution(4413658653012670592)
XLA Ops:
  0.6 0.5 %collective-permute-start.1 = (f32[3,1,8,64,128]{4,3,2,1,0:T(8,128)}, f32[3,1,8,64,128]{4,3,2,1,0:T(8,128)S(1)}, u32[]{:S(2)}, u32[]{:S(2)}) collective-permute-start(f32[3,1,8,64,128]{4,3,2,1,0:T(8,128)} %param.7), channel_id=1, source_target_pairs={{0,1},{1,0},{2,3},{3,2},{4,5},{5,4},{6,7},{7,6},{8,9},{9,8},{10,11... | collective-permute-start | bytes 2359304 | tf_op jit(solution)/shard_map/ppermute | solution.py:52
  1.1 8.0 %all-to-all-start = ((f32[16,32,128]{2,1,0:T(8,128)}), f32[16,32,128]{2,1,0:T(8,128)S(1)}, u32[]{:S(2)}, u32[]{:S(2)}) async-start(f32[16,32,128]{2,1,0:T(8,128)} %bitcast.39), calls=%async_computation | async-start | bytes 524288 | tf_op jit(solution)/shard_map/all_to_all | solution.py:122
  9.2 0.3 collective-permute-start
  10.1 0.1 pad.8.clone
  10.2 0.1 pad.9.clone
  10.3 0.5 %collective-permute-done.prev_ref.next_ref = f32[1,8,64,128]{3,2,1,0:T(8,128)S(1)} collective-permute-done((f32[1,8,64,128]{3,2,1,0:T(8,128)S(1)}, f32[1,8,64,128]{3,2,1,0:T(8,128)S(1)}, u32[]{:S(2)}, u32[]{:S(2)}) %collective-permute-start) | collective-permute-done | bytes 262176 | tf_op jit(solution)/shard_map/ppermute | solution.py:52
  10.8 0.7 %copy-done.1 = f32[1,8,64,128]{3,2,1,0:T(8,128)} copy-done((f32[1,8,64,128]{3,2,1,0:T(8,128)}, f32[1,8,64,128]{3,2,1,0:T(8,128)S(1)}, u32[]{:S(2)}) %copy-start.1) | copy-done | bytes 262168
  11.5 0.3 copy-done
  11.8 3.0 %shard_map.77 = (f32[8,64,128]{2,1,0:T(8,128)}, f32[2,8,128]{2,1,0:T(8,128)}) custom-call(f32[1]{0:T(128)S(6)} %copy.35.pulse_ref, f32[8,64,128]{2,1,0:T(8,128)} %bitcast.40, f32[3,8,64,128]{3,2,1,0:T(8,128)} %bitcast.43, f32[8,64,128]{2,1,0:T(8,128)} %bitcast.44, f32[1,8,64,128]{3,2,1,0:T(8,128)} %copy-done.1, f32[3,1,8,64,128]{4,3,2,1,0:T(8,128)} %copy-done, ...), custom_call_target="tpu_custom_call" | custom-call | tf_op jit(solution)/shard_map/pallas_call | solution.py:102
  14.8 1.1 %convolution_bitcast_fusion = f32[2,128]{1,0:T(2,128)S(1)} fusion(s32[8,128]{1,0:T(8,128)S(1)} %copy-done.5, f32[2,8,128]{2,1,0:T(8,128)} %get-tuple-element.7), kind=kOutput, calls=%fused_computation | convolution fusion | flops 3276800 | bytes 13312 | tf_op jit(solution)/shard_map/dot_general | solution.py:138
  15.8 0.3 collective-permute-start.2
  16.1 3.6 %all-to-all-done = f32[16,32,128]{2,1,0:T(8,128)S(1)} async-done(((f32[16,32,128]{2,1,0:T(8,128)}), f32[16,32,128]{2,1,0:T(8,128)S(1)}, u32[]{:S(2)}, u32[]{:S(2)}) %all-to-all-start) | async-done | bytes 262176 | tf_op jit(solution)/shard_map/all_to_all | solution.py:122
  19.7 0.5 %fusion = f32[16,32,128]{2,0,1:T(8,128)S(1)} fusion(f32[2,8,32,128]{3,2,1,0:T(8,128)S(1)} %bitcast.42), kind=kOutput, calls=%fused_computation.4 | convolution fusion | flops 12589312 | bytes 524288 | tf_op jit(solution)/shard_map/ji,jp->ip/dot_general | solution.py:123
  20.2 0.1 copy-done.4
  20.3 0.1 add_multiply_fusion
  20.4 0.1 reshape.29
  20.5 0.1 fusion.5
  20.6 0.1 copy.19
  20.8 15.1 %all_to_all.10 = f32[16,40,128]{2,1,0:T(8,128)S(1)} all-to-all(f32[16,40,128]{2,1,0:T(8,128)S(1)} %copy.19), channel_id=1, replica_groups=mesh['tm'=16,'space'=2] {'tm'}, dimensions={0} | all-to-all | bytes 655360 | tf_op jit(solution)/shard_map/all_to_all | solution.py:153
  36.0 0.2 slice_reduce_fusion
  36.2 0.1 multiply_reduce_fusion
  36.3 0.9 %copy-done.3 = f32[8,64,128]{2,1,0:T(8,128)S(1)} copy-done((f32[8,64,128]{2,1,0:T(8,128)S(1)}, f32[8,64,128]{2,1,0:T(8,128)}, u32[]{:S(2)}) %copy-start.3) | copy-done | bytes 262168
  37.2 0.7 %fusion.3 = f32[1,8,64,128]{3,2,1,0:T(8,128)} fusion(f32[8,64,128]{2,1,0:T(8,128)S(1)} %copy-done.3, f32[8,64,128]{2,1,0:T(8,128)S(1)} %bitcast.41), kind=kLoop, calls=%fused_computation.8 | loop fusion | flops 65536 | bytes 786432 | tf_op jit(solution)/shard_map/broadcast_in_dim | solution.py:159
  38.0 0.6 %fusion.17 = f32[8]{0:T(128)} fusion(f32[16,1,8]{0,2,1:T(8,128)S(1)} %copy.23, f32[16,1,8]{0,2,1:T(8,128)S(1)} %copy.22, f32[16]{0:T(128)S(1)} %multiply_reduce_fusion), kind=kLoop, calls=%fused_computation.33 | loop fusion | flops 376 | bytes 1120 | tf_op jit(solution)/shard_map/reduce_sum | solution.py:157
  (16 shorter events, 0.2 us)
Async XLA Ops:
  0.6 10.2 %collective-permute-start.1 = (f32[3,1,8,64,128]{4,3,2,1,0:T(8,128)}, f32[3,1,8,64,128]{4,3,2,1,0:T(8,128)S(1)}, u32[]{:S(2)}, u32[]{:S(2)}) collective-permute-start(f32[3,1,8,64,128]{4,3,2,1,0:T(8,128)} %param.7), channel_id=1, source_target_pairs={{0,1},{1,0},{2,3},{3,2},{4,5},{5,4},{6,7},{7,6},{8,9},{9,8},{10,11... | collective-permute-start | bytes 2359304 | tf_op jit(solution)/shard_map/ppermute | solution.py:52
  1.1 8.0 %copy-start.2 = (f32[1,8,64,128]{3,2,1,0:T(8,128)S(1)}, f32[1,8,64,128]{3,2,1,0:T(8,128)}, u32[]{:S(2)}) copy-start(f32[1,8,64,128]{3,2,1,0:T(8,128)} %param.6) | copy-start | bytes 786436
  1.1 18.5 %all-to-all-start = ((f32[16,32,128]{2,1,0:T(8,128)}), f32[16,32,128]{2,1,0:T(8,128)S(1)}, u32[]{:S(2)}, u32[]{:S(2)}) async-start(f32[16,32,128]{2,1,0:T(8,128)} %bitcast.39), calls=%async_computation | async-start | bytes 524288 | tf_op jit(solution)/shard_map/all_to_all | solution.py:122
  9.2 1.6 %collective-permute-start = (f32[1,8,64,128]{3,2,1,0:T(8,128)S(1)}, f32[1,8,64,128]{3,2,1,0:T(8,128)S(1)}, u32[]{:S(2)}, u32[]{:S(2)}) collective-permute-start(f32[1,8,64,128]{3,2,1,0:T(8,128)S(1)} %copy-done.2), channel_id=1, source_target_pairs={{0,1},{1,0},{2,3},{3,2},{4,5},{5,4},{6,7},{7,6},{8,9},{9,8},{10,11... | collective-permute-start | bytes 786440 | tf_op jit(solution)/shard_map/ppermute | solution.py:52
  10.8 0.7 %copy-start.1 = (f32[1,8,64,128]{3,2,1,0:T(8,128)}, f32[1,8,64,128]{3,2,1,0:T(8,128)S(1)}, u32[]{:S(2)}) copy-start(f32[1,8,64,128]{3,2,1,0:T(8,128)S(1)} %collective-permute-done.prev_ref.next_ref) | copy-start | bytes 786436
  10.8 1.0 %copy-start = (f32[3,1,8,64,128]{4,3,2,1,0:T(8,128)}, f32[3,1,8,64,128]{4,3,2,1,0:T(8,128)S(1)}, u32[]{:S(2)}) copy-start(f32[3,1,8,64,128]{4,3,2,1,0:T(8,128)S(1)} %collective-permute-done.1.prev_u_ref.next_u_ref) | copy-start | bytes 2359300
  11.8 3.0 %copy-start.5 = (s32[8,128]{1,0:T(8,128)S(1)}, s32[8,128]{1,0:T(8,128)}, u32[]{:S(2)}) copy-start(s32[8,128]{1,0:T(8,128)} %param.10) | copy-start | bytes 12292
  15.8 4.4 %collective-permute-start.2 = (f32[2,128]{1,0:T(2,128)S(1)}, f32[2,128]{1,0:T(2,128)S(1)}, u32[]{:S(2)}, u32[]{:S(2)}) collective-permute-start(f32[2,128]{1,0:T(2,128)S(1)} %convolution_bitcast_fusion), channel_id=1, source_target_pairs={{0,1},{1,0},{2,3},{3,2},{4,5},{5,4},{6,7},{7,6},{8,9},{9,8},{10,11... | collective-permute-start | bytes 3080 | tf_op jit(solution)/shard_map/ppermute | solution.py:43
  19.7 0.7 %copy-start.4 = (f32[2]{0:T(128)S(1)}, f32[2]{0:T(128)}, u32[]{:S(2)}) copy-start(f32[2]{0:T(128)} %constant.48) | copy-start | bytes 28
  36.3 1.0 %copy-start.3 = (f32[8,64,128]{2,1,0:T(8,128)S(1)}, f32[8,64,128]{2,1,0:T(8,128)}, u32[]{:S(2)}) copy-start(f32[8,64,128]{2,1,0:T(8,128)} %get-tuple-element.8) | copy-start | bytes 786436

commit v12 on v11

--- a/solution.py
+++ b/solution.py
@@ -55,7 +55,7 @@
     return prev, lax.ppermute(slab, axis, down)
 
 
-def stencil_kernel(pulse_ref, field_ref, vel_ref, src_ref, prev_ref, prev_u_ref, next_ref, next_u_ref, kept_ref, walls_ref):
+def kept_layers(pulse_ref, field_ref, vel_ref, src_ref, prev_ref, prev_u_ref, next_ref, next_u_ref):
     nx, cy, cz = field_ref.shape
     row = lax.broadcasted_iota(jnp.int32, (cy, cz), 0)
 
@@ -90,24 +90,49 @@
         beside = beside + wall_up(f) + wall_down(f)
         beside = beside + span_up(f) + span_down(f)
         operator = advect + viscosity * (beside - 6.0 * f) - reaction * f
-        kept = f + pseudo_step * (operator + src_ref[x])
-        kept_ref[x] = kept
+        yield x, f, f + pseudo_step * (operator + src_ref[x])
+
+
+def walls_kernel(*refs):
+    *ins, walls_ref = refs
+    pulse_ref = ins[0]
+    for x, f, kept in kept_layers(*ins):
         walls_ref[0, x : x + 1, :] = pulse_ref[0] * kept[0:1]
         walls_ref[1, x : x + 1, :] = f[0:1]
 
 
-def stencil(pulse, field, velocity, source, prev, nxt):
+def kept_kernel(*refs):
+    *ins, _, kept_ref = refs
+    for x, _, kept in kept_layers(*ins):
+        kept_ref[x] = kept
+
+
+def tile_spec(shape, rows):
+    block = shape[:-2] + (rows, shape[-1])
+    return pl.BlockSpec(block, lambda i: (0,) * len(shape))
+
+
+def wall_terms(pulse, field, velocity, source, prev, nxt):
+    nx, cy, cz = field.shape
+    operands = (field, velocity, source, *prev, *nxt)
+    return pl.pallas_call(
+        walls_kernel,
+        grid=(1,),
+        out_shape=jax.ShapeDtypeStruct((2, nx, cz), jnp.float32),
+        in_specs=[pl.BlockSpec(memory_space=pltpu.SMEM)] + [tile_spec(op.shape, 8) for op in operands],
+        out_specs=pl.BlockSpec((2, nx, cz), lambda i: (0, 0, 0)),
+    )(pulse, *operands)
+
+
+def kept_field(pulse, field, velocity, source, prev, nxt, after):
     nx, cy, cz = field.shape
     vmem = pl.BlockSpec(memory_space=pltpu.VMEM)
     return pl.pallas_call(
-        stencil_kernel,
-        out_shape=(
-            jax.ShapeDtypeStruct((nx, cy, cz), jnp.float32),
-            jax.ShapeDtypeStruct((2, nx, cz), jnp.float32),
-        ),
-        in_specs=[pl.BlockSpec(memory_space=pltpu.SMEM)] + [vmem] * 7,
-        out_specs=(vmem, vmem),
-    )(pulse, field, velocity, source, *prev, *nxt)
+        kept_kernel,
+        out_shape=jax.ShapeDtypeStruct((nx, cy, cz), jnp.float32),
+        in_specs=[pl.BlockSpec(memory_space=pltpu.SMEM)] + [vmem] * 7 + [pl.BlockSpec(memory_space=pl.ANY)],
+        out_specs=vmem,
+    )(pulse, field, velocity, source, *prev, *nxt, after)
 
 
 def on_device(adjoint, base_flow, source, pulse, actuator):
@@ -130,7 +155,8 @@
     field = adjoint[0]
     velocity = base_flow[:, 0]
     prev, nxt = neighbours((adjoint, base_flow), "space")
-    kept, walls = stencil(pulse, field, velocity, source[0], prev, nxt)
+    walls = wall_terms(pulse, field, velocity, source[0], prev, nxt)
+    kept = kept_field(pulse, field, velocity, source[0], prev, nxt, incoming)
 
     onehot = (actuator[:, :, None] == jnp.arange(NACT, dtype=jnp.int32)[None, None, :]).astype(
         jnp.float32
@@ -147,7 +173,6 @@
     slices = jnp.pad(slices, ((0, 0), (0, 0), (0, cz - share)))
     pulse_row = jnp.broadcast_to(pulse.reshape(1, 1, 1), (count, 1, cz))
     grad_rows = jnp.concatenate([slices, pulse_row, jnp.zeros((count, pad - 3, cz), jnp.float32)], axis=1)
-    kept, grad_rows = lax.optimization_barrier((kept, grad_rows))
 
     outgoing = jnp.concatenate([derived.reshape(count, chunk, cz), grad_rows], axis=1)
     incoming = lax.all_to_all(outgoing, "tm", 0, 0, tiled=True)

time: 39 us -> 39.2 us (level)
  blocking collectives: 15.1 us -> 0 us
  waiting for transfers between devices: 4.13 us -> 13.2 us
  starting transfers between devices: 9.06 us -> 12.6 us
  Pallas kernels: 3 us -> 4.83 us
  local copies, waits for them, and re-layouts: 2.75 us -> 3.52 us
    all_to_all x1 -> x0, blocking collectives: 15.1 us -> none  [on_device(): incoming = lax.all_to_all(outgoing, 'tm', 0, 0, tiled=True)]
    all_to_all x0 -> x1, waiting for transfers between devices: none -> 7.88 us  [on_device(): incoming = lax.all_to_all(outgoing, 'tm', 0, 0, tiled=True)]
    all_to_all x0 -> x1, starting transfers between devices: none -> 3.55 us  [on_device(): incoming = lax.all_to_all(outgoing, 'tm', 0, 0, tiled=True)]
    pallas_call x1 -> x2, Pallas kernels: 3 us -> 4.83 us  [the longest x1 3.05 us: kept_field(): pl.pallas_call(kept_kernel, out_shape=jax.ShapeDtypeStruct((nx, cy, cz),...]
    all_to_all x1, waiting for transfers between devices: 3.59 us -> 4.81 us  [on_device(): lax.all_to_all(adjoint.reshape(count, chunk, cz), 'tm', 0, 0, tiled=True)]
    concatenate x1 -> x3, local copies, waits for them, and re-layouts: 0.11 us -> 0.97 us  [on_device(): jnp.concatenate([derived.reshape(count, chunk, cz), grad_rows], axis=1)]
    unnamed x14 -> x16, local copies, waits for them, and re-layouts: 2.17 us -> 2.23 us
  transfers between devices with their start and end apart: 4 -> 5, of which waited for: 2 -> 3; matrix products, arithmetic and copies ran while one was open for 4% -> 4% of each run, Pallas kernels for 8% -> 12%
where the time goes in v12:
time: 39.2 us; the launch traced here: 38.8 us
  waiting for transfers between devices  13.2 us (34%)
  starting transfers between devices  12.6 us (32%)
  Pallas kernels  4.83 us (12%)
  local copies, waits for them, and re-layouts  3.52 us (9%)
  other arithmetic  1.67 us (4%)
  matrix products  1.58 us (4%)
  between operations  1.36 us (3%)
    all_to_all x1, starting transfers between devices, on_device(): lax.all_to_all(adjoint.reshape(count, chunk, cz), 'tm', 0, 0, tiled=True)  8.03 us
    all_to_all x1, waiting for transfers between devices, on_device(): incoming = lax.all_to_all(outgoing, 'tm', 0, 0, tiled=True)  7.88 us
    all_to_all x1, waiting for transfers between devices, on_device(): lax.all_to_all(adjoint.reshape(count, chunk, cz), 'tm', 0, 0, tiled=True)  4.81 us
    all_to_all x1, starting transfers between devices, on_device(): incoming = lax.all_to_all(outgoing, 'tm', 0, 0, tiled=True)  3.55 us
    pallas_call x1, Pallas kernels, kept_field(): pl.pallas_call(kept_kernel, out_shape=jax.ShapeDtypeStruct((nx, cy, cz),...  3.05 us
    unnamed x16, local copies, waits for them, and re-layouts  2.23 us
    pallas_call x1, Pallas kernels, wall_terms(): pl.pallas_call(walls_kernel, grid=(1,), out_shape=jax.ShapeDtypeStruct((2...  1.77 us
    dot_general x1, matrix products, on_device(): jnp.dot(walls.reshape(2, -1), onehot.reshape(-1, NACT), precision=lax.Pre...  1.07 us
  transfers between devices with their start and end apart: 5, of which 3 were waited for; matrix products, arithmetic and copies ran while one was open for 4% of the time, Pallas kernels for 12%

profile of v12, /device:TPU:0, one launch (start us, length us, event | category | flops | bytes accessed | tf_op | source)
XLA Modules:
  0.0 38.8 jit_solution(15952426464455096338)
XLA Ops:
  0.6 0.5 %collective-permute-start.1 = (f32[3,1,8,64,128]{4,3,2,1,0:T(8,128)}, f32[3,1,8,64,128]{4,3,2,1,0:T(8,128)S(1)}, u32[]{:S(2)}, u32[]{:S(2)}) collective-permute-start(f32[3,1,8,64,128]{4,3,2,1,0:T(8,128)} %param.7), channel_id=1, source_target_pairs={{0,1},{1,0},{2,3},{3,2},{4,5},{5,4},{6,7},{7,6},{8,9},{9,8},{10,11... | collective-permute-start | bytes 2359304 | tf_op jit(solution)/shard_map/ppermute | solution.py:52
  1.1 8.0 %all-to-all-start = ((f32[16,32,128]{2,1,0:T(8,128)}), f32[16,32,128]{2,1,0:T(8,128)S(1)}, u32[]{:S(2)}, u32[]{:S(2)}) async-start(f32[16,32,128]{2,1,0:T(8,128)} %bitcast.41), calls=%async_computation | async-start | bytes 524288 | tf_op jit(solution)/shard_map/all_to_all | solution.py:147
  9.2 0.3 collective-permute-start
  10.1 0.1 pad.8.clone
  10.3 0.5 %collective-permute-done.refs_4_.refs_6_ = f32[1,8,64,128]{3,2,1,0:T(8,128)S(1)} collective-permute-done((f32[1,8,64,128]{3,2,1,0:T(8,128)S(1)}, f32[1,8,64,128]{3,2,1,0:T(8,128)S(1)}, u32[]{:S(2)}, u32[]{:S(2)}) %collective-permute-start) | collective-permute-done | bytes 262176 | tf_op jit(solution)/shard_map/ppermute | solution.py:52
  10.8 0.7 %copy-done.1 = f32[1,8,64,128]{3,2,1,0:T(8,128)} copy-done((f32[1,8,64,128]{3,2,1,0:T(8,128)}, f32[1,8,64,128]{3,2,1,0:T(8,128)S(1)}, u32[]{:S(2)}) %copy-start.1) | copy-done | bytes 262168
  11.5 0.3 copy-done
  11.8 1.8 %shard_map.78 = f32[2,8,128]{2,1,0:T(8,128)} custom-call(f32[1]{0:T(128)S(6)} %copy.35.refs_0_, f32[8,64,128]{2,1,0:T(8,128)} %bitcast.42, f32[3,8,64,128]{3,2,1,0:T(8,128)} %bitcast.39, f32[8,64,128]{2,1,0:T(8,128)} %bitcast.45, f32[1,8,64,128]{3,2,1,0:T(8,128)} %copy-done.1, f32[3,1,8,64,128]{4,3,2,1,0:T(8,128)} %copy-done, f32[1,8,64,128]{3,2,1,0:T(8,128)} %copy-done.1, ...), custom_call_target="tpu_custom_call" | custom-call | tf_op jit(solution)/shard_map/pallas_call | solution.py:118
  13.6 1.1 %convolution_bitcast_fusion = f32[2,128]{1,0:T(2,128)S(1)} fusion(s32[8,128]{1,0:T(8,128)S(1)} %copy-done.6, f32[2,8,128]{2,1,0:T(8,128)} %shard_map.78), kind=kOutput, calls=%fused_computation | convolution fusion | flops 3276800 | bytes 13312 | tf_op jit(solution)/shard_map/dot_general | solution.py:164
  14.6 0.3 collective-permute-start.2
  14.9 4.8 %all-to-all-done.refs_8_ = f32[16,32,128]{2,1,0:T(8,128)S(1)} async-done(((f32[16,32,128]{2,1,0:T(8,128)}), f32[16,32,128]{2,1,0:T(8,128)S(1)}, u32[]{:S(2)}, u32[]{:S(2)}) %all-to-all-start) | async-done | bytes 262176 | tf_op jit(solution)/shard_map/all_to_all | solution.py:147
  19.7 0.5 %fusion.3 = f32[16,32,128]{2,0,1:T(8,128)S(1)} fusion(f32[2,8,32,128]{3,2,1,0:T(8,128)S(1)} %bitcast.44), kind=kOutput, calls=%fused_computation.9 | convolution fusion | flops 12589312 | bytes 524288 | tf_op jit(solution)/shard_map/ji,jp->ip/dot_general | solution.py:148
  20.2 0.2 copy-done.3
  20.5 0.1 reshape.31
  20.6 0.2 fusion.1
  20.7 0.8 %copy.19 = f32[16,40,128]{2,1,0:T(8,128)} copy(f32[16,40,128]{2,0,1:T(8,128)S(1)} %fusion.1) | data formatting | bytes 655360 | tf_op jit(solution)/shard_map/concatenate | solution.py:177
  21.5 3.5 %all-to-all-start.1 = ((f32[16,40,128]{2,1,0:T(8,128)}), f32[16,40,128]{2,1,0:T(8,128)S(1)}, u32[]{:S(2)}, u32[]{:S(2)}) async-start(f32[16,40,128]{2,1,0:T(8,128)} %copy.19), calls=%async_computation.1 | async-start | bytes 655360 | tf_op jit(solution)/shard_map/all_to_all | solution.py:178
  25.1 3.1 %shard_map.77 = f32[8,64,128]{2,1,0:T(8,128)} custom-call(f32[1]{0:T(128)S(6)} %copy.35.refs_0_, f32[8,64,128]{2,1,0:T(8,128)} %bitcast.43, f32[3,8,64,128]{3,2,1,0:T(8,128)} %bitcast.40, f32[8,64,128]{2,1,0:T(8,128)} %bitcast.46, f32[1,8,64,128]{3,2,1,0:T(8,128)} %copy-done.1, f32[3,1,8,64,128]{4,3,2,1,0:T(8,128)} %copy-done, f32[1,8,64,128]{3,2,1,0:T(8,128)} %copy-done.1, ...), custom_call_target="tpu_custom_call" | custom-call | tf_op jit(solution)/shard_map/pallas_call | solution.py:130
  28.2 7.9 %all-to-all-done.1 = f32[16,40,128]{2,1,0:T(8,128)S(1)} async-done(((f32[16,40,128]{2,1,0:T(8,128)}), f32[16,40,128]{2,1,0:T(8,128)S(1)}, u32[]{:S(2)}, u32[]{:S(2)}) %all-to-all-start.1) | async-done | bytes 327712 | tf_op jit(solution)/shard_map/all_to_all | solution.py:178
  36.2 0.2 slice_reduce_fusion
  36.4 0.1 multiply_reduce_fusion
  36.5 0.9 %copy-done.4 = f32[8,64,128]{2,1,0:T(8,128)S(1)} copy-done((f32[8,64,128]{2,1,0:T(8,128)S(1)}, f32[8,64,128]{2,1,0:T(8,128)}, u32[]{:S(2)}) %copy-start.4) | copy-done | bytes 262168
  37.4 0.7 %fusion.6 = f32[1,8,64,128]{3,2,1,0:T(8,128)} fusion(f32[8,64,128]{2,1,0:T(8,128)S(1)} %copy-done.4, f32[8,64,128]{2,1,0:T(8,128)S(1)} %bitcast.47), kind=kLoop, calls=%fused_computation.13 | loop fusion | flops 65536 | bytes 786432 | tf_op jit(solution)/shard_map/broadcast_in_dim | solution.py:184
  38.2 0.6 %fusion.19 = f32[8]{0:T(128)} fusion(f32[16,1,8]{0,2,1:T(8,128)S(1)} %copy.23, f32[16,1,8]{0,2,1:T(8,128)S(1)} %copy.22, f32[16]{0:T(128)S(1)} %multiply_reduce_fusion), kind=kLoop, calls=%fused_computation.35 | loop fusion | flops 376 | bytes 1120 | tf_op jit(solution)/shard_map/reduce_sum | solution.py:182
  (19 shorter events, 0.3 us)
Async XLA Ops:
  0.6 10.2 %collective-permute-start.1 = (f32[3,1,8,64,128]{4,3,2,1,0:T(8,128)}, f32[3,1,8,64,128]{4,3,2,1,0:T(8,128)S(1)}, u32[]{:S(2)}, u32[]{:S(2)}) collective-permute-start(f32[3,1,8,64,128]{4,3,2,1,0:T(8,128)} %param.7), channel_id=1, source_target_pairs={{0,1},{1,0},{2,3},{3,2},{4,5},{5,4},{6,7},{7,6},{8,9},{9,8},{10,11... | collective-permute-start | bytes 2359304 | tf_op jit(solution)/shard_map/ppermute | solution.py:52
  1.1 8.0 %copy-start.2 = (f32[1,8,64,128]{3,2,1,0:T(8,128)S(1)}, f32[1,8,64,128]{3,2,1,0:T(8,128)}, u32[]{:S(2)}) copy-start(f32[1,8,64,128]{3,2,1,0:T(8,128)} %param.6) | copy-start | bytes 786436
  1.1 18.5 %all-to-all-start = ((f32[16,32,128]{2,1,0:T(8,128)}), f32[16,32,128]{2,1,0:T(8,128)S(1)}, u32[]{:S(2)}, u32[]{:S(2)}) async-start(f32[16,32,128]{2,1,0:T(8,128)} %bitcast.41), calls=%async_computation | async-start | bytes 524288 | tf_op jit(solution)/shard_map/all_to_all | solution.py:147
  9.2 1.6 %collective-permute-start = (f32[1,8,64,128]{3,2,1,0:T(8,128)S(1)}, f32[1,8,64,128]{3,2,1,0:T(8,128)S(1)}, u32[]{:S(2)}, u32[]{:S(2)}) collective-permute-start(f32[1,8,64,128]{3,2,1,0:T(8,128)S(1)} %copy-done.2), channel_id=1, source_target_pairs={{0,1},{1,0},{2,3},{3,2},{4,5},{5,4},{6,7},{7,6},{8,9},{9,8},{10,11... | collective-permute-start | bytes 786440 | tf_op jit(solution)/shard_map/ppermute | solution.py:52
  10.8 0.7 %copy-start.1 = (f32[1,8,64,128]{3,2,1,0:T(8,128)}, f32[1,8,64,128]{3,2,1,0:T(8,128)S(1)}, u32[]{:S(2)}) copy-start(f32[1,8,64,128]{3,2,1,0:T(8,128)S(1)} %collective-permute-done.refs_4_.refs_6_) | copy-start | bytes 786436
  10.8 1.0 %copy-start = (f32[3,1,8,64,128]{4,3,2,1,0:T(8,128)}, f32[3,1,8,64,128]{4,3,2,1,0:T(8,128)S(1)}, u32[]{:S(2)}) copy-start(f32[3,1,8,64,128]{4,3,2,1,0:T(8,128)S(1)} %collective-permute-done.1.refs_5_.refs_7_) | copy-start | bytes 2359300
  11.8 1.8 %copy-start.6 = (s32[8,128]{1,0:T(8,128)S(1)}, s32[8,128]{1,0:T(8,128)}, u32[]{:S(2)}) copy-start(s32[8,128]{1,0:T(8,128)} %param.10) | copy-start | bytes 12292
  14.6 5.8 %collective-permute-start.2 = (f32[2,128]{1,0:T(2,128)S(1)}, f32[2,128]{1,0:T(2,128)S(1)}, u32[]{:S(2)}, u32[]{:S(2)}) collective-permute-start(f32[2,128]{1,0:T(2,128)S(1)} %convolution_bitcast_fusion), channel_id=1, source_target_pairs={{0,1},{1,0},{2,3},{3,2},{4,5},{5,4},{6,7},{7,6},{8,9},{9,8},{10,11... | collective-permute-start | bytes 3080 | tf_op jit(solution)/shard_map/ppermute | solution.py:43
  19.7 0.7 %copy-start.3 = (f32[16,32,128]{2,1,0:T(8,128)}, f32[16,32,128]{2,1,0:T(8,128)S(1)}, u32[]{:S(2)}) copy-start(f32[16,32,128]{2,1,0:T(8,128)S(1)} %all-to-all-done.refs_8_) | copy-start | bytes 786436
  19.7 0.7 %copy-start.5 = (f32[2]{0:T(128)S(1)}, f32[2]{0:T(128)}, u32[]{:S(2)}) copy-start(f32[2]{0:T(128)} %constant.48) | copy-start | bytes 28
  21.5 14.5 %all-to-all-start.1 = ((f32[16,40,128]{2,1,0:T(8,128)}), f32[16,40,128]{2,1,0:T(8,128)S(1)}, u32[]{:S(2)}, u32[]{:S(2)}) async-start(f32[16,40,128]{2,1,0:T(8,128)} %copy.19), calls=%async_computation.1 | async-start | bytes 655360 | tf_op jit(solution)/shard_map/all_to_all | solution.py:178
  36.5 1.0 %copy-start.4 = (f32[8,64,128]{2,1,0:T(8,128)S(1)}, f32[8,64,128]{2,1,0:T(8,128)}, u32[]{:S(2)}) copy-start(f32[8,64,128]{2,1,0:T(8,128)} %shard_map.77) | copy-start | bytes 786436

commit v13 on v11

--- a/solution.py
+++ b/solution.py
@@ -80,7 +80,7 @@
         if x > 0:
             behind, behind_x = field_ref[x - 1], vel_ref[0, x - 1] * field_ref[x - 1]
         else:
-            behind, behind_x = prev_ref[0, nx - 1], prev_u_ref[0, 0, nx - 1] * prev_ref[0, nx - 1]
+            behind, behind_x = prev_ref[0, 0], prev_u_ref[0, 0, 0] * prev_ref[0, 0]
         flux_y = vel_ref[1, x] * f
         flux_z = vel_ref[2, x] * f
         advect = 0.5 * (ahead_x - behind_x)
@@ -96,17 +96,36 @@
         walls_ref[1, x : x + 1, :] = f[0:1]
 
 
+def whole(shape):
+    return pl.BlockSpec(shape, lambda i: (0,) * len(shape))
+
+
+def layer(shape, dim, at):
+    block = tuple(1 if d == dim else n for d, n in enumerate(shape))
+    return pl.BlockSpec(block, lambda i: tuple(at if d == dim else 0 for d in range(len(shape))))
+
+
 def stencil(pulse, field, velocity, source, prev, nxt):
     nx, cy, cz = field.shape
-    vmem = pl.BlockSpec(memory_space=pltpu.VMEM)
+    slab, flow = prev[0].shape, prev[1].shape
     return pl.pallas_call(
         stencil_kernel,
+        grid=(1,),
         out_shape=(
             jax.ShapeDtypeStruct((nx, cy, cz), jnp.float32),
             jax.ShapeDtypeStruct((2, nx, cz), jnp.float32),
         ),
-        in_specs=[pl.BlockSpec(memory_space=pltpu.SMEM)] + [vmem] * 7,
-        out_specs=(vmem, vmem),
+        in_specs=[
+            pl.BlockSpec(memory_space=pltpu.SMEM),
+            whole(field.shape),
+            whole(velocity.shape),
+            whole(source.shape),
+            layer(slab, 1, nx - 1),
+            layer(flow, 2, nx - 1),
+            layer(slab, 1, 0),
+            layer(flow, 2, 0),
+        ],
+        out_specs=(whole((nx, cy, cz)), whole((2, nx, cz))),
     )(pulse, field, velocity, source, *prev, *nxt)
 
 

time: 39 us -> 38.4 us (0.985)
  blocking collectives: 15.1 us -> 14.5 us
  waiting for transfers between devices: 4.13 us -> 4.7 us
  Pallas kernels: 3 us -> 2.43 us
    all_to_all x1, blocking collectives: 15.1 us -> 14.5 us  [on_device(): incoming = lax.all_to_all(outgoing, 'tm', 0, 0, tiled=True)]
    all_to_all x1, waiting for transfers between devices: 3.59 us -> 4.16 us  [on_device(): lax.all_to_all(adjoint.reshape(count, chunk, cz), 'tm', 0, 0, tiled=True)]
    pallas_call x1, Pallas kernels: 3 us -> 2.43 us  [stencil(): pl.pallas_call(stencil_kernel, grid=(1,), out_shape=(jax.ShapeDtypeStruct...]
  transfers between devices with their start and end apart: 4 -> 4, of which waited for: 2 -> 2; matrix products, arithmetic and copies ran while one was open for 4% -> 5% of each run, Pallas kernels for 8% -> 6%
where the time goes in v13:
time: 38.4 us; the launch traced here: 38 us
  blocking collectives  14.5 us (38%)
  starting transfers between devices  9.06 us (24%)
  waiting for transfers between devices  4.7 us (12%)
  local copies, waits for them, and re-layouts  2.75 us (7%)
  Pallas kernels  2.43 us (6%)
  other arithmetic  1.63 us (4%)
  matrix products  1.57 us (4%)
  between operations  1.37 us (4%)
    all_to_all x1, blocking collectives, on_device(): incoming = lax.all_to_all(outgoing, 'tm', 0, 0, tiled=True)  14.5 us
    all_to_all x1, starting transfers between devices, on_device(): lax.all_to_all(adjoint.reshape(count, chunk, cz), 'tm', 0, 0, tiled=True)  8.03 us
    all_to_all x1, waiting for transfers between devices, on_device(): lax.all_to_all(adjoint.reshape(count, chunk, cz), 'tm', 0, 0, tiled=True)  4.16 us
    pallas_call x1, Pallas kernels, stencil(): pl.pallas_call(stencil_kernel, grid=(1,), out_shape=(jax.ShapeDtypeStruct...  2.43 us
    unnamed x14, local copies, waits for them, and re-layouts  2.17 us
    dot_general x1, matrix products, on_device(): jnp.dot(walls.reshape(2, -1), onehot.reshape(-1, NACT), precision=lax.Pre...  1.07 us
    ppermute x2, starting transfers between devices, neighbours(): prev = lax.ppermute(slab, axis, up)  0.78 us
  transfers between devices with their start and end apart: 4, of which 2 were waited for; matrix products, arithmetic and copies ran while one was open for 5% of the time, Pallas kernels for 6%

profile of v13, /device:TPU:0, one launch (start us, length us, event | category | flops | bytes accessed | tf_op | source)
XLA Modules:
  0.0 38.0 jit_solution(17351813632444889804)
XLA Ops:
  0.6 0.5 %collective-permute-start.1 = (f32[3,1,8,64,128]{4,3,2,1,0:T(8,128)}, f32[3,1,8,64,128]{4,3,2,1,0:T(8,128)S(1)}, u32[]{:S(2)}, u32[]{:S(2)}) collective-permute-start(f32[3,1,8,64,128]{4,3,2,1,0:T(8,128)} %param.7), channel_id=1, source_target_pairs={{0,1},{1,0},{2,3},{3,2},{4,5},{5,4},{6,7},{7,6},{8,9},{9,8},{10,11... | collective-permute-start | bytes 2359304 | tf_op jit(solution)/shard_map/ppermute | solution.py:52
  1.1 8.0 %all-to-all-start = ((f32[16,32,128]{2,1,0:T(8,128)}), f32[16,32,128]{2,1,0:T(8,128)S(1)}, u32[]{:S(2)}, u32[]{:S(2)}) async-start(f32[16,32,128]{2,1,0:T(8,128)} %bitcast.39), calls=%async_computation | async-start | bytes 524288 | tf_op jit(solution)/shard_map/all_to_all | solution.py:141
  9.2 0.3 collective-permute-start
  10.1 0.1 pad.8.clone
  10.2 0.1 pad.9.clone
  10.3 0.5 %collective-permute-done.prev_ref.next_ref = f32[1,8,64,128]{3,2,1,0:T(8,128)S(1)} collective-permute-done((f32[1,8,64,128]{3,2,1,0:T(8,128)S(1)}, f32[1,8,64,128]{3,2,1,0:T(8,128)S(1)}, u32[]{:S(2)}, u32[]{:S(2)}) %collective-permute-start) | collective-permute-done | bytes 262176 | tf_op jit(solution)/shard_map/ppermute | solution.py:52
  10.8 0.7 %copy-done.1 = f32[1,8,64,128]{3,2,1,0:T(8,128)} copy-done((f32[1,8,64,128]{3,2,1,0:T(8,128)}, f32[1,8,64,128]{3,2,1,0:T(8,128)S(1)}, u32[]{:S(2)}) %copy-start.1) | copy-done | bytes 262168
  11.5 0.3 copy-done
  11.8 2.4 %shard_map.77 = (f32[8,64,128]{2,1,0:T(8,128)}, f32[2,8,128]{2,1,0:T(8,128)}) custom-call(f32[1]{0:T(128)S(6)} %copy.35.pulse_ref, f32[8,64,128]{2,1,0:T(8,128)} %bitcast.40, f32[3,8,64,128]{3,2,1,0:T(8,128)} %bitcast.43, f32[8,64,128]{2,1,0:T(8,128)} %bitcast.44, f32[1,8,64,128]{3,2,1,0:T(8,128)} %copy-done.1, f32[3,1,8,64,128]{4,3,2,1,0:T(8,128)} %copy-done, ...), custom_call_target="tpu_custom_call" | custom-call | tf_op jit(solution)/shard_map/pallas_call | solution.py:111
  14.2 1.1 %convolution_bitcast_fusion = f32[2,128]{1,0:T(2,128)S(1)} fusion(s32[8,128]{1,0:T(8,128)S(1)} %copy-done.5, f32[2,8,128]{2,1,0:T(8,128)} %get-tuple-element.7), kind=kOutput, calls=%fused_computation | convolution fusion | flops 3276800 | bytes 13312 | tf_op jit(solution)/shard_map/dot_general | solution.py:157
  15.3 0.3 collective-permute-start.2
  15.5 4.2 %all-to-all-done = f32[16,32,128]{2,1,0:T(8,128)S(1)} async-done(((f32[16,32,128]{2,1,0:T(8,128)}), f32[16,32,128]{2,1,0:T(8,128)S(1)}, u32[]{:S(2)}, u32[]{:S(2)}) %all-to-all-start) | async-done | bytes 262176 | tf_op jit(solution)/shard_map/all_to_all | solution.py:141
  19.7 0.5 %fusion = f32[16,32,128]{2,0,1:T(8,128)S(1)} fusion(f32[2,8,32,128]{3,2,1,0:T(8,128)S(1)} %bitcast.42), kind=kOutput, calls=%fused_computation.4 | convolution fusion | flops 12589312 | bytes 524288 | tf_op jit(solution)/shard_map/ji,jp->ip/dot_general | solution.py:142
  20.2 0.1 copy-done.4
  20.3 0.1 add_multiply_fusion
  20.4 0.1 reshape.29
  20.5 0.1 fusion.5
  20.6 0.1 copy.19
  20.8 14.5 %all_to_all.10 = f32[16,40,128]{2,1,0:T(8,128)S(1)} all-to-all(f32[16,40,128]{2,1,0:T(8,128)S(1)} %copy.19), channel_id=1, replica_groups=mesh['tm'=16,'space'=2] {'tm'}, dimensions={0} | all-to-all | bytes 655360 | tf_op jit(solution)/shard_map/all_to_all | solution.py:172
  35.4 0.2 slice_reduce_fusion
  35.6 0.1 multiply_reduce_fusion
  35.7 0.9 %copy-done.3 = f32[8,64,128]{2,1,0:T(8,128)S(1)} copy-done((f32[8,64,128]{2,1,0:T(8,128)S(1)}, f32[8,64,128]{2,1,0:T(8,128)}, u32[]{:S(2)}) %copy-start.3) | copy-done | bytes 262168
  36.7 0.7 %fusion.3 = f32[1,8,64,128]{3,2,1,0:T(8,128)} fusion(f32[8,64,128]{2,1,0:T(8,128)S(1)} %copy-done.3, f32[8,64,128]{2,1,0:T(8,128)S(1)} %bitcast.41), kind=kLoop, calls=%fused_computation.8 | loop fusion | flops 65536 | bytes 786432 | tf_op jit(solution)/shard_map/broadcast_in_dim | solution.py:178
  37.4 0.6 %fusion.17 = f32[8]{0:T(128)} fusion(f32[16,1,8]{0,2,1:T(8,128)S(1)} %copy.23, f32[16,1,8]{0,2,1:T(8,128)S(1)} %copy.22, f32[16]{0:T(128)S(1)} %multiply_reduce_fusion), kind=kLoop, calls=%fused_computation.33 | loop fusion | flops 376 | bytes 1120 | tf_op jit(solution)/shard_map/reduce_sum | solution.py:176
  (16 shorter events, 0.2 us)
Async XLA Ops:
  0.6 10.2 %collective-permute-start.1 = (f32[3,1,8,64,128]{4,3,2,1,0:T(8,128)}, f32[3,1,8,64,128]{4,3,2,1,0:T(8,128)S(1)}, u32[]{:S(2)}, u32[]{:S(2)}) collective-permute-start(f32[3,1,8,64,128]{4,3,2,1,0:T(8,128)} %param.7), channel_id=1, source_target_pairs={{0,1},{1,0},{2,3},{3,2},{4,5},{5,4},{6,7},{7,6},{8,9},{9,8},{10,11... | collective-permute-start | bytes 2359304 | tf_op jit(solution)/shard_map/ppermute | solution.py:52
  1.1 8.0 %copy-start.2 = (f32[1,8,64,128]{3,2,1,0:T(8,128)S(1)}, f32[1,8,64,128]{3,2,1,0:T(8,128)}, u32[]{:S(2)}) copy-start(f32[1,8,64,128]{3,2,1,0:T(8,128)} %param.6) | copy-start | bytes 786436
  1.1 18.5 %all-to-all-start = ((f32[16,32,128]{2,1,0:T(8,128)}), f32[16,32,128]{2,1,0:T(8,128)S(1)}, u32[]{:S(2)}, u32[]{:S(2)}) async-start(f32[16,32,128]{2,1,0:T(8,128)} %bitcast.39), calls=%async_computation | async-start | bytes 524288 | tf_op jit(solution)/shard_map/all_to_all | solution.py:141
  9.2 1.6 %collective-permute-start = (f32[1,8,64,128]{3,2,1,0:T(8,128)S(1)}, f32[1,8,64,128]{3,2,1,0:T(8,128)S(1)}, u32[]{:S(2)}, u32[]{:S(2)}) collective-permute-start(f32[1,8,64,128]{3,2,1,0:T(8,128)S(1)} %copy-done.2), channel_id=1, source_target_pairs={{0,1},{1,0},{2,3},{3,2},{4,5},{5,4},{6,7},{7,6},{8,9},{9,8},{10,11... | collective-permute-start | bytes 786440 | tf_op jit(solution)/shard_map/ppermute | solution.py:52
  10.8 0.7 %copy-start.1 = (f32[1,8,64,128]{3,2,1,0:T(8,128)}, f32[1,8,64,128]{3,2,1,0:T(8,128)S(1)}, u32[]{:S(2)}) copy-start(f32[1,8,64,128]{3,2,1,0:T(8,128)S(1)} %collective-permute-done.prev_ref.next_ref) | copy-start | bytes 786436
  10.8 1.0 %copy-start = (f32[3,1,8,64,128]{4,3,2,1,0:T(8,128)}, f32[3,1,8,64,128]{4,3,2,1,0:T(8,128)S(1)}, u32[]{:S(2)}) copy-start(f32[3,1,8,64,128]{4,3,2,1,0:T(8,128)S(1)} %collective-permute-done.1.prev_u_ref.next_u_ref) | copy-start | bytes 2359300
  11.8 2.4 %copy-start.5 = (s32[8,128]{1,0:T(8,128)S(1)}, s32[8,128]{1,0:T(8,128)}, u32[]{:S(2)}) copy-start(s32[8,128]{1,0:T(8,128)} %param.10) | copy-start | bytes 12292
  15.3 4.9 %collective-permute-start.2 = (f32[2,128]{1,0:T(2,128)S(1)}, f32[2,128]{1,0:T(2,128)S(1)}, u32[]{:S(2)}, u32[]{:S(2)}) collective-permute-start(f32[2,128]{1,0:T(2,128)S(1)} %convolution_bitcast_fusion), channel_id=1, source_target_pairs={{0,1},{1,0},{2,3},{3,2},{4,5},{5,4},{6,7},{7,6},{8,9},{9,8},{10,11... | collective-permute-start | bytes 3080 | tf_op jit(solution)/shard_map/ppermute | solution.py:43
  19.7 0.7 %copy-start.4 = (f32[2]{0:T(128)S(1)}, f32[2]{0:T(128)}, u32[]{:S(2)}) copy-start(f32[2]{0:T(128)} %constant.48) | copy-start | bytes 28
  35.7 1.0 %copy-start.3 = (f32[8,64,128]{2,1,0:T(8,128)S(1)}, f32[8,64,128]{2,1,0:T(8,128)}, u32[]{:S(2)}) copy-start(f32[8,64,128]{2,1,0:T(8,128)} %get-tuple-element.8) | copy-start | bytes 786436

commit v14 on v13

--- a/solution.py
+++ b/solution.py
@@ -139,12 +139,6 @@
     dmat = spectral_matrix(total)
 
     incoming = lax.all_to_all(adjoint.reshape(count, chunk, cz), "tm", 0, 0, tiled=True)
-    derived = jnp.einsum(
-        "ji,jp->ip",
-        (-pseudo_step * omega_rate) * dmat,
-        incoming.reshape(total, chunk * cz),
-        precision=lax.Precision.HIGHEST,
-    )
 
     field = adjoint[0]
     velocity = base_flow[:, 0]
@@ -166,9 +160,15 @@
     slices = jnp.pad(slices, ((0, 0), (0, 0), (0, cz - share)))
     pulse_row = jnp.broadcast_to(pulse.reshape(1, 1, 1), (count, 1, cz))
     grad_rows = jnp.concatenate([slices, pulse_row, jnp.zeros((count, pad - 3, cz), jnp.float32)], axis=1)
-    kept, grad_rows = lax.optimization_barrier((kept, grad_rows))
+    kept, grad_rows, incoming = lax.optimization_barrier((kept, grad_rows, incoming))
+    derived = jnp.einsum(
+        "ji,jrc->irc",
+        (-pseudo_step * omega_rate) * dmat,
+        incoming,
+        precision=lax.Precision.HIGHEST,
+    )
 
-    outgoing = jnp.concatenate([derived.reshape(count, chunk, cz), grad_rows], axis=1)
+    outgoing = jnp.concatenate([derived, grad_rows], axis=1)
     incoming = lax.all_to_all(outgoing, "tm", 0, 0, tiled=True)
     scaled_term = incoming[:, :chunk].reshape(nx, cy, cz)
     tile = incoming[:, chunk : chunk + 3, :share]

time: 38.4 us -> 38.3 us (level)
  blocking collectives: 14.5 us -> 14.9 us
    ppermute x1, waiting for transfers between devices: 0.01 us -> 0.97 us  [butterfly_sum(): x = x + lax.ppermute(x, axis, [(i, i ^ bit) for i in range(groups)])]
    all_to_all x1, waiting for transfers between devices: 4.16 us -> 3.52 us  [on_device(): lax.all_to_all(adjoint.reshape(count, chunk, cz), 'tm', 0, 0, tiled=True)]
    ppermute x2, waiting for transfers between devices: 0.54 us -> 0.01 us  [neighbours(): prev = lax.ppermute(slab, axis, up)]
    unnamed x14 -> x12, local copies, waits for them, and re-layouts: 2.17 us -> 2.02 us
  transfers between devices with their start and end apart: 4 -> 4, of which waited for: 2 -> 2; matrix products, arithmetic and copies ran while one was open for 5% -> 4% of each run, Pallas kernels for 6% -> 6%
where the time goes in v14:
time: 38.3 us; the launch traced here: 37.9 us
  blocking collectives  14.9 us (39%)
  starting transfers between devices  8.96 us (23%)
  waiting for transfers between devices  4.5 us (12%)
  local copies, waits for them, and re-layouts  2.59 us (7%)
  Pallas kernels  2.42 us (6%)
  other arithmetic  1.63 us (4%)
  matrix products  1.58 us (4%)
  between operations  1.39 us (4%)
    all_to_all x1, blocking collectives, on_device(): incoming = lax.all_to_all(outgoing, 'tm', 0, 0, tiled=True)  14.9 us
    all_to_all x1, starting transfers between devices, on_device(): lax.all_to_all(adjoint.reshape(count, chunk, cz), 'tm', 0, 0, tiled=True)  8.29 us
    all_to_all x1, waiting for transfers between devices, on_device(): lax.all_to_all(adjoint.reshape(count, chunk, cz), 'tm', 0, 0, tiled=True)  3.52 us
    pallas_call x1, Pallas kernels, stencil(): pl.pallas_call(stencil_kernel, grid=(1,), out_shape=(jax.ShapeDtypeStruct...  2.42 us
    unnamed x12, local copies, waits for them, and re-layouts  2.02 us
    dot_general x1, matrix products, on_device(): jnp.dot(walls.reshape(2, -1), onehot.reshape(-1, NACT), precision=lax.Pre...  1.07 us
    ppermute x1, waiting for transfers between devices, butterfly_sum(): x = x + lax.ppermute(x, axis, [(i, i ^ bit) for i in range(groups)])  0.97 us
  transfers between devices with their start and end apart: 4, of which 2 were waited for; matrix products, arithmetic and copies ran while one was open for 4% of the time, Pallas kernels for 6%

profile of v14, /device:TPU:0, one launch (start us, length us, event | category | flops | bytes accessed | tf_op | source)
XLA Modules:
  0.0 37.9 jit_solution(190730260871278709)
XLA Ops:
  0.6 0.5 %collective-permute-start.1 = (f32[3,1,8,64,128]{4,3,2,1,0:T(8,128)}, f32[3,1,8,64,128]{4,3,2,1,0:T(8,128)S(1)}, u32[]{:S(2)}, u32[]{:S(2)}) collective-permute-start(f32[3,1,8,64,128]{4,3,2,1,0:T(8,128)} %param.7), channel_id=1, source_target_pairs={{0,1},{1,0},{2,3},{3,2},{4,5},{5,4},{6,7},{7,6},{8,9},{9,8},{10,11... | collective-permute-start | bytes 2359304 | tf_op jit(solution)/shard_map/ppermute | solution.py:52
  1.1 0.1 collective-permute-start
  1.2 8.3 %all-to-all-start = ((f32[16,32,128]{2,1,0:T(8,128)}), f32[16,32,128]{2,1,0:T(8,128)S(1)}, u32[]{:S(2)}, u32[]{:S(2)}) async-start(f32[16,32,128]{2,1,0:T(8,128)} %bitcast.26), calls=%async_computation | async-start | bytes 524288 | tf_op jit(solution)/shard_map/all_to_all | solution.py:141
  10.2 0.7 %copy-done.1 = f32[1,8,64,128]{3,2,1,0:T(8,128)} copy-done((f32[1,8,64,128]{3,2,1,0:T(8,128)}, f32[1,8,64,128]{3,2,1,0:T(8,128)S(1)}, u32[]{:S(2)}) %copy-start.1) | copy-done | bytes 262168
  10.9 0.3 copy-done
  11.2 2.4 %shard_map.77 = (f32[8,64,128]{2,1,0:T(8,128)}, f32[2,8,128]{2,1,0:T(8,128)}) custom-call(f32[1]{0:T(128)S(6)} %copy.29.pulse_ref, f32[8,64,128]{2,1,0:T(8,128)} %bitcast.27, f32[3,8,64,128]{3,2,1,0:T(8,128)} %bitcast.29, f32[8,64,128]{2,1,0:T(8,128)} %bitcast.30, f32[1,8,64,128]{3,2,1,0:T(8,128)} %copy-done.1, f32[3,1,8,64,128]{4,3,2,1,0:T(8,128)} %copy-done, ...), custom_call_target="tpu_custom_call" | custom-call | tf_op jit(solution)/shard_map/pallas_call | solution.py:111
  13.6 1.1 %convolution_bitcast_fusion = f32[2,128]{1,0:T(2,128)S(1)} fusion(s32[8,128]{1,0:T(8,128)S(1)} %copy-done.4, f32[2,8,128]{2,1,0:T(8,128)} %get-tuple-element.8), kind=kOutput, calls=%fused_computation | convolution fusion | flops 3276800 | bytes 13312 | tf_op jit(solution)/shard_map/dot_general | solution.py:151
  14.7 0.1 collective-permute-start.2
  14.7 0.1 pad.8.clone
  14.8 0.1 pad.9.clone
  14.9 1.0 %collective-permute-done.2 = f32[2,128]{1,0:T(2,128)S(1)} collective-permute-done((f32[2,128]{1,0:T(2,128)S(1)}, f32[2,128]{1,0:T(2,128)S(1)}, u32[]{:S(2)}, u32[]{:S(2)}) %collective-permute-start.2) | collective-permute-done | bytes 1056 | tf_op jit(solution)/shard_map/ppermute | solution.py:43
  15.9 0.1 add_multiply_fusion
  15.9 0.1 reshape.24
  16.0 0.1 fusion.4
  16.1 3.5 %all-to-all-done = f32[16,32,128]{2,1,0:T(8,128)S(1)} async-done(((f32[16,32,128]{2,1,0:T(8,128)}), f32[16,32,128]{2,1,0:T(8,128)S(1)}, u32[]{:S(2)}, u32[]{:S(2)}) %all-to-all-start) | async-done | bytes 262176 | tf_op jit(solution)/shard_map/all_to_all | solution.py:141
  19.6 0.5 %fusion.1 = f32[16,32,128]{2,0,1:T(8,128)S(1)} fusion(f32[16,32,128]{2,1,0:T(8,128)S(1)} %all-to-all-done), kind=kOutput, calls=%fused_computation.5 | convolution fusion | flops 12589312 | bytes 524288 | tf_op jit(solution)/shard_map/ji,jrc->irc/dot_general | solution.py:164
  20.2 0.1 copy.20
  20.3 14.9 %all_to_all.10 = f32[16,40,128]{2,1,0:T(8,128)S(1)} all-to-all(f32[16,40,128]{2,1,0:T(8,128)S(1)} %copy.20), channel_id=1, replica_groups=mesh['tm'=16,'space'=2] {'tm'}, dimensions={0} | all-to-all | bytes 655360 | tf_op jit(solution)/shard_map/all_to_all | solution.py:172
  35.2 0.1 copy.23
  35.3 0.2 slice_reduce_fusion
  35.5 0.1 multiply_reduce_fusion
  35.7 0.9 %copy-done.2 = f32[8,64,128]{2,1,0:T(8,128)S(1)} copy-done((f32[8,64,128]{2,1,0:T(8,128)S(1)}, f32[8,64,128]{2,1,0:T(8,128)}, u32[]{:S(2)}) %copy-start.2) | copy-done | bytes 262168
  36.6 0.7 %fusion = f32[1,8,64,128]{3,2,1,0:T(8,128)} fusion(f32[8,64,128]{2,1,0:T(8,128)S(1)} %copy-done.2, f32[8,64,128]{2,1,0:T(8,128)S(1)} %bitcast.28), kind=kLoop, calls=%fused_computation.4 | loop fusion | flops 65536 | bytes 786432 | tf_op jit(solution)/shard_map/broadcast_in_dim | solution.py:178
  37.3 0.6 %fusion.16 = f32[8]{0:T(128)} fusion(f32[16,1,8]{0,2,1:T(8,128)S(1)} %copy.24, f32[16,1,8]{0,2,1:T(8,128)S(1)} %copy.23, f32[16]{0:T(128)S(1)} %multiply_reduce_fusion), kind=kLoop, calls=%fused_computation.31 | loop fusion | flops 376 | bytes 1120 | tf_op jit(solution)/shard_map/reduce_sum | solution.py:176
  (14 shorter events, 0.1 us)
Async XLA Ops:
  0.6 9.6 %collective-permute-start.1 = (f32[3,1,8,64,128]{4,3,2,1,0:T(8,128)}, f32[3,1,8,64,128]{4,3,2,1,0:T(8,128)S(1)}, u32[]{:S(2)}, u32[]{:S(2)}) collective-permute-start(f32[3,1,8,64,128]{4,3,2,1,0:T(8,128)} %param.7), channel_id=1, source_target_pairs={{0,1},{1,0},{2,3},{3,2},{4,5},{5,4},{6,7},{7,6},{8,9},{9,8},{10,11... | collective-permute-start | bytes 2359304 | tf_op jit(solution)/shard_map/ppermute | solution.py:52
  1.1 9.0 %collective-permute-start = (f32[1,8,64,128]{3,2,1,0:T(8,128)}, f32[1,8,64,128]{3,2,1,0:T(8,128)S(1)}, u32[]{:S(2)}, u32[]{:S(2)}) collective-permute-start(f32[1,8,64,128]{3,2,1,0:T(8,128)} %param.6), channel_id=1, source_target_pairs={{0,1},{1,0},{2,3},{3,2},{4,5},{5,4},{6,7},{7,6},{8,9},{9,8},{10,11... | collective-permute-start | bytes 786440 | tf_op jit(solution)/shard_map/ppermute | solution.py:52
  1.2 18.4 %all-to-all-start = ((f32[16,32,128]{2,1,0:T(8,128)}), f32[16,32,128]{2,1,0:T(8,128)S(1)}, u32[]{:S(2)}, u32[]{:S(2)}) async-start(f32[16,32,128]{2,1,0:T(8,128)} %bitcast.26), calls=%async_computation | async-start | bytes 524288 | tf_op jit(solution)/shard_map/all_to_all | solution.py:141
  10.2 0.7 %copy-start.1 = (f32[1,8,64,128]{3,2,1,0:T(8,128)}, f32[1,8,64,128]{3,2,1,0:T(8,128)S(1)}, u32[]{:S(2)}) copy-start(f32[1,8,64,128]{3,2,1,0:T(8,128)S(1)} %collective-permute-done.prev_ref.next_ref) | copy-start | bytes 786436
  10.2 1.0 %copy-start = (f32[3,1,8,64,128]{4,3,2,1,0:T(8,128)}, f32[3,1,8,64,128]{4,3,2,1,0:T(8,128)S(1)}, u32[]{:S(2)}) copy-start(f32[3,1,8,64,128]{4,3,2,1,0:T(8,128)S(1)} %collective-permute-done.1.prev_u_ref.next_u_ref) | copy-start | bytes 2359300
  11.2 2.4 %copy-start.4 = (s32[8,128]{1,0:T(8,128)S(1)}, s32[8,128]{1,0:T(8,128)}, u32[]{:S(2)}) copy-start(s32[8,128]{1,0:T(8,128)} %param.10) | copy-start | bytes 12292
  14.7 1.2 %collective-permute-start.2 = (f32[2,128]{1,0:T(2,128)S(1)}, f32[2,128]{1,0:T(2,128)S(1)}, u32[]{:S(2)}, u32[]{:S(2)}) collective-permute-start(f32[2,128]{1,0:T(2,128)S(1)} %convolution_bitcast_fusion), channel_id=1, source_target_pairs={{0,1},{1,0},{2,3},{3,2},{4,5},{5,4},{6,7},{7,6},{8,9},{9,8},{10,11... | collective-permute-start | bytes 3080 | tf_op jit(solution)/shard_map/ppermute | solution.py:43
  14.8 1.1 %copy-start.3 = (f32[2]{0:T(128)S(1)}, f32[2]{0:T(128)}, u32[]{:S(2)}) copy-start(f32[2]{0:T(128)} %constant.48) | copy-start | bytes 28
  35.6 1.0 %copy-start.2 = (f32[8,64,128]{2,1,0:T(8,128)S(1)}, f32[8,64,128]{2,1,0:T(8,128)}, u32[]{:S(2)}) copy-start(f32[8,64,128]{2,1,0:T(8,128)} %get-tuple-element.9) | copy-start | bytes 786436

commit v15 on v14

--- a/solution.py
+++ b/solution.py
@@ -129,6 +129,46 @@
     )(pulse, field, velocity, source, *prev, *nxt)
 
 
+def finish_kernel(dmat_ref, term_ref, tile_ref, kept_ref, out_ref, grad_ref):
+    block, chunk, cz = term_ref.shape
+    out_ref[...] = kept_ref[...] + term_ref[...].reshape(block * chunk, cz)
+
+    @pl.when(pl.program_id(0) == 0)
+    def _():
+        count = tile_ref.shape[0]
+        pulses = tile_ref[:, 2, :]
+        weights = jnp.zeros((count, cz), jnp.float32)
+        for i in range(count):
+            weights = weights + dmat_ref[:, i : i + 1] * pulses[i : i + 1, :]
+        parts = tile_ref[:, 0, :] + weights * tile_ref[:, 1, :]
+        grad_ref[...] = jnp.sum(parts, axis=0, keepdims=True)[0, : grad_ref.shape[0]]
+
+
+def finish(dmat, incoming, kept, share):
+    count, width, cz = incoming.shape
+    chunk = width - 8
+    rows = kept.shape[0]
+    steps = 4 if count % 4 == 0 else 1
+    return pl.pallas_call(
+        finish_kernel,
+        grid=(steps,),
+        out_shape=(
+            jax.ShapeDtypeStruct((rows, cz), jnp.float32),
+            jax.ShapeDtypeStruct((share,), jnp.float32),
+        ),
+        in_specs=[
+            pl.BlockSpec((count, count), lambda s: (0, 0)),
+            pl.BlockSpec((count // steps, chunk, cz), lambda s: (s, 0, 0)),
+            pl.BlockSpec((count, 8, cz), lambda s: (0, chunk // 8, 0)),
+            pl.BlockSpec((rows // steps, cz), lambda s: (s, 0)),
+        ],
+        out_specs=(
+            pl.BlockSpec((rows // steps, cz), lambda s: (s, 0)),
+            pl.BlockSpec((share,), lambda s: (0,)),
+        ),
+    )(dmat, incoming, incoming, kept)
+
+
 def on_device(adjoint, base_flow, source, pulse, actuator):
     count = lax.axis_size("tm")
     nt_loc, nx, cy, cz = adjoint.shape
@@ -170,11 +210,8 @@
 
     outgoing = jnp.concatenate([derived, grad_rows], axis=1)
     incoming = lax.all_to_all(outgoing, "tm", 0, 0, tiled=True)
-    scaled_term = incoming[:, :chunk].reshape(nx, cy, cz)
-    tile = incoming[:, chunk : chunk + 3, :share]
-    weights = jnp.sum(dmat * tile[None, :, 2, 0], axis=1)
-    gradient = jnp.sum(tile[:, 0] + weights[:, None] * tile[:, 1], axis=0)
-    updated = kept + scaled_term
+    updated, gradient = finish(dmat, incoming, kept.reshape(nx * cy, cz), share)
+    updated = updated.reshape(nx, cy, cz)
     return (updated[None], gradient)
 
 

time: 38.3 us -> 40.6 us (1.060)
  blocking collectives: 14.9 us -> 0 us
  waiting for transfers between devices: 4.5 us -> 15.4 us
  starting transfers between devices: 8.96 us -> 12.5 us
  Pallas kernels: 2.42 us -> 5.63 us
  local copies, waits for them, and re-layouts: 2.59 us -> 2.02 us
    all_to_all x1 -> x0, blocking collectives: 14.9 us -> none  [on_device(): incoming = lax.all_to_all(outgoing, 'tm', 0, 0, tiled=True)]
    all_to_all x0 -> x1, waiting for transfers between devices: none -> 10.9 us  [on_device(): incoming = lax.all_to_all(outgoing, 'tm', 0, 0, tiled=True)]
    all_to_all x0 -> x1, starting transfers between devices: none -> 3.55 us  [on_device(): incoming = lax.all_to_all(outgoing, 'tm', 0, 0, tiled=True)]
    pallas_call x0 -> x1, Pallas kernels: none -> 3.19 us  [finish(): pl.pallas_call(finish_kernel, grid=(steps,), out_shape=(jax.ShapeDtypeStr...]
    broadcast_in_dim x1 -> x0, other arithmetic: 0.73 us -> none  [on_device(): return (updated[None], gradient)]
    concatenate x1, other arithmetic: 0.02 us -> 0.74 us  [on_device(): outgoing = jnp.concatenate([derived, grad_rows], axis=1)]
    reduce_sum x2 -> x0, other arithmetic: 0.71 us -> none  [the longest x1 0.63 us: on_device(): gradient = jnp.sum(tile[:, 0] + weights[:, None] * tile[:, 1], axis=0)]
    select_n x0 -> x1, other arithmetic: none -> 0.66 us  [spectral_matrix(): jnp.where(skipped, jnp.float32(0.0), 0.5 * parity / safe_tan)]
  transfers between devices with their start and end apart: 4 -> 5, of which waited for: 2 -> 3; matrix products, arithmetic and copies ran while one was open for 4% -> 5% of each run, Pallas kernels for 6% -> 6%
where the time goes in v15:
time: 40.6 us; the launch traced here: 40 us
  waiting for transfers between devices  15.4 us (38%)
  starting transfers between devices  12.5 us (31%)
  Pallas kernels  5.63 us (14%)
  local copies, waits for them, and re-layouts  2.02 us (5%)
  matrix products  1.61 us (4%)
  other arithmetic  1.55 us (4%)
  between operations  1.37 us (3%)
    all_to_all x1, waiting for transfers between devices, on_device(): incoming = lax.all_to_all(outgoing, 'tm', 0, 0, tiled=True)  10.9 us
    all_to_all x1, starting transfers between devices, on_device(): lax.all_to_all(adjoint.reshape(count, chunk, cz), 'tm', 0, 0, tiled=True)  8.29 us
    all_to_all x1, starting transfers between devices, on_device(): incoming = lax.all_to_all(outgoing, 'tm', 0, 0, tiled=True)  3.55 us
    all_to_all x1, waiting for transfers between devices, on_device(): lax.all_to_all(adjoint.reshape(count, chunk, cz), 'tm', 0, 0, tiled=True)  3.49 us
    pallas_call x1, Pallas kernels, finish(): pl.pallas_call(finish_kernel, grid=(steps,), out_shape=(jax.ShapeDtypeStr...  3.19 us
    pallas_call x1, Pallas kernels, stencil(): pl.pallas_call(stencil_kernel, grid=(1,), out_shape=(jax.ShapeDtypeStruct...  2.44 us
    unnamed x10, local copies, waits for them, and re-layouts  1.68 us
    dot_general x1, matrix products, on_device(): jnp.dot(walls.reshape(2, -1), onehot.reshape(-1, NACT), precision=lax.Pre...  1.07 us
  transfers between devices with their start and end apart: 5, of which 3 were waited for; matrix products, arithmetic and copies ran while one was open for 5% of the time, Pallas kernels for 6%

profile of v15, /device:TPU:0, one launch (start us, length us, event | category | flops | bytes accessed | tf_op | source)
XLA Modules:
  0.0 40.0 jit_solution(16185593466262285663)
XLA Ops:
  0.6 0.5 %collective-permute-start.1 = (f32[3,1,8,64,128]{4,3,2,1,0:T(8,128)}, f32[3,1,8,64,128]{4,3,2,1,0:T(8,128)S(1)}, u32[]{:S(2)}, u32[]{:S(2)}) collective-permute-start(f32[3,1,8,64,128]{4,3,2,1,0:T(8,128)} %param.7), channel_id=1, source_target_pairs={{0,1},{1,0},{2,3},{3,2},{4,5},{5,4},{6,7},{7,6},{8,9},{9,8},{10,11... | collective-permute-start | bytes 2359304 | tf_op jit(solution)/shard_map/ppermute | solution.py:52
  1.1 0.1 collective-permute-start
  1.2 8.3 %all-to-all-start = ((f32[16,32,128]{2,1,0:T(8,128)}), f32[16,32,128]{2,1,0:T(8,128)S(1)}, u32[]{:S(2)}, u32[]{:S(2)}) async-start(f32[16,32,128]{2,1,0:T(8,128)} %bitcast.15), calls=%async_computation | async-start | bytes 524288 | tf_op jit(solution)/shard_map/all_to_all | solution.py:181
  10.2 0.0 copy-start.2
  10.2 0.7 %copy-done.2 = f32[1,8,64,128]{3,2,1,0:T(8,128)} copy-done((f32[1,8,64,128]{3,2,1,0:T(8,128)}, f32[1,8,64,128]{3,2,1,0:T(8,128)S(1)}, u32[]{:S(2)}) %copy-start.2) | copy-done | bytes 262168
  10.9 0.3 copy-done
  11.2 2.4 %shard_map.77 = (f32[8,64,128]{2,1,0:T(8,128)}, f32[2,8,128]{2,1,0:T(8,128)}) custom-call(f32[1]{0:T(128)S(6)} %copy.30.pulse_ref, f32[8,64,128]{2,1,0:T(8,128)} %bitcast.16, f32[3,8,64,128]{3,2,1,0:T(8,128)} %bitcast.17, f32[8,64,128]{2,1,0:T(8,128)} %bitcast.18, f32[1,8,64,128]{3,2,1,0:T(8,128)} %copy-done.2, f32[3,1,8,64,128]{4,3,2,1,0:T(8,128)} %copy-done, ...), custom_call_target="tpu_custom_call" | custom-call | tf_op jit(solution)/shard_map/pallas_call | solution.py:111
  13.6 1.1 %convolution_bitcast_fusion = f32[2,128]{1,0:T(2,128)S(1)} fusion(s32[8,128]{1,0:T(8,128)S(1)} %copy-done.4, f32[2,8,128]{2,1,0:T(8,128)} %get-tuple-element.10), kind=kOutput, calls=%fused_computation | convolution fusion | flops 3276800 | bytes 13312 | tf_op jit(solution)/shard_map/dot_general | solution.py:191
  14.7 0.1 collective-permute-start.2
  14.8 0.1 pad.8.clone
  14.8 0.1 pad.9.clone
  14.9 1.0 %collective-permute-done.2 = f32[2,128]{1,0:T(2,128)S(1)} collective-permute-done((f32[2,128]{1,0:T(2,128)S(1)}, f32[2,128]{1,0:T(2,128)S(1)}, u32[]{:S(2)}, u32[]{:S(2)}) %collective-permute-start.2) | collective-permute-done | bytes 1056 | tf_op jit(solution)/shard_map/ppermute | solution.py:43
  15.9 0.1 add_multiply_fusion
  16.0 0.1 reshape.22
  16.1 0.1 fusion.3
  16.1 3.5 %all-to-all-done = f32[16,32,128]{2,1,0:T(8,128)S(1)} async-done(((f32[16,32,128]{2,1,0:T(8,128)}), f32[16,32,128]{2,1,0:T(8,128)S(1)}, u32[]{:S(2)}, u32[]{:S(2)}) %all-to-all-start) | async-done | bytes 262176 | tf_op jit(solution)/shard_map/all_to_all | solution.py:181
  19.6 0.5 %fusion = f32[16,32,128]{2,0,1:T(8,128)S(1)} fusion(f32[16,32,128]{2,1,0:T(8,128)S(1)} %all-to-all-done), kind=kOutput, calls=%fused_computation.3 | convolution fusion | flops 12589312 | bytes 524288 | tf_op jit(solution)/shard_map/ji,jrc->irc/dot_general | solution.py:204
  20.2 0.1 copy.21
  20.3 0.7 %pad_maximum_fusion = f32[16,40,128]{2,1,0:T(8,128)} fusion(f32[16,8,128]{2,1,0:T(8,128)S(1)} %fusion.3, f32[16,32,128]{2,1,0:T(8,128)S(1)} %copy.21), kind=kLoop, calls=%fused_computation.2 | loop fusion | flops 81920 | bytes 655360 | tf_op jit(solution)/shard_map/concatenate | solution.py:211
  21.0 3.5 %all-to-all-start.1 = ((f32[16,40,128]{2,1,0:T(8,128)}), f32[16,40,128]{2,1,0:T(8,128)S(1)}, u32[]{:S(2)}, u32[]{:S(2)}) async-start(f32[16,40,128]{2,1,0:T(8,128)} %pad_maximum_fusion), calls=%async_computation.1 | async-start | bytes 655360 | tf_op jit(solution)/shard_map/all_to_all | solution.py:212
  24.6 0.7 %divide_select_fusion.dmat_ref = f32[16,16]{1,0:T(8,128)} fusion(), kind=kLoop, calls=%fused_computation.18 | loop fusion | flops 6144 | bytes 1024 | tf_op jit(solution)/shard_map/jit(_where)/select_n | solution.py:26
  25.2 10.9 %all-to-all-done.1.term_ref.tile_ref = f32[16,40,128]{2,1,0:T(8,128)S(1)} async-done(((f32[16,40,128]{2,1,0:T(8,128)}), f32[16,40,128]{2,1,0:T(8,128)S(1)}, u32[]{:S(2)}, u32[]{:S(2)}) %all-to-all-start.1) | async-done | bytes 327712 | tf_op jit(solution)/shard_map/all_to_all | solution.py:212
  36.1 0.7 %copy-done.1 = f32[16,40,128]{2,1,0:T(8,128)} copy-done((f32[16,40,128]{2,1,0:T(8,128)}, f32[16,40,128]{2,1,0:T(8,128)S(1)}, u32[]{:S(2)}) %copy-start.1) | copy-done | bytes 327704
  36.8 3.2 %shard_map.78 = (f32[512,128]{1,0:T(8,128)}, f32[8]{0:T(128)}) custom-call(f32[16,16]{1,0:T(8,128)} %divide_select_fusion.dmat_ref, f32[16,40,128]{2,1,0:T(8,128)} %copy-done.1, f32[16,40,128]{2,1,0:T(8,128)} %copy-done.1, f32[512,128]{1,0:T(8,128)} %bitcast.19), custom_call_target="tpu_custom_call" | custom-call | tf_op jit(solution)/shard_map/pallas_call | solution.py:152
  (10 shorter events, 0.0 us)
Async XLA Ops:
  0.6 9.6 %collective-permute-start.1 = (f32[3,1,8,64,128]{4,3,2,1,0:T(8,128)}, f32[3,1,8,64,128]{4,3,2,1,0:T(8,128)S(1)}, u32[]{:S(2)}, u32[]{:S(2)}) collective-permute-start(f32[3,1,8,64,128]{4,3,2,1,0:T(8,128)} %param.7), channel_id=1, source_target_pairs={{0,1},{1,0},{2,3},{3,2},{4,5},{5,4},{6,7},{7,6},{8,9},{9,8},{10,11... | collective-permute-start | bytes 2359304 | tf_op jit(solution)/shard_map/ppermute | solution.py:52
  1.1 9.0 %collective-permute-start = (f32[1,8,64,128]{3,2,1,0:T(8,128)}, f32[1,8,64,128]{3,2,1,0:T(8,128)S(1)}, u32[]{:S(2)}, u32[]{:S(2)}) collective-permute-start(f32[1,8,64,128]{3,2,1,0:T(8,128)} %param.6), channel_id=1, source_target_pairs={{0,1},{1,0},{2,3},{3,2},{4,5},{5,4},{6,7},{7,6},{8,9},{9,8},{10,11... | collective-permute-start | bytes 786440 | tf_op jit(solution)/shard_map/ppermute | solution.py:52
  1.2 18.4 %all-to-all-start = ((f32[16,32,128]{2,1,0:T(8,128)}), f32[16,32,128]{2,1,0:T(8,128)S(1)}, u32[]{:S(2)}, u32[]{:S(2)}) async-start(f32[16,32,128]{2,1,0:T(8,128)} %bitcast.15), calls=%async_computation | async-start | bytes 524288 | tf_op jit(solution)/shard_map/all_to_all | solution.py:181
  10.2 0.7 %copy-start.2 = (f32[1,8,64,128]{3,2,1,0:T(8,128)}, f32[1,8,64,128]{3,2,1,0:T(8,128)S(1)}, u32[]{:S(2)}) copy-start(f32[1,8,64,128]{3,2,1,0:T(8,128)S(1)} %collective-permute-done.prev_ref.next_ref) | copy-start | bytes 786436
  10.2 1.0 %copy-start = (f32[3,1,8,64,128]{4,3,2,1,0:T(8,128)}, f32[3,1,8,64,128]{4,3,2,1,0:T(8,128)S(1)}, u32[]{:S(2)}) copy-start(f32[3,1,8,64,128]{4,3,2,1,0:T(8,128)S(1)} %collective-permute-done.1.prev_u_ref.next_u_ref) | copy-start | bytes 2359300
  11.2 2.4 %copy-start.4 = (s32[8,128]{1,0:T(8,128)S(1)}, s32[8,128]{1,0:T(8,128)}, u32[]{:S(2)}) copy-start(s32[8,128]{1,0:T(8,128)} %param.10) | copy-start | bytes 12292
  14.7 1.2 %collective-permute-start.2 = (f32[2,128]{1,0:T(2,128)S(1)}, f32[2,128]{1,0:T(2,128)S(1)}, u32[]{:S(2)}, u32[]{:S(2)}) collective-permute-start(f32[2,128]{1,0:T(2,128)S(1)} %convolution_bitcast_fusion), channel_id=1, source_target_pairs={{0,1},{1,0},{2,3},{3,2},{4,5},{5,4},{6,7},{7,6},{8,9},{9,8},{10,11... | collective-permute-start | bytes 3080 | tf_op jit(solution)/shard_map/ppermute | solution.py:43
  14.8 1.1 %copy-start.3 = (f32[2]{0:T(128)S(1)}, f32[2]{0:T(128)}, u32[]{:S(2)}) copy-start(f32[2]{0:T(128)} %constant.48) | copy-start | bytes 28
  21.0 15.1 %all-to-all-start.1 = ((f32[16,40,128]{2,1,0:T(8,128)}), f32[16,40,128]{2,1,0:T(8,128)S(1)}, u32[]{:S(2)}, u32[]{:S(2)}) async-start(f32[16,40,128]{2,1,0:T(8,128)} %pad_maximum_fusion), calls=%async_computation.1 | async-start | bytes 655360 | tf_op jit(solution)/shard_map/all_to_all | solution.py:212
  36.1 0.7 %copy-start.1 = (f32[16,40,128]{2,1,0:T(8,128)}, f32[16,40,128]{2,1,0:T(8,128)S(1)}, u32[]{:S(2)}) copy-start(f32[16,40,128]{2,1,0:T(8,128)S(1)} %all-to-all-done.1.term_ref.tile_ref) | copy-start | bytes 983044

commit v16 on v14

--- a/solution.py
+++ b/solution.py
@@ -171,9 +171,9 @@
     outgoing = jnp.concatenate([derived, grad_rows], axis=1)
     incoming = lax.all_to_all(outgoing, "tm", 0, 0, tiled=True)
     scaled_term = incoming[:, :chunk].reshape(nx, cy, cz)
-    tile = incoming[:, chunk : chunk + 3, :share]
-    weights = jnp.sum(dmat * tile[None, :, 2, 0], axis=1)
-    gradient = jnp.sum(tile[:, 0] + weights[:, None] * tile[:, 1], axis=0)
+    weights = jnp.sum(dmat * incoming[None, :, chunk + 2, 0], axis=1)
+    lanes = incoming[:, chunk, :] + weights[:, None] * incoming[:, chunk + 1, :]
+    gradient = jnp.sum(lanes, axis=0)[:share]
     updated = kept + scaled_term
     return (updated[None], gradient)
 

time: 38.3 us -> 38.1 us (level)
    unnamed x12 -> x10, local copies, waits for them, and re-layouts: 2.02 us -> 1.88 us
where the time goes in v16:
time: 38.1 us; the launch traced here: 37.8 us
  blocking collectives  14.9 us (39%)
  starting transfers between devices  8.96 us (24%)
  waiting for transfers between devices  4.5 us (12%)
  local copies, waits for them, and re-layouts  2.46 us (6%)
  Pallas kernels  2.42 us (6%)
  other arithmetic  1.6 us (4%)
  matrix products  1.58 us (4%)
  between operations  1.38 us (4%)
    all_to_all x1, blocking collectives, on_device(): incoming = lax.all_to_all(outgoing, 'tm', 0, 0, tiled=True)  14.9 us
    all_to_all x1, starting transfers between devices, on_device(): lax.all_to_all(adjoint.reshape(count, chunk, cz), 'tm', 0, 0, tiled=True)  8.29 us
    all_to_all x1, waiting for transfers between devices, on_device(): lax.all_to_all(adjoint.reshape(count, chunk, cz), 'tm', 0, 0, tiled=True)  3.52 us
    pallas_call x1, Pallas kernels, stencil(): pl.pallas_call(stencil_kernel, grid=(1,), out_shape=(jax.ShapeDtypeStruct...  2.42 us
    unnamed x10, local copies, waits for them, and re-layouts  1.88 us
    dot_general x1, matrix products, on_device(): jnp.dot(walls.reshape(2, -1), onehot.reshape(-1, NACT), precision=lax.Pre...  1.07 us
    ppermute x1, waiting for transfers between devices, butterfly_sum(): x = x + lax.ppermute(x, axis, [(i, i ^ bit) for i in range(groups)])  0.97 us
  transfers between devices with their start and end apart: 4, of which 2 were waited for; matrix products, arithmetic and copies ran while one was open for 4% of the time, Pallas kernels for 6%

profile of v16, /device:TPU:0, one launch (start us, length us, event | category | flops | bytes accessed | tf_op | source)
XLA Modules:
  0.0 37.8 jit_solution(3314530705863449417)
XLA Ops:
  0.6 0.5 %collective-permute-start.1 = (f32[3,1,8,64,128]{4,3,2,1,0:T(8,128)}, f32[3,1,8,64,128]{4,3,2,1,0:T(8,128)S(1)}, u32[]{:S(2)}, u32[]{:S(2)}) collective-permute-start(f32[3,1,8,64,128]{4,3,2,1,0:T(8,128)} %param.7), channel_id=1, source_target_pairs={{0,1},{1,0},{2,3},{3,2},{4,5},{5,4},{6,7},{7,6},{8,9},{9,8},{10,11... | collective-permute-start | bytes 2359304 | tf_op jit(solution)/shard_map/ppermute | solution.py:52
  1.1 0.1 collective-permute-start
  1.2 8.3 %all-to-all-start = ((f32[16,32,128]{2,1,0:T(8,128)}), f32[16,32,128]{2,1,0:T(8,128)S(1)}, u32[]{:S(2)}, u32[]{:S(2)}) async-start(f32[16,32,128]{2,1,0:T(8,128)} %bitcast.23), calls=%async_computation | async-start | bytes 524288 | tf_op jit(solution)/shard_map/all_to_all | solution.py:141
  10.2 0.0 copy-start.1
  10.2 0.7 %copy-done.1 = f32[1,8,64,128]{3,2,1,0:T(8,128)} copy-done((f32[1,8,64,128]{3,2,1,0:T(8,128)}, f32[1,8,64,128]{3,2,1,0:T(8,128)S(1)}, u32[]{:S(2)}) %copy-start.1) | copy-done | bytes 262168
  10.9 0.3 copy-done
  11.2 2.4 %shard_map.77 = (f32[8,64,128]{2,1,0:T(8,128)}, f32[2,8,128]{2,1,0:T(8,128)}) custom-call(f32[1]{0:T(128)S(6)} %copy.23.pulse_ref, f32[8,64,128]{2,1,0:T(8,128)} %bitcast.24, f32[3,8,64,128]{3,2,1,0:T(8,128)} %bitcast.26, f32[8,64,128]{2,1,0:T(8,128)} %bitcast.27, f32[1,8,64,128]{3,2,1,0:T(8,128)} %copy-done.1, f32[3,1,8,64,128]{4,3,2,1,0:T(8,128)} %copy-done, ...), custom_call_target="tpu_custom_call" | custom-call | tf_op jit(solution)/shard_map/pallas_call | solution.py:111
  13.6 1.1 %convolution_bitcast_fusion = f32[2,128]{1,0:T(2,128)S(1)} fusion(s32[8,128]{1,0:T(8,128)S(1)} %copy-done.4, f32[2,8,128]{2,1,0:T(8,128)} %get-tuple-element.8), kind=kOutput, calls=%fused_computation | convolution fusion | flops 3276800 | bytes 13312 | tf_op jit(solution)/shard_map/dot_general | solution.py:151
  14.7 0.1 collective-permute-start.2
  14.7 0.1 pad.8.clone
  14.8 0.1 pad.9.clone
  14.9 1.0 %collective-permute-done.2 = f32[2,128]{1,0:T(2,128)S(1)} collective-permute-done((f32[2,128]{1,0:T(2,128)S(1)}, f32[2,128]{1,0:T(2,128)S(1)}, u32[]{:S(2)}, u32[]{:S(2)}) %collective-permute-start.2) | collective-permute-done | bytes 1056 | tf_op jit(solution)/shard_map/ppermute | solution.py:43
  15.9 0.1 add_multiply_fusion
  15.9 0.1 reshape.24
  16.0 0.1 fusion.4
  16.1 3.5 %all-to-all-done = f32[16,32,128]{2,1,0:T(8,128)S(1)} async-done(((f32[16,32,128]{2,1,0:T(8,128)}), f32[16,32,128]{2,1,0:T(8,128)S(1)}, u32[]{:S(2)}, u32[]{:S(2)}) %all-to-all-start) | async-done | bytes 262176 | tf_op jit(solution)/shard_map/all_to_all | solution.py:141
  19.6 0.5 %fusion.1 = f32[16,32,128]{2,0,1:T(8,128)S(1)} fusion(f32[16,32,128]{2,1,0:T(8,128)S(1)} %all-to-all-done), kind=kOutput, calls=%fused_computation.5 | convolution fusion | flops 12589312 | bytes 524288 | tf_op jit(solution)/shard_map/ji,jrc->irc/dot_general | solution.py:164
  20.2 0.1 copy.16
  20.3 14.9 %all_to_all.10 = f32[16,40,128]{2,1,0:T(8,128)S(1)} all-to-all(f32[16,40,128]{2,1,0:T(8,128)S(1)} %copy.16), channel_id=1, replica_groups=mesh['tm'=16,'space'=2] {'tm'}, dimensions={0} | all-to-all | bytes 655360 | tf_op jit(solution)/shard_map/all_to_all | solution.py:172
  35.2 0.2 slice_reduce_fusion
  35.4 0.1 multiply_reduce_fusion
  35.5 0.9 %copy-done.2 = f32[8,64,128]{2,1,0:T(8,128)S(1)} copy-done((f32[8,64,128]{2,1,0:T(8,128)S(1)}, f32[8,64,128]{2,1,0:T(8,128)}, u32[]{:S(2)}) %copy-start.2) | copy-done | bytes 262168
  36.4 0.7 %fusion = f32[1,8,64,128]{3,2,1,0:T(8,128)} fusion(f32[8,64,128]{2,1,0:T(8,128)S(1)} %copy-done.2, f32[8,64,128]{2,1,0:T(8,128)S(1)} %bitcast.25), kind=kLoop, calls=%fused_computation.4 | loop fusion | flops 65536 | bytes 786432 | tf_op jit(solution)/shard_map/broadcast_in_dim | solution.py:178
  37.2 0.6 %add_reduce_fusion = f32[128]{0:T(128)} fusion(f32[16,128]{1,0:T(8,128)S(1)} %bitcast.30, f32[16,128]{1,0:T(8,128)S(1)} %bitcast.29, f32[16]{0:T(128)S(1)} %multiply_reduce_fusion), kind=kLoop, calls=%fused_computation.19 | loop fusion | flops 6016 | bytes 16960 | tf_op jit(solution)/shard_map/reduce_sum | solution.py:176
  (12 shorter events, 0.1 us)
Async XLA Ops:
  0.6 9.6 %collective-permute-start.1 = (f32[3,1,8,64,128]{4,3,2,1,0:T(8,128)}, f32[3,1,8,64,128]{4,3,2,1,0:T(8,128)S(1)}, u32[]{:S(2)}, u32[]{:S(2)}) collective-permute-start(f32[3,1,8,64,128]{4,3,2,1,0:T(8,128)} %param.7), channel_id=1, source_target_pairs={{0,1},{1,0},{2,3},{3,2},{4,5},{5,4},{6,7},{7,6},{8,9},{9,8},{10,11... | collective-permute-start | bytes 2359304 | tf_op jit(solution)/shard_map/ppermute | solution.py:52
  1.1 9.0 %collective-permute-start = (f32[1,8,64,128]{3,2,1,0:T(8,128)}, f32[1,8,64,128]{3,2,1,0:T(8,128)S(1)}, u32[]{:S(2)}, u32[]{:S(2)}) collective-permute-start(f32[1,8,64,128]{3,2,1,0:T(8,128)} %param.6), channel_id=1, source_target_pairs={{0,1},{1,0},{2,3},{3,2},{4,5},{5,4},{6,7},{7,6},{8,9},{9,8},{10,11... | collective-permute-start | bytes 786440 | tf_op jit(solution)/shard_map/ppermute | solution.py:52
  1.2 18.4 %all-to-all-start = ((f32[16,32,128]{2,1,0:T(8,128)}), f32[16,32,128]{2,1,0:T(8,128)S(1)}, u32[]{:S(2)}, u32[]{:S(2)}) async-start(f32[16,32,128]{2,1,0:T(8,128)} %bitcast.23), calls=%async_computation | async-start | bytes 524288 | tf_op jit(solution)/shard_map/all_to_all | solution.py:141
  10.2 0.7 %copy-start.1 = (f32[1,8,64,128]{3,2,1,0:T(8,128)}, f32[1,8,64,128]{3,2,1,0:T(8,128)S(1)}, u32[]{:S(2)}) copy-start(f32[1,8,64,128]{3,2,1,0:T(8,128)S(1)} %collective-permute-done.prev_ref.next_ref) | copy-start | bytes 786436
  10.2 1.0 %copy-start = (f32[3,1,8,64,128]{4,3,2,1,0:T(8,128)}, f32[3,1,8,64,128]{4,3,2,1,0:T(8,128)S(1)}, u32[]{:S(2)}) copy-start(f32[3,1,8,64,128]{4,3,2,1,0:T(8,128)S(1)} %collective-permute-done.1.prev_u_ref.next_u_ref) | copy-start | bytes 2359300
  11.2 2.4 %copy-start.4 = (s32[8,128]{1,0:T(8,128)S(1)}, s32[8,128]{1,0:T(8,128)}, u32[]{:S(2)}) copy-start(s32[8,128]{1,0:T(8,128)} %param.10) | copy-start | bytes 12292
  14.7 1.2 %collective-permute-start.2 = (f32[2,128]{1,0:T(2,128)S(1)}, f32[2,128]{1,0:T(2,128)S(1)}, u32[]{:S(2)}, u32[]{:S(2)}) collective-permute-start(f32[2,128]{1,0:T(2,128)S(1)} %convolution_bitcast_fusion), channel_id=1, source_target_pairs={{0,1},{1,0},{2,3},{3,2},{4,5},{5,4},{6,7},{7,6},{8,9},{9,8},{10,11... | collective-permute-start | bytes 3080 | tf_op jit(solution)/shard_map/ppermute | solution.py:43
  14.8 1.1 %copy-start.3 = (f32[2]{0:T(128)S(1)}, f32[2]{0:T(128)}, u32[]{:S(2)}) copy-start(f32[2]{0:T(128)} %constant.48) | copy-start | bytes 28
  35.5 1.0 %copy-start.2 = (f32[8,64,128]{2,1,0:T(8,128)S(1)}, f32[8,64,128]{2,1,0:T(8,128)}, u32[]{:S(2)}) copy-start(f32[8,64,128]{2,1,0:T(8,128)} %get-tuple-element.9) | copy-start | bytes 786436

commit v17 on v16

--- a/solution.py
+++ b/solution.py
@@ -155,11 +155,16 @@
         preferred_element_type=jnp.float32,
     )
     terms = butterfly_sum(terms, "space")
+    position = lax.axis_index("tm")
     scales = jnp.array([1.0, -pseudo_step * omega_rate], jnp.float32)[:, None] / total
-    slices = jnp.transpose((terms * scales).reshape(2, count, share), (1, 0, 2))
-    slices = jnp.pad(slices, ((0, 0), (0, 0), (0, cz - share)))
-    pulse_row = jnp.broadcast_to(pulse.reshape(1, 1, 1), (count, 1, cz))
-    grad_rows = jnp.concatenate([slices, pulse_row, jnp.zeros((count, pad - 3, cz), jnp.float32)], axis=1)
+    scaled = (terms * scales).reshape(2, count, share)
+    own_row = lax.dynamic_index_in_dim(dmat, position, 0, keepdims=False)
+    spread = (own_row[None, :, None] * scaled[1][:, None, :]).reshape(count, NACT)
+    mine = jnp.where(jnp.arange(count) == position, pulse[0], 0.0)
+    pulse_lanes = jnp.broadcast_to(jnp.repeat(mine, share)[None, :], (count, NACT))
+    rows = jnp.stack([jnp.pad(scaled[0], ((0, 0), (0, NACT - share))), spread, pulse_lanes], axis=1)
+    rows = jnp.pad(rows, ((0, 0), (0, 0), (0, cz - NACT)))
+    grad_rows = jnp.concatenate([rows, jnp.zeros((count, pad - 3, cz), jnp.float32)], axis=1)
     kept, grad_rows, incoming = lax.optimization_barrier((kept, grad_rows, incoming))
     derived = jnp.einsum(
         "ji,jrc->irc",
@@ -171,9 +176,8 @@
     outgoing = jnp.concatenate([derived, grad_rows], axis=1)
     incoming = lax.all_to_all(outgoing, "tm", 0, 0, tiled=True)
     scaled_term = incoming[:, :chunk].reshape(nx, cy, cz)
-    weights = jnp.sum(dmat * incoming[None, :, chunk + 2, 0], axis=1)
-    lanes = incoming[:, chunk, :] + weights[:, None] * incoming[:, chunk + 1, :]
-    gradient = jnp.sum(lanes, axis=0)[:share]
+    sums = jnp.sum(incoming[:, chunk : chunk + 3, :NACT], axis=0)
+    gradient = sums[0, :share] + jnp.sum((sums[1] * sums[2]).reshape(count, share), axis=0)
     updated = kept + scaled_term
     return (updated[None], gradient)
 

time: 38.1 us -> 38.5 us (1.010)
  waiting for transfers between devices: 4.5 us -> 3.86 us
  blocking collectives: 14.9 us -> 15.4 us
    reduce_sum x2, other arithmetic: 0.68 us -> 0.05 us  [the longest x1 0.02 us: on_device(): sums = jnp.sum(incoming[:, chunk:chunk + 3, :NACT], axis=0)]
    all_to_all x1, blocking collectives: 14.9 us -> 15.4 us  [on_device(): incoming = lax.all_to_all(outgoing, 'tm', 0, 0, tiled=True)]
    add x0 -> x1, other arithmetic: none -> 0.53 us  [on_device(): sums[0, :share] + jnp.sum((sums[1] * sums[2]).reshape(count, share), axis=0)]
    mul x0 -> x8, local copies, waits for them, and re-layouts: none -> 0.47 us  [the longest x7 0.39 us: on_device(): own_row[None, :, None] * scaled[1][:, None, :]]
  transfers between devices with their start and end apart: 4 -> 4, of which waited for: 2 -> 2; matrix products, arithmetic and copies ran while one was open for 4% -> 5% of each run, Pallas kernels for 6% -> 6%
where the time goes in v17:
time: 38.5 us; the launch traced here: 38.1 us
  blocking collectives  15.4 us (40%)
  starting transfers between devices  8.96 us (23%)
  waiting for transfers between devices  3.86 us (10%)
  local copies, waits for them, and re-layouts  2.83 us (7%)
  Pallas kernels  2.44 us (6%)
  matrix products  1.61 us (4%)
  other arithmetic  1.58 us (4%)
  between operations  1.42 us (4%)
    all_to_all x1, blocking collectives, on_device(): incoming = lax.all_to_all(outgoing, 'tm', 0, 0, tiled=True)  15.4 us
    all_to_all x1, starting transfers between devices, on_device(): lax.all_to_all(adjoint.reshape(count, chunk, cz), 'tm', 0, 0, tiled=True)  8.29 us
    all_to_all x1, waiting for transfers between devices, on_device(): lax.all_to_all(adjoint.reshape(count, chunk, cz), 'tm', 0, 0, tiled=True)  3.18 us
    pallas_call x1, Pallas kernels, stencil(): pl.pallas_call(stencil_kernel, grid=(1,), out_shape=(jax.ShapeDtypeStruct...  2.44 us
    unnamed x10, local copies, waits for them, and re-layouts  1.87 us
    dot_general x1, matrix products, on_device(): jnp.dot(walls.reshape(2, -1), onehot.reshape(-1, NACT), precision=lax.Pre...  1.07 us
  transfers between devices with their start and end apart: 4, of which 2 were waited for; matrix products, arithmetic and copies ran while one was open for 5% of the time, Pallas kernels for 6%

profile of v17, /device:TPU:0, one launch (start us, length us, event | category | flops | bytes accessed | tf_op | source)
XLA Modules:
  0.0 38.1 jit_solution(3115875982119339041)
XLA Ops:
  0.6 0.5 %collective-permute-start.1 = (f32[3,1,8,64,128]{4,3,2,1,0:T(8,128)}, f32[3,1,8,64,128]{4,3,2,1,0:T(8,128)S(1)}, u32[]{:S(2)}, u32[]{:S(2)}) collective-permute-start(f32[3,1,8,64,128]{4,3,2,1,0:T(8,128)} %param.7), channel_id=1, source_target_pairs={{0,1},{1,0},{2,3},{3,2},{4,5},{5,4},{6,7},{7,6},{8,9},{9,8},{10,11... | collective-permute-start | bytes 2359304 | tf_op jit(solution)/shard_map/ppermute | solution.py:52
  1.1 0.1 collective-permute-start
  1.2 8.3 %all-to-all-start = ((f32[16,32,128]{2,1,0:T(8,128)}), f32[16,32,128]{2,1,0:T(8,128)S(1)}, u32[]{:S(2)}, u32[]{:S(2)}) async-start(f32[16,32,128]{2,1,0:T(8,128)} %bitcast.26), calls=%async_computation | async-start | bytes 524288 | tf_op jit(solution)/shard_map/all_to_all | solution.py:141
  10.3 0.7 %copy-done.1 = f32[1,8,64,128]{3,2,1,0:T(8,128)} copy-done((f32[1,8,64,128]{3,2,1,0:T(8,128)}, f32[1,8,64,128]{3,2,1,0:T(8,128)S(1)}, u32[]{:S(2)}) %copy-start.1) | copy-done | bytes 262168
  11.0 0.3 copy-done
  11.2 2.4 %shard_map.77 = (f32[8,64,128]{2,1,0:T(8,128)}, f32[2,8,128]{2,1,0:T(8,128)}) custom-call(f32[1]{0:T(128)} %copy.30.pulse_ref, f32[8,64,128]{2,1,0:T(8,128)} %bitcast.27, f32[3,8,64,128]{3,2,1,0:T(8,128)} %bitcast.29, f32[8,64,128]{2,1,0:T(8,128)} %bitcast.30, f32[1,8,64,128]{3,2,1,0:T(8,128)} %copy-done.1, f32[3,1,8,64,128]{4,3,2,1,0:T(8,128)} %copy-done, ...), custom_call_target="tpu_custom_call" | custom-call | tf_op jit(solution)/shard_map/pallas_call | solution.py:111
  13.7 1.1 %convolution_bitcast_fusion = f32[2,128]{1,0:T(2,128)S(1)} fusion(s32[8,128]{1,0:T(8,128)S(1)} %copy-done.4, f32[2,8,128]{2,1,0:T(8,128)} %get-tuple-element.8), kind=kOutput, calls=%fused_computation | convolution fusion | flops 3276800 | bytes 13312 | tf_op jit(solution)/shard_map/dot_general | solution.py:151
  14.7 0.1 collective-permute-start.2
  14.9 0.1 broadcast_in_dim_reshape.3
  15.1 0.1 mul.71
  15.2 0.1 pad.10.clone
  15.3 0.7 %collective-permute-done.2 = f32[2,128]{1,0:T(2,128)S(1)} collective-permute-done((f32[2,128]{1,0:T(2,128)S(1)}, f32[2,128]{1,0:T(2,128)S(1)}, u32[]{:S(2)}, u32[]{:S(2)}) %collective-permute-start.2) | collective-permute-done | bytes 1056 | tf_op jit(solution)/shard_map/ppermute | solution.py:43
  16.0 0.1 mul.73
  16.1 0.1 copy.19
  16.2 0.1 squeeze.25
  16.4 0.1 maximum_maximum_fusion
  16.5 3.2 %all-to-all-done = f32[16,32,128]{2,1,0:T(8,128)S(1)} async-done(((f32[16,32,128]{2,1,0:T(8,128)}), f32[16,32,128]{2,1,0:T(8,128)S(1)}, u32[]{:S(2)}, u32[]{:S(2)}) %all-to-all-start) | async-done | bytes 262176 | tf_op jit(solution)/shard_map/all_to_all | solution.py:141
  19.6 0.5 %fusion.1 = f32[16,32,128]{2,0,1:T(8,128)S(1)} fusion(f32[16,32,128]{2,1,0:T(8,128)S(1)} %all-to-all-done), kind=kOutput, calls=%fused_computation.5 | convolution fusion | flops 12589312 | bytes 524288 | tf_op jit(solution)/shard_map/ji,jrc->irc/dot_general | solution.py:169
  20.2 0.1 copy.23
  20.3 15.4 %all_to_all.10 = f32[16,40,128]{2,1,0:T(8,128)S(1)} all-to-all(f32[16,40,128]{2,1,0:T(8,128)S(1)} %copy.23), channel_id=1, replica_groups=mesh['tm'=16,'space'=2] {'tm'}, dimensions={0} | all-to-all | bytes 655360 | tf_op jit(solution)/shard_map/all_to_all | solution.py:177
  35.8 0.1 mul.80
  35.9 0.5 %bitcast_add_fusion.1 = f32[8]{0:T(128)} fusion(f32[8]{0:T(128)S(1)} %reduce_sum.19, f32[3,128]{1,0:T(4,128)S(1)} %slice_reduce_fusion), kind=kLoop, calls=%fused_computation.32 | loop fusion | flops 8 | bytes 96 | tf_op jit(solution)/shard_map/add | solution.py:180
  36.5 0.9 %copy-done.2 = f32[8,64,128]{2,1,0:T(8,128)S(1)} copy-done((f32[8,64,128]{2,1,0:T(8,128)S(1)}, f32[8,64,128]{2,1,0:T(8,128)}, u32[]{:S(2)}) %copy-start.2) | copy-done | bytes 262168
  37.4 0.7 %fusion = f32[1,8,64,128]{3,2,1,0:T(8,128)} fusion(f32[8,64,128]{2,1,0:T(8,128)S(1)} %copy-done.2, f32[8,64,128]{2,1,0:T(8,128)S(1)} %bitcast.28), kind=kLoop, calls=%fused_computation.4 | loop fusion | flops 65536 | bytes 786432 | tf_op jit(solution)/shard_map/broadcast_in_dim | solution.py:182
  (27 shorter events, 0.5 us)
Async XLA Ops:
  0.6 9.6 %collective-permute-start.1 = (f32[3,1,8,64,128]{4,3,2,1,0:T(8,128)}, f32[3,1,8,64,128]{4,3,2,1,0:T(8,128)S(1)}, u32[]{:S(2)}, u32[]{:S(2)}) collective-permute-start(f32[3,1,8,64,128]{4,3,2,1,0:T(8,128)} %param.7), channel_id=1, source_target_pairs={{0,1},{1,0},{2,3},{3,2},{4,5},{5,4},{6,7},{7,6},{8,9},{9,8},{10,11... | collective-permute-start | bytes 2359304 | tf_op jit(solution)/shard_map/ppermute | solution.py:52
  1.1 9.1 %collective-permute-start = (f32[1,8,64,128]{3,2,1,0:T(8,128)}, f32[1,8,64,128]{3,2,1,0:T(8,128)S(1)}, u32[]{:S(2)}, u32[]{:S(2)}) collective-permute-start(f32[1,8,64,128]{3,2,1,0:T(8,128)} %param.6), channel_id=1, source_target_pairs={{0,1},{1,0},{2,3},{3,2},{4,5},{5,4},{6,7},{7,6},{8,9},{9,8},{10,11... | collective-permute-start | bytes 786440 | tf_op jit(solution)/shard_map/ppermute | solution.py:52
  1.2 18.4 %all-to-all-start = ((f32[16,32,128]{2,1,0:T(8,128)}), f32[16,32,128]{2,1,0:T(8,128)S(1)}, u32[]{:S(2)}, u32[]{:S(2)}) async-start(f32[16,32,128]{2,1,0:T(8,128)} %bitcast.26), calls=%async_computation | async-start | bytes 524288 | tf_op jit(solution)/shard_map/all_to_all | solution.py:141
  10.3 0.7 %copy-start.1 = (f32[1,8,64,128]{3,2,1,0:T(8,128)}, f32[1,8,64,128]{3,2,1,0:T(8,128)S(1)}, u32[]{:S(2)}) copy-start(f32[1,8,64,128]{3,2,1,0:T(8,128)S(1)} %collective-permute-done.prev_ref.next_ref) | copy-start | bytes 786436
  10.3 0.9 %copy-start = (f32[3,1,8,64,128]{4,3,2,1,0:T(8,128)}, f32[3,1,8,64,128]{4,3,2,1,0:T(8,128)S(1)}, u32[]{:S(2)}) copy-start(f32[3,1,8,64,128]{4,3,2,1,0:T(8,128)S(1)} %collective-permute-done.1.prev_u_ref.next_u_ref) | copy-start | bytes 2359300
  11.2 2.4 %copy-start.4 = (s32[8,128]{1,0:T(8,128)S(1)}, s32[8,128]{1,0:T(8,128)}, u32[]{:S(2)}) copy-start(s32[8,128]{1,0:T(8,128)} %param.10) | copy-start | bytes 12292
  14.7 1.2 %collective-permute-start.2 = (f32[2,128]{1,0:T(2,128)S(1)}, f32[2,128]{1,0:T(2,128)S(1)}, u32[]{:S(2)}, u32[]{:S(2)}) collective-permute-start(f32[2,128]{1,0:T(2,128)S(1)} %convolution_bitcast_fusion), channel_id=1, source_target_pairs={{0,1},{1,0},{2,3},{3,2},{4,5},{5,4},{6,7},{7,6},{8,9},{9,8},{10,11... | collective-permute-start | bytes 3080 | tf_op jit(solution)/shard_map/ppermute | solution.py:43
  15.2 0.8 %copy-start.3 = (f32[2]{0:T(128)S(1)}, f32[2]{0:T(128)}, u32[]{:S(2)}) copy-start(f32[2]{0:T(128)} %constant.59) | copy-start | bytes 28
  36.4 0.9 %copy-start.2 = (f32[8,64,128]{2,1,0:T(8,128)S(1)}, f32[8,64,128]{2,1,0:T(8,128)}, u32[]{:S(2)}) copy-start(f32[8,64,128]{2,1,0:T(8,128)} %get-tuple-element.9) | copy-start | bytes 786436

commit v18 on v16

--- a/solution.py
+++ b/solution.py
@@ -161,12 +161,8 @@
     pulse_row = jnp.broadcast_to(pulse.reshape(1, 1, 1), (count, 1, cz))
     grad_rows = jnp.concatenate([slices, pulse_row, jnp.zeros((count, pad - 3, cz), jnp.float32)], axis=1)
     kept, grad_rows, incoming = lax.optimization_barrier((kept, grad_rows, incoming))
-    derived = jnp.einsum(
-        "ji,jrc->irc",
-        (-pseudo_step * omega_rate) * dmat,
-        incoming,
-        precision=lax.Precision.HIGHEST,
-    )
+    weighted = (-pseudo_step * omega_rate) * dmat
+    derived = jnp.sum(weighted[:, :, None, None] * incoming[:, None], axis=0)
 
     outgoing = jnp.concatenate([derived, grad_rows], axis=1)
     incoming = lax.all_to_all(outgoing, "tm", 0, 0, tiled=True)

time: 38.1 us -> 37.2 us (0.976)
  local copies, waits for them, and re-layouts: 2.46 us -> 1.45 us
  matrix products: 1.58 us -> 1.07 us
  other arithmetic: 1.6 us -> 2.09 us
    unnamed x10 -> x11, local copies, waits for them, and re-layouts: 1.88 us -> 0.97 us
    dot_general x1 -> x0, matrix products: 0.51 us -> none  [on_device(): jnp.einsum('ji,jrc->irc', -pseudo_step * omega_rate * dmat, incoming, pre...]
  transfers between devices with their start and end apart: 4 -> 4, of which waited for: 2 -> 2; matrix products, arithmetic and copies ran while one was open for 4% -> 4% of each run, Pallas kernels for 6% -> 7%
where the time goes in v18:
time: 37.2 us; the launch traced here: 36.8 us
  blocking collectives  15 us (40%)
  starting transfers between devices  8.96 us (24%)
  waiting for transfers between devices  4.41 us (12%)
  Pallas kernels  2.45 us (7%)
  other arithmetic  2.09 us (6%)
  local copies, waits for them, and re-layouts  1.45 us (4%)
  between operations  1.39 us (4%)
  matrix products  1.07 us (3%)
    all_to_all x1, blocking collectives, on_device(): incoming = lax.all_to_all(outgoing, 'tm', 0, 0, tiled=True)  15 us
    all_to_all x1, starting transfers between devices, on_device(): lax.all_to_all(adjoint.reshape(count, chunk, cz), 'tm', 0, 0, tiled=True)  8.29 us
    all_to_all x1, waiting for transfers between devices, on_device(): lax.all_to_all(adjoint.reshape(count, chunk, cz), 'tm', 0, 0, tiled=True)  3.5 us
    pallas_call x1, Pallas kernels, stencil(): pl.pallas_call(stencil_kernel, grid=(1,), out_shape=(jax.ShapeDtypeStruct...  2.45 us
    dot_general x1, matrix products, on_device(): jnp.dot(walls.reshape(2, -1), onehot.reshape(-1, NACT), precision=lax.Pre...  1.07 us
    unnamed x11, local copies, waits for them, and re-layouts  0.97 us
    ppermute x1, waiting for transfers between devices, butterfly_sum(): x = x + lax.ppermute(x, axis, [(i, i ^ bit) for i in range(groups)])  0.9 us
  transfers between devices with their start and end apart: 4, of which 2 were waited for; matrix products, arithmetic and copies ran while one was open for 4% of the time, Pallas kernels for 7%

profile of v18, /device:TPU:0, one launch (start us, length us, event | category | flops | bytes accessed | tf_op | source)
XLA Modules:
  0.0 36.8 jit_solution(4531809262830949352)
XLA Ops:
  0.6 0.5 %collective-permute-start.1 = (f32[3,1,8,64,128]{4,3,2,1,0:T(8,128)}, f32[3,1,8,64,128]{4,3,2,1,0:T(8,128)S(1)}, u32[]{:S(2)}, u32[]{:S(2)}) collective-permute-start(f32[3,1,8,64,128]{4,3,2,1,0:T(8,128)} %param.7), channel_id=1, source_target_pairs={{0,1},{1,0},{2,3},{3,2},{4,5},{5,4},{6,7},{7,6},{8,9},{9,8},{10,11... | collective-permute-start | bytes 2359304 | tf_op jit(solution)/shard_map/ppermute | solution.py:52
  1.1 0.1 collective-permute-start
  1.2 8.3 %all-to-all-start = ((f32[16,32,128]{2,1,0:T(8,128)}), f32[16,32,128]{2,1,0:T(8,128)S(1)}, u32[]{:S(2)}, u32[]{:S(2)}) async-start(f32[16,32,128]{2,1,0:T(8,128)} %bitcast.20), calls=%async_computation | async-start | bytes 524288 | tf_op jit(solution)/shard_map/all_to_all | solution.py:141
  10.2 0.0 collective-permute-done.prev_ref.next_ref
  10.2 0.0 copy-start.1
  10.2 0.7 %copy-done.1 = f32[1,8,64,128]{3,2,1,0:T(8,128)} copy-done((f32[1,8,64,128]{3,2,1,0:T(8,128)}, f32[1,8,64,128]{3,2,1,0:T(8,128)S(1)}, u32[]{:S(2)}) %copy-start.1) | copy-done | bytes 262168
  10.9 0.3 copy-done
  11.2 2.4 %shard_map.77 = (f32[8,64,128]{2,1,0:T(8,128)}, f32[2,8,128]{2,1,0:T(8,128)}) custom-call(f32[1]{0:T(128)S(6)} %copy.27.pulse_ref, f32[8,64,128]{2,1,0:T(8,128)} %bitcast.21, f32[3,8,64,128]{3,2,1,0:T(8,128)} %bitcast.23, f32[8,64,128]{2,1,0:T(8,128)} %bitcast.24, f32[1,8,64,128]{3,2,1,0:T(8,128)} %copy-done.1, f32[3,1,8,64,128]{4,3,2,1,0:T(8,128)} %copy-done, ...), custom_call_target="tpu_custom_call" | custom-call | tf_op jit(solution)/shard_map/pallas_call | solution.py:111
  13.6 1.1 %convolution_bitcast_fusion = f32[2,128]{1,0:T(2,128)S(1)} fusion(s32[8,128]{1,0:T(8,128)S(1)} %copy-done.4, f32[2,8,128]{2,1,0:T(8,128)} %get-tuple-element.8), kind=kOutput, calls=%fused_computation.1 | convolution fusion | flops 3276800 | bytes 13312 | tf_op jit(solution)/shard_map/dot_general | solution.py:151
  14.7 0.1 collective-permute-start.2
  14.8 0.1 broadcast_multiply_fusion
  14.8 0.1 pad.8.clone
  14.9 0.1 pad.9.clone
  15.0 0.9 %collective-permute-done.2 = f32[2,128]{1,0:T(2,128)S(1)} collective-permute-done((f32[2,128]{1,0:T(2,128)S(1)}, f32[2,128]{1,0:T(2,128)S(1)}, u32[]{:S(2)}, u32[]{:S(2)}) %collective-permute-start.2) | collective-permute-done | bytes 1056 | tf_op jit(solution)/shard_map/ppermute | solution.py:43
  15.9 0.1 add_multiply_fusion
  16.0 0.1 reshape.62
  16.1 0.1 fusion.2
  16.1 3.5 %all-to-all-done = f32[16,32,128]{2,1,0:T(8,128)S(1)} async-done(((f32[16,32,128]{2,1,0:T(8,128)}), f32[16,32,128]{2,1,0:T(8,128)S(1)}, u32[]{:S(2)}, u32[]{:S(2)}) %all-to-all-start) | async-done | bytes 262176 | tf_op jit(solution)/shard_map/all_to_all | solution.py:141
  19.6 0.3 multiply_reduce_fusion
  20.0 15.0 %all_to_all.10 = f32[16,40,128]{2,1,0:T(8,128)S(1)} all-to-all(f32[16,40,128]{2,1,0:T(8,128)S(1)} %pad_maximum_fusion), channel_id=1, replica_groups=mesh['tm'=16,'space'=2] {'tm'}, dimensions={0} | all-to-all | bytes 655360 | tf_op jit(solution)/shard_map/all_to_all | solution.py:168
  35.1 0.2 slice_reduce_fusion
  35.3 0.2 multiply_reduce_fusion.1
  35.5 0.7 %fusion = f32[1,8,64,128]{3,2,1,0:T(8,128)} fusion(f32[8,64,128]{2,1,0:T(8,128)S(1)} %copy-done.2, f32[8,64,128]{2,1,0:T(8,128)S(1)} %bitcast.22), kind=kLoop, calls=%fused_computation.5 | loop fusion | flops 65536 | bytes 786432 | tf_op jit(solution)/shard_map/broadcast_in_dim | solution.py:174
  36.2 0.6 %add_reduce_fusion = f32[128]{0:T(128)} fusion(f32[16,128]{1,0:T(8,128)S(1)} %bitcast.27, f32[16,128]{1,0:T(8,128)S(1)} %bitcast.26, f32[16]{0:T(128)S(1)} %multiply_reduce_fusion.1), kind=kLoop, calls=%fused_computation.17 | loop fusion | flops 6016 | bytes 16960 | tf_op jit(solution)/shard_map/reduce_sum | solution.py:172
  (13 shorter events, 0.1 us)
Async XLA Ops:
  0.6 9.6 %collective-permute-start.1 = (f32[3,1,8,64,128]{4,3,2,1,0:T(8,128)}, f32[3,1,8,64,128]{4,3,2,1,0:T(8,128)S(1)}, u32[]{:S(2)}, u32[]{:S(2)}) collective-permute-start(f32[3,1,8,64,128]{4,3,2,1,0:T(8,128)} %param.7), channel_id=1, source_target_pairs={{0,1},{1,0},{2,3},{3,2},{4,5},{5,4},{6,7},{7,6},{8,9},{9,8},{10,11... | collective-permute-start | bytes 2359304 | tf_op jit(solution)/shard_map/ppermute | solution.py:52
  1.1 9.0 %collective-permute-start = (f32[1,8,64,128]{3,2,1,0:T(8,128)}, f32[1,8,64,128]{3,2,1,0:T(8,128)S(1)}, u32[]{:S(2)}, u32[]{:S(2)}) collective-permute-start(f32[1,8,64,128]{3,2,1,0:T(8,128)} %param.6), channel_id=1, source_target_pairs={{0,1},{1,0},{2,3},{3,2},{4,5},{5,4},{6,7},{7,6},{8,9},{9,8},{10,11... | collective-permute-start | bytes 786440 | tf_op jit(solution)/shard_map/ppermute | solution.py:52
  1.2 18.4 %all-to-all-start = ((f32[16,32,128]{2,1,0:T(8,128)}), f32[16,32,128]{2,1,0:T(8,128)S(1)}, u32[]{:S(2)}, u32[]{:S(2)}) async-start(f32[16,32,128]{2,1,0:T(8,128)} %bitcast.20), calls=%async_computation | async-start | bytes 524288 | tf_op jit(solution)/shard_map/all_to_all | solution.py:141
  10.2 0.7 %copy-start.1 = (f32[1,8,64,128]{3,2,1,0:T(8,128)}, f32[1,8,64,128]{3,2,1,0:T(8,128)S(1)}, u32[]{:S(2)}) copy-start(f32[1,8,64,128]{3,2,1,0:T(8,128)S(1)} %collective-permute-done.prev_ref.next_ref) | copy-start | bytes 786436
  10.2 0.9 %copy-start = (f32[3,1,8,64,128]{4,3,2,1,0:T(8,128)}, f32[3,1,8,64,128]{4,3,2,1,0:T(8,128)S(1)}, u32[]{:S(2)}) copy-start(f32[3,1,8,64,128]{4,3,2,1,0:T(8,128)S(1)} %collective-permute-done.1.prev_u_ref.next_u_ref) | copy-start | bytes 2359300
  11.2 2.5 %copy-start.4 = (s32[8,128]{1,0:T(8,128)S(1)}, s32[8,128]{1,0:T(8,128)}, u32[]{:S(2)}) copy-start(s32[8,128]{1,0:T(8,128)} %param.10) | copy-start | bytes 12292
  11.2 4.7 %copy-start.3 = (f32[2]{0:T(128)S(1)}, f32[2]{0:T(128)}, u32[]{:S(2)}) copy-start(f32[2]{0:T(128)} %constant.51) | copy-start | bytes 28
  14.7 1.2 %collective-permute-start.2 = (f32[2,128]{1,0:T(2,128)S(1)}, f32[2,128]{1,0:T(2,128)S(1)}, u32[]{:S(2)}, u32[]{:S(2)}) collective-permute-start(f32[2,128]{1,0:T(2,128)S(1)} %convolution_bitcast_fusion), channel_id=1, source_target_pairs={{0,1},{1,0},{2,3},{3,2},{4,5},{5,4},{6,7},{7,6},{8,9},{9,8},{10,11... | collective-permute-start | bytes 3080 | tf_op jit(solution)/shard_map/ppermute | solution.py:43
  20.0 15.5 %copy-start.2 = (f32[8,64,128]{2,1,0:T(8,128)S(1)}, f32[8,64,128]{2,1,0:T(8,128)}, u32[]{:S(2)}) copy-start(f32[8,64,128]{2,1,0:T(8,128)} %get-tuple-element.9) | copy-start | bytes 786436

commit v19 on v18

--- a/solution.py
+++ b/solution.py
@@ -167,9 +167,8 @@
     outgoing = jnp.concatenate([derived, grad_rows], axis=1)
     incoming = lax.all_to_all(outgoing, "tm", 0, 0, tiled=True)
     scaled_term = incoming[:, :chunk].reshape(nx, cy, cz)
-    weights = jnp.sum(dmat * incoming[None, :, chunk + 2, 0], axis=1)
-    lanes = incoming[:, chunk, :] + weights[:, None] * incoming[:, chunk + 1, :]
-    gradient = jnp.sum(lanes, axis=0)[:share]
+    cross = dmat[:, :, None] * incoming[None, :, chunk + 2, :] * incoming[:, None, chunk + 1, :]
+    gradient = (jnp.sum(incoming[:, chunk, :], axis=0) + jnp.sum(cross, axis=(0, 1)))[:share]
     updated = kept + scaled_term
     return (updated[None], gradient)
 

time: 37.2 us -> 37.8 us (1.016)
  blocking collectives: 15 us -> 0 us
  waiting for transfers between devices: 4.41 us -> 15.9 us
  starting transfers between devices: 8.96 us -> 12.6 us
  other arithmetic: 2.09 us -> 2.79 us
    all_to_all x1 -> x0, blocking collectives: 15 us -> none  [on_device(): incoming = lax.all_to_all(outgoing, 'tm', 0, 0, tiled=True)]
    all_to_all x0 -> x1, waiting for transfers between devices: none -> 11.5 us  [on_device(): incoming = lax.all_to_all(outgoing, 'tm', 0, 0, tiled=True)]
    all_to_all x0 -> x1, starting transfers between devices: none -> 3.68 us  [on_device(): incoming = lax.all_to_all(outgoing, 'tm', 0, 0, tiled=True)]
    concatenate x1, other arithmetic: 0.03 us -> 0.75 us  [on_device(): outgoing = jnp.concatenate([derived, grad_rows], axis=1)]
    reduce_sum x2 -> x1, other arithmetic: 0.77 us -> 0.11 us  [on_device(): jnp.sum(cross, axis=(0, 1))]
    add x0 -> x1, other arithmetic: none -> 0.52 us  [on_device(): jnp.sum(incoming[:, chunk, :], axis=0) + jnp.sum(cross, axis=(0, 1))]
    unnamed x11 -> x10, local copies, waits for them, and re-layouts: 0.97 us -> 0.97 us
  transfers between devices with their start and end apart: 4 -> 5, of which waited for: 2 -> 3; matrix products, arithmetic and copies ran while one was open for 4% -> 4% of each run, Pallas kernels for 7% -> 7%
where the time goes in v19:
time: 37.8 us; the launch traced here: 37.4 us
  waiting for transfers between devices  15.9 us (42%)
  starting transfers between devices  12.6 us (33%)
  other arithmetic  2.79 us (7%)
  Pallas kernels  2.44 us (6%)
  between operations  1.38 us (4%)
  local copies, waits for them, and re-layouts  1.24 us (3%)
  matrix products  1.07 us (3%)
    all_to_all x1, waiting for transfers between devices, on_device(): incoming = lax.all_to_all(outgoing, 'tm', 0, 0, tiled=True)  11.5 us
    all_to_all x1, starting transfers between devices, on_device(): lax.all_to_all(adjoint.reshape(count, chunk, cz), 'tm', 0, 0, tiled=True)  8.29 us
    all_to_all x1, starting transfers between devices, on_device(): incoming = lax.all_to_all(outgoing, 'tm', 0, 0, tiled=True)  3.68 us
    all_to_all x1, waiting for transfers between devices, on_device(): lax.all_to_all(adjoint.reshape(count, chunk, cz), 'tm', 0, 0, tiled=True)  3.49 us
    pallas_call x1, Pallas kernels, stencil(): pl.pallas_call(stencil_kernel, grid=(1,), out_shape=(jax.ShapeDtypeStruct...  2.44 us
    dot_general x1, matrix products, on_device(): jnp.dot(walls.reshape(2, -1), onehot.reshape(-1, NACT), precision=lax.Pre...  1.07 us
    unnamed x10, local copies, waits for them, and re-layouts  0.97 us
    ppermute x1, waiting for transfers between devices, butterfly_sum(): x = x + lax.ppermute(x, axis, [(i, i ^ bit) for i in range(groups)])  0.9 us
  transfers between devices with their start and end apart: 5, of which 3 were waited for; matrix products, arithmetic and copies ran while one was open for 4% of the time, Pallas kernels for 7%

profile of v19, /device:TPU:0, one launch (start us, length us, event | category | flops | bytes accessed | tf_op | source)
XLA Modules:
  0.0 37.4 jit_solution(15263967039015954446)
XLA Ops:
  0.6 0.5 %collective-permute-start.1 = (f32[3,1,8,64,128]{4,3,2,1,0:T(8,128)}, f32[3,1,8,64,128]{4,3,2,1,0:T(8,128)S(1)}, u32[]{:S(2)}, u32[]{:S(2)}) collective-permute-start(f32[3,1,8,64,128]{4,3,2,1,0:T(8,128)} %param.7), channel_id=1, source_target_pairs={{0,1},{1,0},{2,3},{3,2},{4,5},{5,4},{6,7},{7,6},{8,9},{9,8},{10,11... | collective-permute-start | bytes 2359304 | tf_op jit(solution)/shard_map/ppermute | solution.py:52
  1.1 0.1 collective-permute-start
  1.2 8.3 %all-to-all-start = ((f32[16,32,128]{2,1,0:T(8,128)}), f32[16,32,128]{2,1,0:T(8,128)S(1)}, u32[]{:S(2)}, u32[]{:S(2)}) async-start(f32[16,32,128]{2,1,0:T(8,128)} %bitcast.20), calls=%async_computation | async-start | bytes 524288 | tf_op jit(solution)/shard_map/all_to_all | solution.py:141
  10.2 0.7 %copy-done.1 = f32[1,8,64,128]{3,2,1,0:T(8,128)} copy-done((f32[1,8,64,128]{3,2,1,0:T(8,128)}, f32[1,8,64,128]{3,2,1,0:T(8,128)S(1)}, u32[]{:S(2)}) %copy-start.1) | copy-done | bytes 262168
  10.9 0.3 copy-done
  11.2 2.4 %shard_map.77 = (f32[8,64,128]{2,1,0:T(8,128)}, f32[2,8,128]{2,1,0:T(8,128)}) custom-call(f32[1]{0:T(128)S(6)} %copy.18.pulse_ref, f32[8,64,128]{2,1,0:T(8,128)} %bitcast.21, f32[3,8,64,128]{3,2,1,0:T(8,128)} %bitcast.23, f32[8,64,128]{2,1,0:T(8,128)} %bitcast.24, f32[1,8,64,128]{3,2,1,0:T(8,128)} %copy-done.1, f32[3,1,8,64,128]{4,3,2,1,0:T(8,128)} %copy-done, ...), custom_call_target="tpu_custom_call" | custom-call | tf_op jit(solution)/shard_map/pallas_call | solution.py:111
  13.6 1.1 %convolution_bitcast_fusion = f32[2,128]{1,0:T(2,128)S(1)} fusion(s32[8,128]{1,0:T(8,128)S(1)} %copy-done.4, f32[2,8,128]{2,1,0:T(8,128)} %get-tuple-element.8), kind=kOutput, calls=%fused_computation.1 | convolution fusion | flops 3276800 | bytes 13312 | tf_op jit(solution)/shard_map/dot_general | solution.py:151
  14.7 0.1 collective-permute-start.2
  14.8 0.1 broadcast_multiply_fusion
  14.8 0.1 pad.8.clone
  14.9 0.1 pad.9.clone
  15.0 0.9 %collective-permute-done.2 = f32[2,128]{1,0:T(2,128)S(1)} collective-permute-done((f32[2,128]{1,0:T(2,128)S(1)}, f32[2,128]{1,0:T(2,128)S(1)}, u32[]{:S(2)}, u32[]{:S(2)}) %collective-permute-start.2) | collective-permute-done | bytes 1056 | tf_op jit(solution)/shard_map/ppermute | solution.py:43
  15.9 0.1 add_multiply_fusion
  16.0 0.1 reshape.97
  16.1 0.1 fusion.2
  16.1 3.5 %all-to-all-done = f32[16,32,128]{2,1,0:T(8,128)S(1)} async-done(((f32[16,32,128]{2,1,0:T(8,128)}), f32[16,32,128]{2,1,0:T(8,128)S(1)}, u32[]{:S(2)}, u32[]{:S(2)}) %all-to-all-start) | async-done | bytes 262176 | tf_op jit(solution)/shard_map/all_to_all | solution.py:141
  19.6 0.3 multiply_reduce_fusion
  20.0 0.8 %pad_maximum_fusion = f32[16,40,128]{2,1,0:T(8,128)} fusion(f32[16,8,128]{2,1,0:T(8,128)S(1)} %fusion.2, f32[16,32,128]{2,1,0:T(8,128)S(1)} %multiply_reduce_fusion), kind=kLoop, calls=%fused_computation.3 | loop fusion | flops 81920 | bytes 655360 | tf_op jit(solution)/shard_map/concatenate | solution.py:167
  20.7 3.7 %all-to-all-start.1 = ((f32[16,40,128]{2,1,0:T(8,128)}), f32[16,40,128]{2,1,0:T(8,128)S(1)}, u32[]{:S(2)}, u32[]{:S(2)}) async-start(f32[16,40,128]{2,1,0:T(8,128)} %pad_maximum_fusion), calls=%async_computation.1 | async-start | bytes 655360 | tf_op jit(solution)/shard_map/all_to_all | solution.py:168
  24.4 0.1 divide_select_fusion
  24.5 11.5 %all-to-all-done.1 = f32[16,40,128]{2,1,0:T(8,128)S(1)} async-done(((f32[16,40,128]{2,1,0:T(8,128)}), f32[16,40,128]{2,1,0:T(8,128)S(1)}, u32[]{:S(2)}, u32[]{:S(2)}) %all-to-all-start.1) | async-done | bytes 327712 | tf_op jit(solution)/shard_map/all_to_all | solution.py:168
  36.0 0.1 multiply_reduce_fusion.1
  36.1 0.5 %add.30 = f32[128]{0:T(128)} add(f32[128]{0:T(128)S(1)} %get-tuple-element.14, f32[128]{0:T(128)S(1)} %multiply_reduce_fusion.1) | non-fusion elementwise | flops 128 | bytes 1536 | tf_op jit(solution)/shard_map/add | solution.py:171
  36.7 0.7 %fusion = f32[1,8,64,128]{3,2,1,0:T(8,128)} fusion(f32[8,64,128]{2,1,0:T(8,128)S(1)} %copy-done.2, f32[8,64,128]{2,1,0:T(8,128)S(1)} %bitcast.22), kind=kLoop, calls=%fused_computation.5 | loop fusion | flops 65536 | bytes 786432 | tf_op jit(solution)/shard_map/broadcast_in_dim | solution.py:173
  (14 shorter events, 0.1 us)
Async XLA Ops:
  0.6 9.6 %collective-permute-start.1 = (f32[3,1,8,64,128]{4,3,2,1,0:T(8,128)}, f32[3,1,8,64,128]{4,3,2,1,0:T(8,128)S(1)}, u32[]{:S(2)}, u32[]{:S(2)}) collective-permute-start(f32[3,1,8,64,128]{4,3,2,1,0:T(8,128)} %param.7), channel_id=1, source_target_pairs={{0,1},{1,0},{2,3},{3,2},{4,5},{5,4},{6,7},{7,6},{8,9},{9,8},{10,11... | collective-permute-start | bytes 2359304 | tf_op jit(solution)/shard_map/ppermute | solution.py:52
  1.1 9.0 %collective-permute-start = (f32[1,8,64,128]{3,2,1,0:T(8,128)}, f32[1,8,64,128]{3,2,1,0:T(8,128)S(1)}, u32[]{:S(2)}, u32[]{:S(2)}) collective-permute-start(f32[1,8,64,128]{3,2,1,0:T(8,128)} %param.6), channel_id=1, source_target_pairs={{0,1},{1,0},{2,3},{3,2},{4,5},{5,4},{6,7},{7,6},{8,9},{9,8},{10,11... | collective-permute-start | bytes 786440 | tf_op jit(solution)/shard_map/ppermute | solution.py:52
  1.2 18.4 %all-to-all-start = ((f32[16,32,128]{2,1,0:T(8,128)}), f32[16,32,128]{2,1,0:T(8,128)S(1)}, u32[]{:S(2)}, u32[]{:S(2)}) async-start(f32[16,32,128]{2,1,0:T(8,128)} %bitcast.20), calls=%async_computation | async-start | bytes 524288 | tf_op jit(solution)/shard_map/all_to_all | solution.py:141
  10.2 0.7 %copy-start.1 = (f32[1,8,64,128]{3,2,1,0:T(8,128)}, f32[1,8,64,128]{3,2,1,0:T(8,128)S(1)}, u32[]{:S(2)}) copy-start(f32[1,8,64,128]{3,2,1,0:T(8,128)S(1)} %collective-permute-done.prev_ref.next_ref) | copy-start | bytes 786436
  10.2 1.0 %copy-start = (f32[3,1,8,64,128]{4,3,2,1,0:T(8,128)}, f32[3,1,8,64,128]{4,3,2,1,0:T(8,128)S(1)}, u32[]{:S(2)}) copy-start(f32[3,1,8,64,128]{4,3,2,1,0:T(8,128)S(1)} %collective-permute-done.1.prev_u_ref.next_u_ref) | copy-start | bytes 2359300
  11.2 2.4 %copy-start.4 = (s32[8,128]{1,0:T(8,128)S(1)}, s32[8,128]{1,0:T(8,128)}, u32[]{:S(2)}) copy-start(s32[8,128]{1,0:T(8,128)} %param.10) | copy-start | bytes 12292
  11.2 4.7 %copy-start.3 = (f32[2]{0:T(128)S(1)}, f32[2]{0:T(128)}, u32[]{:S(2)}) copy-start(f32[2]{0:T(128)} %constant.51) | copy-start | bytes 28
  14.7 1.2 %collective-permute-start.2 = (f32[2,128]{1,0:T(2,128)S(1)}, f32[2,128]{1,0:T(2,128)S(1)}, u32[]{:S(2)}, u32[]{:S(2)}) collective-permute-start(f32[2,128]{1,0:T(2,128)S(1)} %convolution_bitcast_fusion), channel_id=1, source_target_pairs={{0,1},{1,0},{2,3},{3,2},{4,5},{5,4},{6,7},{7,6},{8,9},{9,8},{10,11... | collective-permute-start | bytes 3080 | tf_op jit(solution)/shard_map/ppermute | solution.py:43
  20.7 15.9 %copy-start.2 = (f32[8,64,128]{2,1,0:T(8,128)S(1)}, f32[8,64,128]{2,1,0:T(8,128)}, u32[]{:S(2)}) copy-start(f32[8,64,128]{2,1,0:T(8,128)} %get-tuple-element.9) | copy-start | bytes 786436
  20.7 15.2 %all-to-all-start.1 = ((f32[16,40,128]{2,1,0:T(8,128)}), f32[16,40,128]{2,1,0:T(8,128)S(1)}, u32[]{:S(2)}, u32[]{:S(2)}) async-start(f32[16,40,128]{2,1,0:T(8,128)} %pad_maximum_fusion), calls=%async_computation.1 | async-start | bytes 655360 | tf_op jit(solution)/shard_map/all_to_all | solution.py:168
